TPU v7x, 256 devices: a whole 4x4x8 slice. The times are simulated.
256 devices in a mesh: layer: 32 (over z, y), fblk: 8 (over x, core).
Axes of the slice: x: 4, y: 4, z: 8, core: 2. Of those that a mesh axis runs over, the one named last changes fastest.
Arguments:
- decoder: bfloat16 [4608, 131072], P('fblk', 'layer'), may hold values from -0.09375 to 0.09375
- encoder: bfloat16 [4608, 131072], P('fblk', 'layer'), may hold values from -0.09375 to 0.09375
- activation: bfloat16 [4, 131072], P(None, 'layer'), may hold values from 0.29882812 to 3
- blocks: int32 [4, 9, 3], replicated, may hold values from 0 to 31, as said below
- counts: int32 [4, 9], replicated, may hold values from 1 to 3
Outputs:
- influence: bfloat16 [32, 1536, 1536], P('layer', 'fblk')
Inputs may be any that keep to these rules, and one draw needn't show every extreme that they name: `blocks`: the 3 block numbers of one prompt and layer are distinct.
All inputs are finite; a program needn't handle non-finite values.
Results may differ from a plain program's by a relative error of at most 0.038.
Values may be sent and summed in bfloat16 or wider, within the bound.
No kernel may reach another device: no remote copies, remote signals or barrier semaphores. Data moves between devices by JAX's collectives and lax.ppermute only.
A program may use at most 128 MiB of HBM per device.

v0:
```python
import jax
import jax.numpy as jnp
from jax import lax
from jax.sharding import PartitionSpec as P

BLK = 512
ACTIVE_SLOTS = 3
LAYERS = 8


def partner(value, axis, apart):
    mask = 2**apart
    pairs = [(source, source ^ mask) for source in range(lax.axis_size(axis))]
    return lax.ppermute(value, axis, pairs)


def select_blocks(block_ids, active_count, quarter, local_blocks):
    slots = block_ids.shape[1]
    owner_index = block_ids // local_blocks
    local_index = block_ids % local_blocks
    live_slots = (jnp.arange(slots)[None, :] < active_count[:, None]) & (owner_index == quarter)
    onehot = (local_index[:, :, None] == jnp.arange(local_blocks)[None, None, :]) & live_slots[
        :, :, None
    ]
    return onehot.astype(jnp.bfloat16)


def on_device(decoder, encoder, activation, blocks, counts):
    layer_count = lax.axis_size("layer")
    store_shards = layer_count // LAYERS
    layer_index = lax.axis_index("layer")
    layer_group = layer_index // store_shards
    quarter = layer_index % store_shards
    fblk_count = lax.axis_size("fblk")
    slice_width, local_columns = decoder.shape
    local_blocks = local_columns // BLK
    prompts = activation.shape[0]
    active_width = ACTIVE_SLOTS * BLK
    column_share = active_width // fblk_count
    source_ids = lax.dynamic_index_in_dim(blocks, layer_group, 1, False)
    source_counts = lax.dynamic_index_in_dim(counts, layer_group, 1, False)
    target_ids = lax.dynamic_index_in_dim(blocks, layer_group + 1, 1, False)
    target_counts = lax.dynamic_index_in_dim(counts, layer_group + 1, 1, False)
    source_hot = select_blocks(source_ids, source_counts, quarter, local_blocks)
    target_hot = select_blocks(target_ids, target_counts, quarter, local_blocks)
    decoder_blocks = decoder.reshape(slice_width, local_blocks, BLK)
    encoder_blocks = encoder.reshape(slice_width, local_blocks, BLK)
    raw_source = jnp.einsum(
        "pak,dkb->pdab", source_hot, decoder_blocks, preferred_element_type=jnp.float32
    )
    act_blocks = jnp.einsum(
        "pak,pkb->pab",
        source_hot,
        activation.reshape(prompts, local_blocks, BLK),
        preferred_element_type=jnp.float32,
    )
    source = (
        (raw_source * act_blocks[:, None])
        .astype(jnp.bfloat16)
        .reshape(prompts, slice_width, active_width)
    )
    target = jnp.einsum(
        "pak,dkb->pdab", target_hot, encoder_blocks, preferred_element_type=jnp.float32
    )
    target = target.astype(jnp.bfloat16).reshape(prompts, slice_width, active_width)
    combined = jnp.concatenate([source, target], axis=2)
    for bit_index in reversed(range(store_shards.bit_length() - 1)):
        half_count = combined.shape[0] // 2
        is_upper = quarter // (1 << bit_index) % 2 == 1
        lower_half = combined[:half_count]
        upper_half = combined[half_count:]
        outgoing = jnp.where(is_upper, lower_half, upper_half)
        retained = jnp.where(is_upper, upper_half, lower_half)
        combined = retained + partner(outgoing, "layer", bit_index)
    source = combined[0, :, :active_width]
    target = combined[0, :, active_width:]
    gram_sum = lax.psum_scatter(
        lax.dot_general(
            target, source, (((0,), (0,)), ((), ())), preferred_element_type=jnp.float32
        ).astype(jnp.bfloat16),
        "fblk",
        scatter_dimension=0,
        tiled=True,
    ).astype(jnp.float32)
    live_rows = (lax.dynamic_slice(counts, (quarter, layer_group), (1, 1))[0, 0] * BLK).astype(
        jnp.float32
    )
    row_mean = jnp.sum(jnp.abs(gram_sum), axis=1) / live_rows
    step_rows = (0.7 * gram_sum / ((row_mean[:, None] + 1e-06) * jnp.sqrt(live_rows))).astype(
        jnp.bfloat16
    )
    prefix_part = step_rows
    range_total = step_rows
    base_bit = store_shards.bit_length() - 1
    for tree_level in range(LAYERS.bit_length() - 1):
        is_upper = layer_group // (1 << tree_level) % 2 == 1
        partner_rows = partner(range_total, "layer", base_bit + tree_level)
        stacked = jnp.concatenate([prefix_part, jnp.where(is_upper, range_total, partner_rows)], 0)
        products = jnp.dot(
            stacked,
            lax.all_gather(
                jnp.where(is_upper, partner_rows, range_total), "fblk", axis=0, tiled=True
            ),
            preferred_element_type=jnp.float32,
        )
        products = products.astype(jnp.bfloat16)
        prefix_part = jnp.where(is_upper, products[:column_share], prefix_part)
        range_total = products[column_share:]
    influence = (jnp.sqrt(jnp.float32(active_width)) * prefix_part.astype(jnp.float32)).astype(
        jnp.bfloat16
    )
    return influence[None]


def solution(mesh):
    in_specs = (P("fblk", "layer"), P("fblk", "layer"), P(None, "layer"), P(), P())
    out_specs = P("layer", "fblk", None)
    return jax.shard_map(
        on_device, mesh=mesh, in_specs=in_specs, out_specs=out_specs, check_vma=False
    )
```

profile of v0, /device:TPU:134, one launch (start us, length us, event | category | flops | bytes accessed | tf_op | source)
XLA Modules:
  0.0 615.0 jit_solution(348833225355845040)
XLA Ops:
  9.9 5.4 copy.36
  15.4 5.1 fusion.1
  20.4 13.8 %copy.23 = bf16[4,576,3,512]{1,3,2,0:T(8,128)(2,1)} copy(bf16[4,576,3,512]{3,0,1,2:T(4,128)(2,1)} %fusion.1) | data formatting | bytes 14155776 | tf_op jit(solution)/shard_map/convert_element_type | solution.py:59
  34.2 5.4 copy.38
  39.7 5.6 convert_bitcast_fusion
  45.2 13.8 %copy.27 = bf16[4,576,3,512]{1,3,2,0:T(8,128)(2,1)} copy(bf16[4,576,3,512]{3,0,1,2:T(4,128)(2,1)} %convert_bitcast_fusion) | data formatting | bytes 14155776 | tf_op jit(solution)/shard_map/convert_element_type | solution.py:65
  59.0 11.4 %broadcast_select_fusion = bf16[2,576,3072]{1,2,0:T(8,128)(2,1)} fusion(pred[]{:T(512)S(6)} %eq.73, bf16[4,576,1536]{1,2,0:T(8,128)(2,1)} %bitcast.89, bf16[4,576,1536]{1,2,0:T(8,128)(2,1)} %bitcast.87), kind=kLoop, calls=%fused_computation.6 | loop fusion | flops 31850496 | bytes 21233664 | tf_op jit(solution)/shard_map/jit(_where)/select_n | solution.py:72
  70.3 10.2 %copy.28 = bf16[2,576,3072]{2,1,0:T(8,128)(2,1)} copy(bf16[2,576,3072]{1,2,0:T(8,128)(2,1)} %broadcast_select_fusion) | data formatting | bytes 14155776 | tf_op jit(solution)/shard_map/jit(_where)/select_n | solution.py:72
  80.5 3.2 collective-permute-start
  83.7 152.7 %collective-permute-done = bf16[2,576,3072]{2,1,0:T(8,128)(2,1)} collective-permute-done((bf16[2,576,3072]{2,1,0:T(8,128)(2,1)}, bf16[2,576,3072]{2,1,0:T(8,128)(2,1)}, u32[]{:S(2)}, u32[]{:S(2)}) %collective-permute-start) | collective-permute-done | bytes 7077920 | tf_op jit(solution)/shard_map/ppermute | solution.py:14
  236.4 10.2 %copy.29 = bf16[2,576,3072]{1,2,0:T(8,128)(2,1)} copy(bf16[2,576,3072]{2,1,0:T(8,128)(2,1)} %collective-permute-done) | data formatting | bytes 14155776 | tf_op jit(solution)/shard_map/ppermute | solution.py:14
  246.6 10.0 %select_add_fusion = bf16[2,576,3072]{1,2,0:T(8,128)(2,1)S(1)} fusion(bf16[2,576,3072]{1,2,0:T(8,128)(2,1)} %copy.29, pred[]{:T(512)S(6)} %eq.73, bf16[4,576,1536]{1,2,0:T(8,128)(2,1)} %bitcast.90, bf16[4,576,1536]{1,2,0:T(8,128)(2,1)} %bitcast.88), kind=kLoop, calls=%fused_computation.5 | loop fusion | flops 46006272 | bytes 28311552 | tf_op jit(solution)/shard_map/add | solution.py:74
  256.6 3.0 copy-done
  259.6 2.4 broadcast_select_fusion.1
  262.0 4.4 copy.30
  266.5 1.9 collective-permute-start.1
  268.3 75.9 %collective-permute-done.1 = bf16[1,576,3072]{2,1,0:T(8,128)(2,1)} collective-permute-done((bf16[1,576,3072]{2,1,0:T(8,128)(2,1)S(1)}, bf16[1,576,3072]{2,1,0:T(8,128)(2,1)}, u32[]{:S(2)}, u32[]{:S(2)}) %collective-permute-start.1) | collective-permute-done | bytes 3538976 | tf_op jit(solution)/shard_map/ppermute | solution.py:14
  344.3 5.9 copy.31
  350.2 4.7 select_add_fusion.1
  355.0 5.7 convolution_convert_fusion
  360.7 1.3 dynamic_slice.27
  362.7 37.5 %reduce-scatter.2.cloned.1.call-done = bf16[192,1536]{1,0:T(8,128)(2,1)} async-done(((bf16[1536,1536]{1,0:T(8,128)(2,1)}), bf16[192,1536]{1,0:T(8,128)(2,1)}) %reduce-scatter.2.cloned.1.call-update) | async-done | bytes 589840 | tf_op jit(solution)/shard_map/reduce_scatter | solution.py:77
  403.5 14.4 %collective-permute-done.2 = bf16[192,1536]{1,0:T(8,128)(2,1)S(1)} collective-permute-done((bf16[192,1536]{1,0:T(8,128)(2,1)S(1)}, bf16[192,1536]{1,0:T(8,128)(2,1)S(1)}, u32[]{:S(2)}, u32[]{:S(2)}) %collective-permute-start.2) | collective-permute-done | bytes 589856 | tf_op jit(solution)/shard_map/ppermute | solution.py:14
  417.9 2.3 broadcast_select_fusion.3
  420.2 36.6 %all-gather.4.cloned.1.call-done = bf16[1536,1536]{1,0:T(8,128)(2,1)} async-done(((bf16[192,1536]{1,0:T(8,128)(2,1)}), bf16[1536,1536]{1,0:T(8,128)(2,1)}) %all-gather.4.cloned.1.call-update) | async-done | bytes 4718608 | tf_op jit(solution)/shard_map/all_gather | solution.py:101
  456.9 4.4 convolution_convert_fusion.2
  462.1 28.3 %collective-permute-done.3 = bf16[192,1536]{1,0:T(8,128)(2,1)S(1)} collective-permute-done((bf16[192,1536]{1,0:T(8,128)(2,1)S(1)}, bf16[192,1536]{1,0:T(8,128)(2,1)S(1)}, u32[]{:S(2)}, u32[]{:S(2)}) %collective-permute-start.3) | collective-permute-done | bytes 589856 | tf_op jit(solution)/shard_map/ppermute | solution.py:14
  491.8 36.9 %all-gather.6.cloned.1.call-done = bf16[1536,1536]{1,0:T(8,128)(2,1)} async-done(((bf16[192,1536]{1,0:T(8,128)(2,1)}), bf16[1536,1536]{1,0:T(8,128)(2,1)}) %all-gather.6.cloned.1.call-update) | async-done | bytes 4718608 | tf_op jit(solution)/shard_map/all_gather | solution.py:101
  528.6 4.3 convolution_convert_fusion.1
  533.3 31.9 %collective-permute-done.4 = bf16[192,1536]{1,0:T(8,128)(2,1)S(1)} collective-permute-done((bf16[192,1536]{1,0:T(8,128)(2,1)S(1)}, bf16[192,1536]{1,0:T(8,128)(2,1)S(1)}, u32[]{:S(2)}, u32[]{:S(2)}) %collective-permute-start.4) | collective-permute-done | bytes 589856 | tf_op jit(solution)/shard_map/ppermute | solution.py:14
  566.2 36.9 %all-gather.8.cloned.1.call-done = bf16[1536,1536]{1,0:T(8,128)(2,1)} async-done(((bf16[192,1536]{1,0:T(8,128)(2,1)}), bf16[1536,1536]{1,0:T(8,128)(2,1)}) %all-gather.8.cloned.1.call-update) | async-done | bytes 4718608 | tf_op jit(solution)/shard_map/all_gather | solution.py:101
  603.2 4.3 fusion.11
  (34 shorter events, 11.2 us)
Async XLA Ops:
  6.5 393.7 %reduce-scatter.2.cloned.1.call-start = ((), (), s32[]{:S(2)}) async-start(), calls=%async_computation.1 | async-start | bytes 5308416 | tf_op jit(solution)/shard_map/reduce_scatter | solution.py:77
  80.5 155.9 %collective-permute-start = (bf16[2,576,3072]{2,1,0:T(8,128)(2,1)}, bf16[2,576,3072]{2,1,0:T(8,128)(2,1)}, u32[]{:S(2)}, u32[]{:S(2)}) collective-permute-start(bf16[2,576,3072]{2,1,0:T(8,128)(2,1)} %copy.28), channel_id=1, source_target_pairs={{0,16},{8,24},{16,0},{24,8},{32,48},{40,56},{48,32},{56,40},{64,80... | collective-permute-start | bytes 21233672 | tf_op jit(solution)/shard_map/ppermute | solution.py:14
  256.6 3.0 copy-start
  266.5 77.8 %collective-permute-start.1 = (bf16[1,576,3072]{2,1,0:T(8,128)(2,1)S(1)}, bf16[1,576,3072]{2,1,0:T(8,128)(2,1)}, u32[]{:S(2)}, u32[]{:S(2)}) collective-permute-start(bf16[1,576,3072]{2,1,0:T(8,128)(2,1)S(1)} %copy.30), channel_id=1, source_target_pairs={{0,8},{8,0},{16,24},{24,16},{32,40},{40,32},{48,56},{56,48},{64,72... | collective-permute-start | bytes 10616840 | tf_op jit(solution)/shard_map/ppermute | solution.py:14
  360.7 96.2 %all-gather.4.cloned.1.call-start = ((), (), s32[]{:S(2)}) async-start(), calls=%async_computation.2 | async-start | bytes 5308416 | tf_op jit(solution)/shard_map/all_gather | solution.py:101
  402.7 15.2 %collective-permute-start.2 = (bf16[192,1536]{1,0:T(8,128)(2,1)S(1)}, bf16[192,1536]{1,0:T(8,128)(2,1)S(1)}, u32[]{:S(2)}, u32[]{:S(2)}) collective-permute-start(bf16[192,1536]{1,0:T(8,128)(2,1)S(1)} %fusion.3), channel_id=1, source_target_pairs={{0,32},{8,40},{16,48},{24,56},{32,0},{40,8},{48,16},{56,24},{64,96... | collective-permute-start | bytes 1769480 | tf_op jit(solution)/shard_map/ppermute | solution.py:14
  420.2 108.4 %all-gather.6.cloned.1.call-start = ((), (), s32[]{:S(2)}) async-start(), calls=%async_computation.3 | async-start | bytes 5308416 | tf_op jit(solution)/shard_map/all_gather | solution.py:101
  456.9 33.5 %copy-start.1 = (bf16[192,1536]{1,0:T(8,128)(2,1)S(1)}, bf16[192,1536]{1,0:T(8,128)(2,1)}, u32[]{:S(2)}) copy-start(bf16[192,1536]{1,0:T(8,128)(2,1)} %reduce-scatter.2.cloned.1.call-done) | copy-start | bytes 1769476
  461.3 29.1 %collective-permute-start.3 = (bf16[192,1536]{1,0:T(8,128)(2,1)S(1)}, bf16[192,1536]{1,0:T(8,128)(2,1)S(1)}, u32[]{:S(2)}, u32[]{:S(2)}) collective-permute-start(bf16[192,1536]{1,0:T(8,128)(2,1)S(1)} %slice.51), channel_id=1, source_target_pairs={{0,64},{8,72},{16,80},{24,88},{32,96},{40,104},{48,112},{56,120},{... | collective-permute-start | bytes 1769480 | tf_op jit(solution)/shard_map/ppermute | solution.py:14
  491.7 111.5 %all-gather.8.cloned.1.call-start = ((), (), s32[]{:S(2)}) async-start(), calls=%async_computation.4 | async-start | bytes 5308416 | tf_op jit(solution)/shard_map/all_gather | solution.py:101
  533.0 32.2 %collective-permute-start.4 = (bf16[192,1536]{1,0:T(8,128)(2,1)S(1)}, bf16[192,1536]{1,0:T(8,128)(2,1)S(1)}, u32[]{:S(2)}, u32[]{:S(2)}) collective-permute-start(bf16[192,1536]{1,0:T(8,128)(2,1)S(1)} %slice.53), channel_id=1, source_target_pairs={{0,128},{8,136},{16,144},{24,152},{32,160},{40,168},{48,176},{56,1... | collective-permute-start | bytes 1769480 | tf_op jit(solution)/shard_map/ppermute | solution.py:14
Sparse Core Ops, SparseCore 0:
  360.8 39.3 reduce-scatter.1
  420.3 36.5 all-gather.3
  491.8 36.7 all-gather.5
  566.3 36.7 all-gather.7
where the time goes:
time: 621 us; the launch traced here: 615 us
  waiting for transfers between devices  451 us (73%)
  local copies, waits for them, and re-layouts  75.8 us (12%)
  other arithmetic  36.6 us (6%)
  matrix products  30.3 us (5%)
  between operations  13.9 us (2%)
  starting transfers between devices  7.04 us (1%)
    ppermute x5, waiting for transfers between devices, partner(): return lax.ppermute(value, axis, pairs)  303 us
    all_gather x3, waiting for transfers between devices, on_device(): lax.all_gather(jnp.where(is_upper, partner_rows, range_total), 'fblk', ax...  110 us
    reduce_scatter x1, waiting for transfers between devices, on_device(): lax.psum_scatter(lax.dot_general(target, source, (((0,), (0,)), ((), ()))...  37.5 us
    ppermute x2, local copies, waits for them, and re-layouts, partner(): return lax.ppermute(value, axis, pairs)  16.1 us
    add x2, other arithmetic, on_device(): combined = retained + partner(outgoing, 'layer', bit_index)  14.7 us
    select_n x2, local copies, waits for them, and re-layouts, on_device(): outgoing = jnp.where(is_upper, lower_half, upper_half)  14.6 us
    unnamed x6, local copies, waits for them, and re-layouts  13.9 us
    convert_element_type x1, local copies, waits for them, and re-layouts, on_device(): source = (raw_source * act_blocks[:, None]).astype(jnp.bfloat16).reshape(...  13.8 us
  transfers between devices with their start and end apart: 9, of which 9 were waited for; matrix products, arithmetic and copies ran while one was open for 0% of the time, Pallas kernels for 0%

commit v1 on v0

v1 whole, which is shorter than its diff:
```python
import jax
import jax.numpy as jnp
from jax import lax
from jax.sharding import Mesh
from jax.sharding import PartitionSpec as P

BLK = 512
ACTIVE_SLOTS = 3
LAYERS = 8


def pick_blocks(matrix, weights, block_ids, active_count, quarter, local_blocks):
    prompts, slots = block_ids.shape
    rows = matrix.shape[0]
    out = []
    for prompt in range(prompts):
        pieces = []
        for slot in range(slots):
            block = block_ids[prompt, slot]
            local = block % local_blocks
            live = (slot < active_count[prompt]) & (block // local_blocks == quarter)
            column_block = lax.dynamic_slice(matrix, (0, local * BLK), (rows, BLK)).astype(jnp.float32)
            if weights is not None:
                factor = lax.dynamic_slice(weights[prompt], (local * BLK,), (BLK,)).astype(jnp.float32)
                column_block = column_block * factor[None, :]
            pieces.append(jnp.where(live, column_block, 0.0).astype(jnp.bfloat16))
        out.append(jnp.concatenate(pieces, 1))
    return jnp.stack(out, 0)


def on_device(decoder, encoder, activation, blocks, counts):
    group_count = lax.axis_size("lg")
    layer_group = lax.axis_index("lg")
    quarter = lax.axis_index("q")
    fblk = lax.axis_index("fblk")
    fblk_count = lax.axis_size("fblk")
    slice_width, local_columns = decoder.shape
    local_blocks = local_columns // BLK
    active_width = ACTIVE_SLOTS * BLK
    column_share = active_width // fblk_count

    source_ids = lax.dynamic_index_in_dim(blocks, layer_group, 1, False)
    source_counts = lax.dynamic_index_in_dim(counts, layer_group, 1, False)
    target_ids = lax.dynamic_index_in_dim(blocks, layer_group + 1, 1, False)
    target_counts = lax.dynamic_index_in_dim(counts, layer_group + 1, 1, False)
    source = pick_blocks(decoder, activation, source_ids, source_counts, quarter, local_blocks)
    target = pick_blocks(encoder, None, target_ids, target_counts, quarter, local_blocks)
    combined = jnp.concatenate([source, target], axis=2)
    combined = lax.psum_scatter(combined, "q", scatter_dimension=0, tiled=True)
    source = combined[0, :, :active_width]
    target = combined[0, :, active_width:]

    partial_gram = lax.dot_general(
        target, source, (((0,), (0,)), ((), ())), preferred_element_type=jnp.float32
    ).astype(jnp.bfloat16)
    gram_sum = lax.psum(partial_gram, "fblk").astype(jnp.float32)
    live_rows = (lax.dynamic_slice(counts, (quarter, layer_group), (1, 1))[0, 0] * BLK).astype(
        jnp.float32
    )
    row_mean = jnp.sum(jnp.abs(gram_sum), axis=1) / live_rows
    edges = (0.7 * gram_sum / ((row_mean[:, None] + 1e-06) * jnp.sqrt(live_rows))).astype(
        jnp.bfloat16
    )

    chain = lax.dynamic_slice_in_dim(edges, fblk * column_share, column_share, 1)
    forward = [(index, index + 1) for index in range(group_count - 1)]
    for step in range(1, group_count):
        previous = lax.ppermute(chain, "lg", forward)
        product = jnp.dot(edges, previous, preferred_element_type=jnp.float32).astype(jnp.bfloat16)
        chain = jnp.where(layer_group == step, product, chain)
    rows = lax.all_to_all(chain, "fblk", 0, 1, tiled=True)
    influence = (jnp.sqrt(jnp.float32(active_width)) * rows.astype(jnp.float32)).astype(
        jnp.bfloat16
    )
    return influence[None]


def solution(mesh):
    layer_count = mesh.shape["layer"]
    fblk_count = mesh.shape["fblk"]
    split = Mesh(
        mesh.devices.reshape(LAYERS, layer_count // LAYERS, fblk_count), ("lg", "q", "fblk")
    )
    layer = ("lg", "q")
    in_specs = (P("fblk", layer), P("fblk", layer), P(None, layer), P(), P())
    out_specs = P(layer, "fblk", None)
    return jax.shard_map(
        on_device, mesh=split, in_specs=in_specs, out_specs=out_specs, check_vma=False
    )
```

time: 621 us -> 502 us (0.81)
  waiting for transfers between devices: 451 us -> 312 us
  between operations: 13.9 us -> 90.5 us
  local copies, waits for them, and re-layouts: 75.8 us -> 13.9 us
  other arithmetic: 36.6 us -> 18 us
  blocking collectives: 0 us -> 15.4 us
  starting transfers between devices: 7.04 us -> 14.5 us
    ppermute x5 -> x7, waiting for transfers between devices: 303 us -> 106 us  [on_device(): previous = lax.ppermute(chain, 'lg', forward)]
    all_gather x3 -> x0, waiting for transfers between devices: 110 us -> none  [on_device(): lax.all_gather(jnp.where(is_upper, partner_rows, range_total), 'fblk', ax...]
    reduce_scatter x1, waiting for transfers between devices: 37.5 us -> 131 us  [on_device(): combined = lax.psum_scatter(combined, 'q', scatter_dimension=0, tiled=True)]
    psum x0 -> x1, waiting for transfers between devices: none -> 74.6 us  [on_device(): gram_sum = lax.psum(partial_gram, 'fblk').astype(jnp.float32)]
    convert_element_type x2, local copies, waits for them, and re-layouts: 27.6 us -> 1.94 us  [on_device(): (jnp.sqrt(jnp.float32(active_width)) * rows.astype(jnp.float32)).astype(j...]
    select_n x7 -> x0, other arithmetic: 18.2 us -> none  [the longest x2 13.7 us: on_device(): outgoing = jnp.where(is_upper, lower_half, upper_half)]
    ppermute x2 -> x0, local copies, waits for them, and re-layouts: 16.1 us -> none  [partner(): return lax.ppermute(value, axis, pairs)]
    all_to_all x0 -> x1, blocking collectives: none -> 15.4 us  [on_device(): rows = lax.all_to_all(chain, 'fblk', 0, 1, tiled=True)]
where the time goes in v1:
time: 502 us; the launch traced here: 499 us
  waiting for transfers between devices  312 us (62%)
  between operations  90.5 us (18%)
  matrix products  34.2 us (7%)
  other arithmetic  18 us (4%)
  blocking collectives  15.4 us (3%)
  starting transfers between devices  14.5 us (3%)
  local copies, waits for them, and re-layouts  13.9 us (3%)
    reduce_scatter x1, waiting for transfers between devices, on_device(): combined = lax.psum_scatter(combined, 'q', scatter_dimension=0, tiled=True)  131 us
    ppermute x7, waiting for transfers between devices, on_device(): previous = lax.ppermute(chain, 'lg', forward)  106 us
    psum x1, waiting for transfers between devices, on_device(): gram_sum = lax.psum(partial_gram, 'fblk').astype(jnp.float32)  74.6 us
    dot_general x7, matrix products, on_device(): jnp.dot(edges, previous, preferred_element_type=jnp.float32)  26.2 us
    all_to_all x1, blocking collectives, on_device(): rows = lax.all_to_all(chain, 'fblk', 0, 1, tiled=True)  15.4 us
    ppermute x7, starting transfers between devices, on_device(): previous = lax.ppermute(chain, 'lg', forward)  14.3 us
  transfers between devices with their start and end apart: 9, of which 9 were waited for; matrix products, arithmetic and copies ran while one was open for 0% of the time, Pallas kernels for 0%

profile of v1, /device:TPU:134, one launch (start us, length us, event | category | flops | bytes accessed | tf_op | source)
XLA Modules:
  0.0 498.8 jit_solution(49611215681181649)
XLA Ops:
  87.5 3.0 select_convert_fusion.23
  93.9 1.6 select_convert_fusion.11
  96.0 5.3 %maximum_maximum_fusion = bf16[4,576,3072]{2,1,0:T(8,128)(2,1)} fusion(bf16[1,576,1536]{2,1,0:T(8,128)(2,1)S(1)} %maximum_bitcast_fusion.7, bf16[1,576,1536]{2,1,0:T(8,128)(2,1)S(1)} %maximum_bitcast_fusion.6, bf16[1,576,1536]{2,1,0:T(8,128)(2,1)S(1)} %maximum_bitcast_fusion.5, bf16[1,576,1536]{2,1,0:T(8,128)(2,1)S(1)} %maximum_bitcast_fusion.4, ...), kind=kLoop, calls=%fused_computation | loop fusion | flops 113246208 | bytes 28311552 | tf_op jit(solution)/shard_map/concatenate | solution.py:48
  101.6 131.2 %reduce-scatter.2.cloned.1.call-done = bf16[1,576,3072]{2,1,0:T(8,128)(2,1)} async-done(((bf16[4,576,3072]{2,1,0:T(8,128)(2,1)}), bf16[1,576,3072]{2,1,0:T(8,128)(2,1)}) %reduce-scatter.2.cloned.1.call-update) | async-done | bytes 3538960 | tf_op jit(solution)/shard_map/reduce_scatter | solution.py:49
  232.8 8.0 %convolution_convert_fusion = bf16[1536,1536]{1,0:T(8,128)(2,1)} fusion(bf16[1,576,3072]{2,1,0:T(8,128)(2,1)} %reduce-scatter.2.cloned.1.call-done), kind=kOutput, calls=%fused_computation.6 | convolution fusion | flops 2720268288 | bytes 8257536 | tf_op jit(solution)/shard_map/dot_general | solution.py:53
  242.8 74.6 %all-reduce.2.cloned.1.call-done = bf16[1536,1536]{1,0:T(8,128)(2,1)} async-done(((bf16[1536,1536]{1,0:T(8,128)(2,1)}), bf16[1536,1536]{1,0:T(8,128)(2,1)}) %all-reduce.2.cloned.1.call-update) | async-done | bytes 4718608 | tf_op jit(solution)/shard_map/psum | solution.py:56
  317.4 3.5 fusion.2
  321.2 1.9 fusion.1
  323.1 2.1 copy-done.2
  325.8 2.6 collective-permute-start
  328.4 15.4 %collective-permute-done = bf16[1536,192]{0,1:T(8,128)(2,1)S(1)} collective-permute-done((bf16[1536,192]{0,1:T(8,128)(2,1)S(1)}, bf16[1536,192]{0,1:T(8,128)(2,1)S(1)}, u32[]{:S(2)}, u32[]{:S(2)}) %collective-permute-start) | collective-permute-done | bytes 589856 | tf_op jit(solution)/shard_map/ppermute | solution.py:68
  343.8 3.7 fusion.3
  347.8 1.9 collective-permute-start.1
  349.7 17.2 %collective-permute-done.1 = bf16[1536,192]{0,1:T(8,128)(2,1)S(1)} collective-permute-done((bf16[1536,192]{0,1:T(8,128)(2,1)S(1)}, bf16[1536,192]{0,1:T(8,128)(2,1)S(1)}, u32[]{:S(2)}, u32[]{:S(2)}) %collective-permute-start.1) | collective-permute-done | bytes 589856 | tf_op jit(solution)/shard_map/ppermute | solution.py:68
  366.9 3.7 fusion.4
  370.9 1.9 collective-permute-start.2
  372.8 16.5 %collective-permute-done.2 = bf16[1536,192]{0,1:T(8,128)(2,1)S(1)} collective-permute-done((bf16[1536,192]{0,1:T(8,128)(2,1)S(1)}, bf16[1536,192]{0,1:T(8,128)(2,1)S(1)}, u32[]{:S(2)}, u32[]{:S(2)}) %collective-permute-start.2) | collective-permute-done | bytes 589856 | tf_op jit(solution)/shard_map/ppermute | solution.py:68
  389.4 3.7 fusion.5
  393.4 2.1 collective-permute-start.3
  395.5 15.4 %collective-permute-done.3 = bf16[1536,192]{0,1:T(8,128)(2,1)S(1)} collective-permute-done((bf16[1536,192]{0,1:T(8,128)(2,1)S(1)}, bf16[1536,192]{0,1:T(8,128)(2,1)S(1)}, u32[]{:S(2)}, u32[]{:S(2)}) %collective-permute-start.3) | collective-permute-done | bytes 589856 | tf_op jit(solution)/shard_map/ppermute | solution.py:68
  411.0 3.7 fusion.6
  415.0 1.9 collective-permute-start.4
  416.9 14.8 %collective-permute-done.4 = bf16[1536,192]{0,1:T(8,128)(2,1)S(1)} collective-permute-done((bf16[1536,192]{0,1:T(8,128)(2,1)S(1)}, bf16[1536,192]{0,1:T(8,128)(2,1)S(1)}, u32[]{:S(2)}, u32[]{:S(2)}) %collective-permute-start.4) | collective-permute-done | bytes 589856 | tf_op jit(solution)/shard_map/ppermute | solution.py:68
  431.7 3.7 fusion.7
  435.7 1.9 collective-permute-start.5
  437.7 14.0 %collective-permute-done.5 = bf16[1536,192]{0,1:T(8,128)(2,1)S(1)} collective-permute-done((bf16[1536,192]{0,1:T(8,128)(2,1)S(1)}, bf16[1536,192]{0,1:T(8,128)(2,1)S(1)}, u32[]{:S(2)}, u32[]{:S(2)}) %collective-permute-start.5) | collective-permute-done | bytes 589856 | tf_op jit(solution)/shard_map/ppermute | solution.py:68
  451.6 3.7 fusion.8
  455.6 1.9 collective-permute-start.6
  457.6 13.1 %collective-permute-done.6 = bf16[1536,192]{0,1:T(8,128)(2,1)S(1)} collective-permute-done((bf16[1536,192]{0,1:T(8,128)(2,1)S(1)}, bf16[1536,192]{0,1:T(8,128)(2,1)S(1)}, u32[]{:S(2)}, u32[]{:S(2)}) %collective-permute-start.6) | collective-permute-done | bytes 589856 | tf_op jit(solution)/shard_map/ppermute | solution.py:68
  470.7 3.7 fusion.9
  474.4 15.4 %all_to_all.13 = bf16[8,192,192]{2,1,0:T(8,128)(2,1)S(1)} all-to-all(bf16[8,192,192]{2,1,0:T(8,128)(2,1)S(1)} %bitcast.104), channel_id=1, replica_groups=mesh['lg'=8,'q'=4,'fblk'=8] {'fblk'}, dimensions={0} | all-to-all | bytes 1179648 | tf_op jit(solution)/shard_map/all_to_all | solution.py:71
  490.4 1.5 convert_element_type.295
  (46 shorter events, 13.3 us)
Async XLA Ops:
  6.5 226.3 %reduce-scatter.2.cloned.1.call-start = ((), (), s32[]{:S(2)}) async-start(), calls=%async_computation.2 | async-start | bytes 17694720 | tf_op jit(solution)/shard_map/reduce_scatter | solution.py:49
  87.5 3.4 copy-start.1
  90.9 2.2 slice-start
  92.0 1.4 slice-start.1
  101.4 216.0 %all-reduce.2.cloned.1.call-start = ((), (), s32[]{:S(2)}) async-start(), calls=%async_computation.3 | async-start | bytes 9437184 | tf_op jit(solution)/shard_map/psum | solution.py:56
  317.4 3.8 copy-start
  323.1 2.1 copy-start.2
  325.8 18.0 %collective-permute-start = (bf16[1536,192]{0,1:T(8,128)(2,1)S(1)}, bf16[1536,192]{0,1:T(8,128)(2,1)S(1)}, u32[]{:S(2)}, u32[]{:S(2)}) collective-permute-start(bf16[1536,192]{0,1:T(8,128)(2,1)S(1)} %copy.18), channel_id=1, source_target_pairs={{0,32},{32,64},{64,96},{96,128},{128,160},{160,192},{192,224},{1,3... | collective-permute-start | bytes 1769480 | tf_op jit(solution)/shard_map/ppermute | solution.py:68
  347.8 19.1 %collective-permute-start.1 = (bf16[1536,192]{0,1:T(8,128)(2,1)S(1)}, bf16[1536,192]{0,1:T(8,128)(2,1)S(1)}, u32[]{:S(2)}, u32[]{:S(2)}) collective-permute-start(bf16[1536,192]{0,1:T(8,128)(2,1)S(1)} %copy.20), channel_id=1, source_target_pairs={{0,32},{32,64},{64,96},{96,128},{128,160},{160,192},{192,224},{1,3... | collective-permute-start | bytes 1769480 | tf_op jit(solution)/shard_map/ppermute | solution.py:68
  370.9 18.5 %collective-permute-start.2 = (bf16[1536,192]{0,1:T(8,128)(2,1)S(1)}, bf16[1536,192]{0,1:T(8,128)(2,1)S(1)}, u32[]{:S(2)}, u32[]{:S(2)}) collective-permute-start(bf16[1536,192]{0,1:T(8,128)(2,1)S(1)} %copy.22), channel_id=1, source_target_pairs={{0,32},{32,64},{64,96},{96,128},{128,160},{160,192},{192,224},{1,3... | collective-permute-start | bytes 1769480 | tf_op jit(solution)/shard_map/ppermute | solution.py:68
  393.4 17.6 %collective-permute-start.3 = (bf16[1536,192]{0,1:T(8,128)(2,1)S(1)}, bf16[1536,192]{0,1:T(8,128)(2,1)S(1)}, u32[]{:S(2)}, u32[]{:S(2)}) collective-permute-start(bf16[1536,192]{0,1:T(8,128)(2,1)S(1)} %copy.24), channel_id=1, source_target_pairs={{0,32},{32,64},{64,96},{96,128},{128,160},{160,192},{192,224},{1,3... | collective-permute-start | bytes 1769480 | tf_op jit(solution)/shard_map/ppermute | solution.py:68
  415.0 16.7 %collective-permute-start.4 = (bf16[1536,192]{0,1:T(8,128)(2,1)S(1)}, bf16[1536,192]{0,1:T(8,128)(2,1)S(1)}, u32[]{:S(2)}, u32[]{:S(2)}) collective-permute-start(bf16[1536,192]{0,1:T(8,128)(2,1)S(1)} %copy.26), channel_id=1, source_target_pairs={{0,32},{32,64},{64,96},{96,128},{128,160},{160,192},{192,224},{1,3... | collective-permute-start | bytes 1769480 | tf_op jit(solution)/shard_map/ppermute | solution.py:68
  435.7 15.9 %collective-permute-start.5 = (bf16[1536,192]{0,1:T(8,128)(2,1)S(1)}, bf16[1536,192]{0,1:T(8,128)(2,1)S(1)}, u32[]{:S(2)}, u32[]{:S(2)}) collective-permute-start(bf16[1536,192]{0,1:T(8,128)(2,1)S(1)} %copy.28), channel_id=1, source_target_pairs={{0,32},{32,64},{64,96},{96,128},{128,160},{160,192},{192,224},{1,3... | collective-permute-start | bytes 1769480 | tf_op jit(solution)/shard_map/ppermute | solution.py:68
  455.6 15.0 %collective-permute-start.6 = (bf16[1536,192]{0,1:T(8,128)(2,1)S(1)}, bf16[1536,192]{0,1:T(8,128)(2,1)S(1)}, u32[]{:S(2)}, u32[]{:S(2)}) collective-permute-start(bf16[1536,192]{0,1:T(8,128)(2,1)S(1)} %copy.30), channel_id=1, source_target_pairs={{0,32},{32,64},{64,96},{96,128},{128,160},{160,192},{192,224},{1,3... | collective-permute-start | bytes 1769480 | tf_op jit(solution)/shard_map/ppermute | solution.py:68
Sparse Core Ops, SparseCore 0:
  101.5 131.2 reduce-scatter.1
  241.0 76.3 all-reduce.1

commit v2 on v1

v2 whole, which is shorter than its diff:
```python
import jax
import jax.numpy as jnp
from jax import lax
from jax.experimental import pallas as pl
from jax.experimental.pallas import tpu as pltpu
from jax.sharding import Mesh
from jax.sharding import PartitionSpec as P

BLK = 512
ACTIVE_SLOTS = 3
LAYERS = 8
CHUNKS = 4


def select_kernel(src_loc, tgt_loc, src_live, tgt_live, dec_ref, enc_ref, act_ref, out_ref):
    prompt = pl.program_id(0)
    column = pl.program_id(1)

    @pl.when(column < ACTIVE_SLOTS)
    def _():
        weights = act_ref[...].astype(jnp.float32)
        row = lax.broadcasted_iota(jnp.int32, weights.shape, 0)
        factor = jnp.sum(jnp.where(row == prompt, weights, 0.0), axis=0, keepdims=True)
        value = dec_ref[...].astype(jnp.float32) * factor
        live = src_live[prompt, column] > 0
        out_ref[0] = jnp.where(live, value, 0.0).astype(out_ref.dtype)

    @pl.when(column >= ACTIVE_SLOTS)
    def _():
        live = tgt_live[prompt, column - ACTIVE_SLOTS] > 0
        out_ref[0] = jnp.where(live, enc_ref[...], jnp.zeros_like(enc_ref[...]))


def select_blocks(decoder, encoder, activation, src_loc, tgt_loc, src_live, tgt_live):
    rows, _ = decoder.shape
    prompts = activation.shape[0]
    slots = ACTIVE_SLOTS

    def dec_map(p, j, sl, tl, sv, tv):
        return (0, sl[p, jnp.minimum(j, slots - 1)])

    def enc_map(p, j, sl, tl, sv, tv):
        return (0, tl[p, jnp.maximum(j - slots, 0)])

    def out_map(p, j, sl, tl, sv, tv):
        return (p, 0, j)

    grid_spec = pltpu.PrefetchScalarGridSpec(
        num_scalar_prefetch=4,
        grid=(prompts, 2 * slots),
        in_specs=[
            pl.BlockSpec((rows, BLK), dec_map),
            pl.BlockSpec((rows, BLK), enc_map),
            pl.BlockSpec((prompts, BLK), dec_map),
        ],
        out_specs=pl.BlockSpec((1, rows, BLK), out_map),
    )
    block_bytes = rows * BLK * 2
    return pl.pallas_call(
        select_kernel,
        grid_spec=grid_spec,
        out_shape=jax.ShapeDtypeStruct((prompts, rows, 2 * slots * BLK), jnp.bfloat16),
        cost_estimate=pl.CostEstimate(
            flops=prompts * slots * rows * BLK,
            transcendentals=0,
            bytes_accessed=4 * prompts * slots * block_bytes,
        ),
    )(src_loc, tgt_loc, src_live, tgt_live, decoder, encoder, activation)


def slot_tables(blocks, counts, layer, quarter, local_blocks):
    ids = lax.dynamic_index_in_dim(blocks, layer, 1, False)
    count = lax.dynamic_index_in_dim(counts, layer, 1, False)
    slot = jnp.arange(ids.shape[1], dtype=jnp.int32)[None, :]
    live = (slot < count[:, None]) & (ids // local_blocks == quarter)
    return (ids % local_blocks).astype(jnp.int32), live.astype(jnp.int32)


def on_device(decoder, encoder, activation, blocks, counts):
    group_count = lax.axis_size("lg")
    layer_group = lax.axis_index("lg")
    quarter = lax.axis_index("q")
    fblk = lax.axis_index("fblk")
    fblk_count = lax.axis_size("fblk")
    local_blocks = decoder.shape[1] // BLK
    active_width = ACTIVE_SLOTS * BLK
    share = active_width // fblk_count

    src_loc, src_live = slot_tables(blocks, counts, layer_group, quarter, local_blocks)
    tgt_loc, tgt_live = slot_tables(blocks, counts, layer_group + 1, quarter, local_blocks)
    combined = select_blocks(decoder, encoder, activation, src_loc, tgt_loc, src_live, tgt_live)
    combined = lax.psum_scatter(combined, "q", scatter_dimension=0, tiled=True)
    source = combined[0, :, :active_width]
    target = combined[0, :, active_width:]

    partial_gram = lax.dot_general(
        target, source, (((0,), (0,)), ((), ())), preferred_element_type=jnp.float32
    ).astype(jnp.bfloat16)
    gram_sum = lax.psum(partial_gram, "fblk").astype(jnp.float32)
    live_rows = (lax.dynamic_slice(counts, (quarter, layer_group), (1, 1))[0, 0] * BLK).astype(
        jnp.float32
    )
    row_mean = jnp.sum(jnp.abs(gram_sum), axis=1) / live_rows
    edges = (0.7 * gram_sum / ((row_mean[:, None] + 1e-06) * jnp.sqrt(live_rows))).astype(
        jnp.bfloat16
    )

    mine = lax.dynamic_slice_in_dim(edges, fblk * share, share, 1).T
    width = share // CHUNKS
    forward = [(index, index + 1) for index in range(group_count - 1)]
    for step in range(1, group_count + CHUNKS - 1):
        sent = jnp.clip(step - 1 - layer_group, 0, CHUNKS - 1)
        outgoing = lax.dynamic_slice_in_dim(mine, sent * width, width, 0)
        previous = lax.ppermute(outgoing, "lg", forward)
        product = lax.dot_general(
            previous, edges, (((1,), (1,)), ((), ())), preferred_element_type=jnp.float32
        ).astype(jnp.bfloat16)
        chunk = step - layer_group
        valid = (layer_group >= 1) & (chunk >= 0) & (chunk < CHUNKS)
        place = jnp.clip(chunk, 0, CHUNKS - 1)
        kept = lax.dynamic_slice_in_dim(mine, place * width, width, 0)
        mine = lax.dynamic_update_slice_in_dim(
            mine, jnp.where(valid, product, kept), place * width, 0
        )

    parts = []
    for shift in range(fblk_count):
        wanted = (fblk + shift) % fblk_count
        piece = lax.dynamic_slice_in_dim(mine, wanted * share, share, 1)
        if shift:
            pairs = [(index, (index + shift) % fblk_count) for index in range(fblk_count)]
            piece = lax.ppermute(piece, "fblk", pairs)
        parts.append(piece.T)
    ordered = [parts[(fblk_count - m) % fblk_count] for m in range(fblk_count)]
    doubled = jnp.concatenate(ordered + ordered, axis=1)
    rows = lax.dynamic_slice_in_dim(doubled, (fblk_count - fblk) * share, active_width, 1)
    influence = (jnp.sqrt(jnp.float32(active_width)) * rows.astype(jnp.float32)).astype(
        jnp.bfloat16
    )
    return influence[None]


def solution(mesh):
    layer_count = mesh.shape["layer"]
    fblk_count = mesh.shape["fblk"]
    split = Mesh(
        mesh.devices.reshape(LAYERS, layer_count // LAYERS, fblk_count), ("lg", "q", "fblk")
    )
    layer = ("lg", "q")
    in_specs = (P("fblk", layer), P("fblk", layer), P(None, layer), P(), P())
    out_specs = P(layer, "fblk", None)
    return jax.shard_map(
        on_device, mesh=split, in_specs=in_specs, out_specs=out_specs, check_vma=False
    )
```

time: 502 us -> 463 us (0.922)
  between operations: 90.5 us -> 14.8 us
  Pallas kernels: 0 us -> 21.3 us
  local copies, waits for them, and re-layouts: 13.9 us -> 30.7 us
  blocking collectives: 15.4 us -> 0 us
  starting transfers between devices: 14.5 us -> 27.1 us
  other arithmetic: 18 us -> 7.77 us
  matrix products: 34.2 us -> 43 us
    dynamic_update_slice x0 -> x10, local copies, waits for them, and re-layouts: none -> 24.1 us  [on_device(): lax.dynamic_update_slice_in_dim(mine, jnp.where(valid, product, kept), pl...]
    pallas_call x0 -> x1, Pallas kernels: none -> 21.3 us  [select_blocks(): pl.pallas_call(select_kernel, grid_spec=grid_spec, out_shape=jax.ShapeDty...]
    all_to_all x1 -> x0, blocking collectives: 15.4 us -> none  [on_device(): rows = lax.all_to_all(chain, 'fblk', 0, 1, tiled=True)]
    ppermute x7 -> x17, starting transfers between devices: 14.3 us -> 27 us  [the longest x10 20.2 us: on_device(): previous = lax.ppermute(outgoing, 'lg', forward)]
    dot_general x7 -> x10, matrix products: 26.2 us -> 34.9 us  [on_device(): lax.dot_general(previous, edges, (((1,), (1,)), ((), ())), preferred_elem...]
    convert_element_type x5 -> x1, other arithmetic: 6.3 us -> 0.66 us  [slot_tables(): return ((ids % local_blocks).astype(jnp.int32), live.astype(jnp.int32))]
    concatenate x1 -> x0, other arithmetic: 5.33 us -> none  [on_device(): combined = jnp.concatenate([source, target], axis=2)]
    ppermute x7 -> x17, waiting for transfers between devices: 106 us -> 110 us  [the longest x10 103 us: on_device(): previous = lax.ppermute(outgoing, 'lg', forward)]
  transfers between devices with their start and end apart: 9 -> 19, of which waited for: 9 -> 14; matrix products, arithmetic and copies ran while one was open for 0% -> 0% of each run, Pallas kernels for 0% -> 0%
where the time goes in v2:
time: 463 us; the launch traced here: 460 us
  waiting for transfers between devices  316 us (68%)
  matrix products  43 us (9%)
  local copies, waits for them, and re-layouts  30.7 us (7%)
  starting transfers between devices  27.1 us (6%)
  Pallas kernels  21.3 us (5%)
  between operations  14.8 us (3%)
  other arithmetic  7.77 us (2%)
    reduce_scatter x1, waiting for transfers between devices, on_device(): combined = lax.psum_scatter(combined, 'q', scatter_dimension=0, tiled=True)  131 us
    ppermute x10, waiting for transfers between devices, on_device(): previous = lax.ppermute(outgoing, 'lg', forward)  103 us
    psum x1, waiting for transfers between devices, on_device(): gram_sum = lax.psum(partial_gram, 'fblk').astype(jnp.float32)  74.5 us
    dot_general x10, matrix products, on_device(): lax.dot_general(previous, edges, (((1,), (1,)), ((), ())), preferred_elem...  34.9 us
    dynamic_update_slice x10, local copies, waits for them, and re-layouts, on_device(): lax.dynamic_update_slice_in_dim(mine, jnp.where(valid, product, kept), pl...  24.1 us
    pallas_call x1, Pallas kernels, select_blocks(): pl.pallas_call(select_kernel, grid_spec=grid_spec, out_shape=jax.ShapeDty...  21.3 us
    ppermute x10, starting transfers between devices, on_device(): previous = lax.ppermute(outgoing, 'lg', forward)  20.2 us
  transfers between devices with their start and end apart: 19, of which 14 were waited for; matrix products, arithmetic and copies ran while one was open for 0% of the time, Pallas kernels for 0%

profile of v2, /device:TPU:134, one launch (start us, length us, event | category | flops | bytes accessed | tf_op | source)
XLA Modules:
  0.0 460.4 jit_solution(6351751869652192682)
XLA Ops:
  9.8 21.3 %shard_map.55 = bf16[4,576,3072]{2,1,0:T(8,128)(2,1)} custom-call(s32[4,3]{1,0:T(4,128)} %get-tuple-element.18.src_loc, s32[4,3]{1,0:T(4,128)} %get-tuple-element.17.tgt_loc, s32[4,3]{1,0:T(4,128)} %get-tuple-element.19.src_live, s32[4,3]{1,0:T(4,128)} %get-tuple-element.20.tgt_live, bf16[576,4096]{1,0:T(8,128)(2,1)} %dec_ref.1, bf16[576,4096]{1,0:T(8,128)(2,1)} %enc_ref.1, ...), custom_call_target="tpu_custom_call" | custom-call | flops 3538944 | bytes 28311552 | tf_op jit(solution)/shard_map/pallas_call | solution.py:59
  31.2 131.4 %reduce-scatter.2.cloned.1.call-done = bf16[1,576,3072]{2,1,0:T(8,128)(2,1)} async-done(((bf16[4,576,3072]{2,1,0:T(8,128)(2,1)}), bf16[1,576,3072]{2,1,0:T(8,128)(2,1)}) %reduce-scatter.2.cloned.1.call-update) | async-done | bytes 3538960 | tf_op jit(solution)/shard_map/reduce_scatter | solution.py:92
  162.6 8.0 %convolution_convert_fusion = bf16[1536,1536]{1,0:T(8,128)(2,1)} fusion(bf16[1,576,3072]{2,1,0:T(8,128)(2,1)} %reduce-scatter.2.cloned.1.call-done), kind=kOutput, calls=%fused_computation.5 | convolution fusion | flops 2720268288 | bytes 8257536 | tf_op jit(solution)/shard_map/dot_general | solution.py:96
  172.6 74.5 %all-reduce.2.cloned.1.call-done = bf16[1536,1536]{1,0:T(8,128)(2,1)} async-done(((bf16[1536,1536]{1,0:T(8,128)(2,1)}), bf16[1536,1536]{1,0:T(8,128)(2,1)}) %all-reduce.2.cloned.1.call-update) | async-done | bytes 4718608 | tf_op jit(solution)/shard_map/psum | solution.py:99
  247.2 3.5 fusion.2
  256.0 10.8 %collective-permute-done = bf16[48,1536]{0,1:T(8,128)(2,1)S(1)} collective-permute-done((bf16[48,1536]{0,1:T(8,128)(2,1)S(1)}, bf16[48,1536]{0,1:T(8,128)(2,1)S(1)}, u32[]{:S(2)}, u32[]{:S(2)}) %collective-permute-start) | collective-permute-done | bytes 147488 | tf_op jit(solution)/shard_map/ppermute | solution.py:114
  272.3 12.8 %collective-permute-done.1 = bf16[48,1536]{0,1:T(8,128)(2,1)S(1)} collective-permute-done((bf16[48,1536]{0,1:T(8,128)(2,1)S(1)}, bf16[48,1536]{0,1:T(8,128)(2,1)S(1)}, u32[]{:S(2)}, u32[]{:S(2)}) %collective-permute-start.1) | collective-permute-done | bytes 147488 | tf_op jit(solution)/shard_map/ppermute | solution.py:114
  285.1 3.7 fusion.4
  292.7 12.3 %collective-permute-done.2 = bf16[48,1536]{0,1:T(8,128)(2,1)S(1)} collective-permute-done((bf16[48,1536]{0,1:T(8,128)(2,1)S(1)}, bf16[48,1536]{0,1:T(8,128)(2,1)S(1)}, u32[]{:S(2)}, u32[]{:S(2)}) %collective-permute-start.2) | collective-permute-done | bytes 147488 | tf_op jit(solution)/shard_map/ppermute | solution.py:114
  305.0 3.7 fusion.5
  312.7 11.4 %collective-permute-done.3 = bf16[48,1536]{0,1:T(8,128)(2,1)S(1)} collective-permute-done((bf16[48,1536]{0,1:T(8,128)(2,1)S(1)}, bf16[48,1536]{0,1:T(8,128)(2,1)S(1)}, u32[]{:S(2)}, u32[]{:S(2)}) %collective-permute-start.3) | collective-permute-done | bytes 147488 | tf_op jit(solution)/shard_map/ppermute | solution.py:114
  324.1 3.7 fusion.6
  331.8 10.6 %collective-permute-done.4 = bf16[48,1536]{0,1:T(8,128)(2,1)S(1)} collective-permute-done((bf16[48,1536]{0,1:T(8,128)(2,1)S(1)}, bf16[48,1536]{0,1:T(8,128)(2,1)S(1)}, u32[]{:S(2)}, u32[]{:S(2)}) %collective-permute-start.4) | collective-permute-done | bytes 147488 | tf_op jit(solution)/shard_map/ppermute | solution.py:114
  342.3 3.7 fusion.7
  346.1 3.0 dynamic_update_slice.34
  351.2 9.7 %collective-permute-done.5 = bf16[48,1536]{0,1:T(8,128)(2,1)S(1)} collective-permute-done((bf16[48,1536]{0,1:T(8,128)(2,1)S(1)}, bf16[48,1536]{0,1:T(8,128)(2,1)S(1)}, u32[]{:S(2)}, u32[]{:S(2)}) %collective-permute-start.5) | collective-permute-done | bytes 147488 | tf_op jit(solution)/shard_map/ppermute | solution.py:114
  360.9 3.7 fusion.8
  364.7 3.0 dynamic_update_slice.35
  370.1 8.7 %collective-permute-done.6 = bf16[48,1536]{0,1:T(8,128)(2,1)S(1)} collective-permute-done((bf16[48,1536]{0,1:T(8,128)(2,1)S(1)}, bf16[48,1536]{0,1:T(8,128)(2,1)S(1)}, u32[]{:S(2)}, u32[]{:S(2)}) %collective-permute-start.6) | collective-permute-done | bytes 147488 | tf_op jit(solution)/shard_map/ppermute | solution.py:114
  378.8 3.7 fusion.9
  382.5 2.7 dynamic_update_slice.36
  387.4 8.9 %collective-permute-done.7 = bf16[48,1536]{0,1:T(8,128)(2,1)S(1)} collective-permute-done((bf16[48,1536]{0,1:T(8,128)(2,1)S(1)}, bf16[48,1536]{0,1:T(8,128)(2,1)S(1)}, u32[]{:S(2)}, u32[]{:S(2)}) %collective-permute-start.7) | collective-permute-done | bytes 147488 | tf_op jit(solution)/shard_map/ppermute | solution.py:114
  396.3 3.7 fusion.10
  400.1 2.7 dynamic_update_slice.37
  404.9 8.9 %collective-permute-done.8 = bf16[48,1536]{0,1:T(8,128)(2,1)S(1)} collective-permute-done((bf16[48,1536]{0,1:T(8,128)(2,1)S(1)}, bf16[48,1536]{0,1:T(8,128)(2,1)S(1)}, u32[]{:S(2)}, u32[]{:S(2)}) %collective-permute-start.8) | collective-permute-done | bytes 147488 | tf_op jit(solution)/shard_map/ppermute | solution.py:114
  413.9 3.7 fusion.11
  417.6 2.7 dynamic_update_slice.38
  422.6 8.8 %collective-permute-done.9 = bf16[48,1536]{0,1:T(8,128)(2,1)S(1)} collective-permute-done((bf16[48,1536]{0,1:T(8,128)(2,1)S(1)}, bf16[48,1536]{0,1:T(8,128)(2,1)S(1)}, u32[]{:S(2)}, u32[]{:S(2)}) %collective-permute-start.9) | collective-permute-done | bytes 147488 | tf_op jit(solution)/shard_map/ppermute | solution.py:114
  431.4 3.7 fusion.12
  435.2 2.7 dynamic_update_slice.39
  438.3 2.8 collective-permute-start.14
  443.1 4.6 collective-permute-done.11
  (58 shorter events, 46.0 us)
Async XLA Ops:
  6.5 156.0 %reduce-scatter.2.cloned.1.call-start = ((), (), s32[]{:S(2)}) async-start(), calls=%async_computation.1 | async-start | bytes 17694720 | tf_op jit(solution)/shard_map/reduce_scatter | solution.py:92
  31.1 216.0 %all-reduce.2.cloned.1.call-start = ((), (), s32[]{:S(2)}) async-start(), calls=%async_computation.2 | async-start | bytes 9437184 | tf_op jit(solution)/shard_map/psum | solution.py:99
  247.2 3.8 copy-start
  252.8 14.0 %copy-start.1 = (bf16[1536,1536]{1,0:T(8,128)(2,1)}, bf16[1536,1536]{1,0:T(8,128)(2,1)S(1)}, u32[]{:S(2)}) copy-start(bf16[1536,1536]{1,0:T(8,128)(2,1)S(1)} %fusion.1) | copy-start | bytes 14155780
  253.1 13.7 %collective-permute-start = (bf16[48,1536]{0,1:T(8,128)(2,1)S(1)}, bf16[48,1536]{0,1:T(8,128)(2,1)S(1)}, u32[]{:S(2)}, u32[]{:S(2)}) collective-permute-start(bf16[48,1536]{0,1:T(8,128)(2,1)S(1)} %dynamic-slice_bitcast_fusion.1), channel_id=1, source_target_pairs={{0,32},{32,64},{64,96},{96,128},{128,160},{160,192},{192,224},{1,3... | collective-permute-start | bytes 442376 | tf_op jit(solution)/shard_map/ppermute | solution.py:114
  270.2 14.9 %collective-permute-start.1 = (bf16[48,1536]{0,1:T(8,128)(2,1)S(1)}, bf16[48,1536]{0,1:T(8,128)(2,1)S(1)}, u32[]{:S(2)}, u32[]{:S(2)}) collective-permute-start(bf16[48,1536]{0,1:T(8,128)(2,1)S(1)} %constant_dynamic-slice_fusion.15), channel_id=1, source_target_pairs={{0,32},{32,64},{64,96},{96,128},{128,160},{160,192},{192,224},{1,3... | collective-permute-start | bytes 442376 | tf_op jit(solution)/shard_map/ppermute | solution.py:114
  290.8 14.2 %collective-permute-start.2 = (bf16[48,1536]{0,1:T(8,128)(2,1)S(1)}, bf16[48,1536]{0,1:T(8,128)(2,1)S(1)}, u32[]{:S(2)}, u32[]{:S(2)}) collective-permute-start(bf16[48,1536]{0,1:T(8,128)(2,1)S(1)} %constant_dynamic-slice_fusion.14), channel_id=1, source_target_pairs={{0,32},{32,64},{64,96},{96,128},{128,160},{160,192},{192,224},{1,3... | collective-permute-start | bytes 442376 | tf_op jit(solution)/shard_map/ppermute | solution.py:114
  310.7 13.4 %collective-permute-start.3 = (bf16[48,1536]{0,1:T(8,128)(2,1)S(1)}, bf16[48,1536]{0,1:T(8,128)(2,1)S(1)}, u32[]{:S(2)}, u32[]{:S(2)}) collective-permute-start(bf16[48,1536]{0,1:T(8,128)(2,1)S(1)} %constant_dynamic-slice_fusion.13), channel_id=1, source_target_pairs={{0,32},{32,64},{64,96},{96,128},{128,160},{160,192},{192,224},{1,3... | collective-permute-start | bytes 442376 | tf_op jit(solution)/shard_map/ppermute | solution.py:114
  329.8 12.5 %collective-permute-start.4 = (bf16[48,1536]{0,1:T(8,128)(2,1)S(1)}, bf16[48,1536]{0,1:T(8,128)(2,1)S(1)}, u32[]{:S(2)}, u32[]{:S(2)}) collective-permute-start(bf16[48,1536]{0,1:T(8,128)(2,1)S(1)} %constant_dynamic-slice_fusion.12), channel_id=1, source_target_pairs={{0,32},{32,64},{64,96},{96,128},{128,160},{160,192},{192,224},{1,3... | collective-permute-start | bytes 442376 | tf_op jit(solution)/shard_map/ppermute | solution.py:114
  349.3 11.7 %collective-permute-start.5 = (bf16[48,1536]{0,1:T(8,128)(2,1)S(1)}, bf16[48,1536]{0,1:T(8,128)(2,1)S(1)}, u32[]{:S(2)}, u32[]{:S(2)}) collective-permute-start(bf16[48,1536]{0,1:T(8,128)(2,1)S(1)} %constant_dynamic-slice_fusion.11), channel_id=1, source_target_pairs={{0,32},{32,64},{64,96},{96,128},{128,160},{160,192},{192,224},{1,3... | collective-permute-start | bytes 442376 | tf_op jit(solution)/shard_map/ppermute | solution.py:114
  367.9 10.9 %collective-permute-start.6 = (bf16[48,1536]{0,1:T(8,128)(2,1)S(1)}, bf16[48,1536]{0,1:T(8,128)(2,1)S(1)}, u32[]{:S(2)}, u32[]{:S(2)}) collective-permute-start(bf16[48,1536]{0,1:T(8,128)(2,1)S(1)} %constant_dynamic-slice_fusion.10), channel_id=1, source_target_pairs={{0,32},{32,64},{64,96},{96,128},{128,160},{160,192},{192,224},{1,3... | collective-permute-start | bytes 442376 | tf_op jit(solution)/shard_map/ppermute | solution.py:114
  385.4 10.9 %collective-permute-start.7 = (bf16[48,1536]{0,1:T(8,128)(2,1)S(1)}, bf16[48,1536]{0,1:T(8,128)(2,1)S(1)}, u32[]{:S(2)}, u32[]{:S(2)}) collective-permute-start(bf16[48,1536]{0,1:T(8,128)(2,1)S(1)} %constant_dynamic-slice_fusion.9), channel_id=1, source_target_pairs={{0,32},{32,64},{64,96},{96,128},{128,160},{160,192},{192,224},{1,3... | collective-permute-start | bytes 442376 | tf_op jit(solution)/shard_map/ppermute | solution.py:114
  403.0 10.9 %collective-permute-start.8 = (bf16[48,1536]{0,1:T(8,128)(2,1)S(1)}, bf16[48,1536]{0,1:T(8,128)(2,1)S(1)}, u32[]{:S(2)}, u32[]{:S(2)}) collective-permute-start(bf16[48,1536]{0,1:T(8,128)(2,1)S(1)} %constant_dynamic-slice_fusion.8), channel_id=1, source_target_pairs={{0,32},{32,64},{64,96},{96,128},{128,160},{160,192},{192,224},{1,3... | collective-permute-start | bytes 442376 | tf_op jit(solution)/shard_map/ppermute | solution.py:114
  420.6 10.9 %collective-permute-start.9 = (bf16[48,1536]{0,1:T(8,128)(2,1)S(1)}, bf16[48,1536]{0,1:T(8,128)(2,1)S(1)}, u32[]{:S(2)}, u32[]{:S(2)}) collective-permute-start(bf16[48,1536]{0,1:T(8,128)(2,1)S(1)} %constant_dynamic-slice_fusion.7), channel_id=1, source_target_pairs={{0,32},{32,64},{64,96},{96,128},{128,160},{160,192},{192,224},{1,3... | collective-permute-start | bytes 442376 | tf_op jit(solution)/shard_map/ppermute | solution.py:114
  438.0 9.6 %collective-permute-start.11 = (bf16[192,192]{0,1:T(8,128)(2,1)S(1)}, bf16[192,192]{0,1:T(8,128)(2,1)S(1)}, u32[]{:S(2)}, u32[]{:S(2)}) collective-permute-start(bf16[192,192]{0,1:T(8,128)(2,1)S(1)} %get-tuple-element.12), channel_id=1, source_target_pairs={{0,6},{1,7},{2,0},{3,1},{4,2},{5,3},{6,4},{7,5},{8,14},{9,15},{10,... | collective-permute-start | bytes 221192 | tf_op jit(solution)/shard_map/ppermute | solution.py:132
  438.1 9.6 %collective-permute-start.12 = (bf16[192,192]{0,1:T(8,128)(2,1)S(1)}, bf16[192,192]{0,1:T(8,128)(2,1)S(1)}, u32[]{:S(2)}, u32[]{:S(2)}) collective-permute-start(bf16[192,192]{0,1:T(8,128)(2,1)S(1)} %get-tuple-element.11), channel_id=1, source_target_pairs={{0,5},{1,6},{2,7},{3,0},{4,1},{5,2},{6,3},{7,4},{8,13},{9,14},{10,... | collective-permute-start | bytes 221192 | tf_op jit(solution)/shard_map/ppermute | solution.py:132
  438.2 11.2 %collective-permute-start.13 = (bf16[192,192]{0,1:T(8,128)(2,1)S(1)}, bf16[192,192]{0,1:T(8,128)(2,1)S(1)}, u32[]{:S(2)}, u32[]{:S(2)}) collective-permute-start(bf16[192,192]{0,1:T(8,128)(2,1)S(1)} %get-tuple-element.10), channel_id=1, source_target_pairs={{0,4},{1,5},{2,6},{3,7},{4,0},{5,1},{6,2},{7,3},{8,12},{9,13},{10,... | collective-permute-start | bytes 221192 | tf_op jit(solution)/shard_map/ppermute | solution.py:132
  438.3 11.1 %collective-permute-start.14 = (bf16[192,192]{0,1:T(8,128)(2,1)S(1)}, bf16[192,192]{0,1:T(8,128)(2,1)S(1)}, u32[]{:S(2)}, u32[]{:S(2)}) collective-permute-start(bf16[192,192]{0,1:T(8,128)(2,1)S(1)} %get-tuple-element.9), channel_id=1, source_target_pairs={{0,3},{1,4},{2,5},{3,6},{4,7},{5,0},{6,1},{7,2},{8,11},{9,12},{10,... | collective-permute-start | bytes 221192 | tf_op jit(solution)/shard_map/ppermute | solution.py:132
  441.1 8.3 %collective-permute-start.15 = (bf16[192,192]{0,1:T(8,128)(2,1)S(1)}, bf16[192,192]{0,1:T(8,128)(2,1)S(1)}, u32[]{:S(2)}, u32[]{:S(2)}) collective-permute-start(bf16[192,192]{0,1:T(8,128)(2,1)S(1)} %get-tuple-element.8), channel_id=1, source_target_pairs={{0,2},{1,3},{2,4},{3,5},{4,6},{5,7},{6,0},{7,1},{8,10},{9,11},{10,... | collective-permute-start | bytes 221192 | tf_op jit(solution)/shard_map/ppermute | solution.py:132
  447.6 4.0 collective-permute-start.16
  447.6 4.0 collective-permute-start.10
Sparse Core Ops, SparseCore 0:
  31.3 131.2 reduce-scatter.1
  170.7 76.3 all-reduce.1

commit v3 on v2

--- a/solution.py
+++ b/solution.py
@@ -9,7 +9,8 @@
 BLK = 512
 ACTIVE_SLOTS = 3
 LAYERS = 8
-CHUNKS = 4
+CHUNKS = 1
+ROW_TILES = 3
 
 
 def select_kernel(src_loc, tgt_loc, src_live, tgt_live, dec_ref, enc_ref, act_ref, out_ref):
@@ -36,24 +37,29 @@
     prompts = activation.shape[0]
     slots = ACTIVE_SLOTS
 
-    def dec_map(p, j, sl, tl, sv, tv):
+    tile = rows // ROW_TILES
+
+    def dec_map(p, j, r, sl, tl, sv, tv):
+        return (r, sl[p, jnp.minimum(j, slots - 1)])
+
+    def enc_map(p, j, r, sl, tl, sv, tv):
+        return (r, tl[p, jnp.maximum(j - slots, 0)])
+
+    def act_map(p, j, r, sl, tl, sv, tv):
         return (0, sl[p, jnp.minimum(j, slots - 1)])
 
-    def enc_map(p, j, sl, tl, sv, tv):
-        return (0, tl[p, jnp.maximum(j - slots, 0)])
-
-    def out_map(p, j, sl, tl, sv, tv):
-        return (p, 0, j)
+    def out_map(p, j, r, sl, tl, sv, tv):
+        return (p, r, j)
 
     grid_spec = pltpu.PrefetchScalarGridSpec(
         num_scalar_prefetch=4,
-        grid=(prompts, 2 * slots),
+        grid=(prompts, 2 * slots, ROW_TILES),
         in_specs=[
-            pl.BlockSpec((rows, BLK), dec_map),
-            pl.BlockSpec((rows, BLK), enc_map),
-            pl.BlockSpec((prompts, BLK), dec_map),
+            pl.BlockSpec((tile, BLK), dec_map),
+            pl.BlockSpec((tile, BLK), enc_map),
+            pl.BlockSpec((prompts, BLK), act_map),
         ],
-        out_specs=pl.BlockSpec((1, rows, BLK), out_map),
+        out_specs=pl.BlockSpec((1, tile, BLK), out_map),
     )
     block_bytes = rows * BLK * 2
     return pl.pallas_call(

time: 463 us -> 453 us (0.978)
  Pallas kernels: 21.3 us -> 45.6 us
  local copies, waits for them, and re-layouts: 30.7 us -> 8.64 us
  matrix products: 43 us -> 34.2 us
  starting transfers between devices: 27.1 us -> 19.4 us
  waiting for transfers between devices: 316 us -> 321 us
    pallas_call x1, Pallas kernels: 21.3 us -> 45.6 us  [select_blocks(): pl.pallas_call(select_kernel, grid_spec=grid_spec, out_shape=jax.ShapeDty...]
    dynamic_update_slice x10 -> x0, local copies, waits for them, and re-layouts: 24.1 us -> none  [on_device(): lax.dynamic_update_slice_in_dim(mine, jnp.where(valid, product, kept), pl...]
    dot_general x10 -> x7, matrix products: 34.9 us -> 26.2 us  [on_device(): lax.dot_general(previous, edges, (((1,), (1,)), ((), ())), preferred_elem...]
    ppermute x10 -> x7, starting transfers between devices: 20.2 us -> 14.3 us  [on_device(): previous = lax.ppermute(outgoing, 'lg', forward)]
    ppermute x10 -> x7, waiting for transfers between devices: 103 us -> 106 us  [on_device(): previous = lax.ppermute(outgoing, 'lg', forward)]
  transfers between devices with their start and end apart: 19 -> 16, of which waited for: 14 -> 12; matrix products, arithmetic and copies ran while one was open for 0% -> 0% of each run, Pallas kernels for 0% -> 0%
where the time goes in v3:
time: 453 us; the launch traced here: 451 us
  waiting for transfers between devices  321 us (71%)
  Pallas kernels  45.6 us (10%)
  matrix products  34.2 us (8%)
  starting transfers between devices  19.4 us (4%)
  between operations  14.6 us (3%)
  local copies, waits for them, and re-layouts  8.64 us (2%)
  other arithmetic  7.76 us (2%)
    reduce_scatter x1, waiting for transfers between devices, on_device(): combined = lax.psum_scatter(combined, 'q', scatter_dimension=0, tiled=True)  131 us
    ppermute x7, waiting for transfers between devices, on_device(): previous = lax.ppermute(outgoing, 'lg', forward)  106 us
    psum x1, waiting for transfers between devices, on_device(): gram_sum = lax.psum(partial_gram, 'fblk').astype(jnp.float32)  74.6 us
    pallas_call x1, Pallas kernels, select_blocks(): pl.pallas_call(select_kernel, grid_spec=grid_spec, out_shape=jax.ShapeDty...  45.6 us
    dot_general x7, matrix products, on_device(): lax.dot_general(previous, edges, (((1,), (1,)), ((), ())), preferred_elem...  26.2 us
    ppermute x7, starting transfers between devices, on_device(): previous = lax.ppermute(outgoing, 'lg', forward)  14.3 us
    ppermute x7, waiting for transfers between devices, on_device(): piece = lax.ppermute(piece, 'fblk', pairs)  9.08 us
  transfers between devices with their start and end apart: 16, of which 12 were waited for; matrix products, arithmetic and copies ran while one was open for 0% of the time, Pallas kernels for 0%

profile of v3, /device:TPU:134, one launch (start us, length us, event | category | flops | bytes accessed | tf_op | source)
XLA Modules:
  0.0 451.5 jit_solution(10100220463294157297)
XLA Ops:
  9.8 45.6 %shard_map.55 = bf16[4,576,3072]{2,1,0:T(8,128)(2,1)} custom-call(s32[4,3]{1,0:T(4,128)} %get-tuple-element.18.src_loc, s32[4,3]{1,0:T(4,128)} %get-tuple-element.17.tgt_loc, s32[4,3]{1,0:T(4,128)} %get-tuple-element.19.src_live, s32[4,3]{1,0:T(4,128)} %get-tuple-element.20.tgt_live, bf16[576,4096]{1,0:T(8,128)(2,1)} %dec_ref.1, bf16[576,4096]{1,0:T(8,128)(2,1)} %enc_ref.1, ...), custom_call_target="tpu_custom_call" | custom-call | flops 3538944 | bytes 28311552 | tf_op jit(solution)/shard_map/pallas_call | solution.py:65
  55.5 131.4 %reduce-scatter.2.cloned.1.call-done = bf16[1,576,3072]{2,1,0:T(8,128)(2,1)} async-done(((bf16[4,576,3072]{2,1,0:T(8,128)(2,1)}), bf16[1,576,3072]{2,1,0:T(8,128)(2,1)}) %reduce-scatter.2.cloned.1.call-update) | async-done | bytes 3538960 | tf_op jit(solution)/shard_map/reduce_scatter | solution.py:98
  186.9 8.0 %convolution_convert_fusion = bf16[1536,1536]{1,0:T(8,128)(2,1)} fusion(bf16[1,576,3072]{2,1,0:T(8,128)(2,1)} %reduce-scatter.2.cloned.1.call-done), kind=kOutput, calls=%fused_computation.5 | convolution fusion | flops 2720268288 | bytes 8257536 | tf_op jit(solution)/shard_map/dot_general | solution.py:102
  196.9 74.6 %all-reduce.2.cloned.1.call-done = bf16[1536,1536]{1,0:T(8,128)(2,1)} async-done(((bf16[1536,1536]{1,0:T(8,128)(2,1)}), bf16[1536,1536]{1,0:T(8,128)(2,1)}) %all-reduce.2.cloned.1.call-update) | async-done | bytes 4718608 | tf_op jit(solution)/shard_map/psum | solution.py:105
  271.5 3.5 fusion.2
  275.3 1.9 fusion.1
  277.2 2.1 copy-done.1
  279.9 2.6 collective-permute-start
  282.5 15.4 %collective-permute-done = bf16[192,1536]{1,0:T(8,128)(2,1)S(1)} collective-permute-done((bf16[192,1536]{1,0:T(8,128)(2,1)S(1)}, bf16[192,1536]{1,0:T(8,128)(2,1)S(1)}, u32[]{:S(2)}, u32[]{:S(2)}) %collective-permute-start) | collective-permute-done | bytes 589856 | tf_op jit(solution)/shard_map/ppermute | solution.py:120
  297.9 3.7 fusion.3
  301.9 1.9 collective-permute-start.1
  303.9 17.2 %collective-permute-done.1 = bf16[192,1536]{1,0:T(8,128)(2,1)S(1)} collective-permute-done((bf16[192,1536]{1,0:T(8,128)(2,1)S(1)}, bf16[192,1536]{1,0:T(8,128)(2,1)S(1)}, u32[]{:S(2)}, u32[]{:S(2)}) %collective-permute-start.1) | collective-permute-done | bytes 589856 | tf_op jit(solution)/shard_map/ppermute | solution.py:120
  321.0 3.7 fusion.4
  325.0 1.9 collective-permute-start.2
  327.0 16.5 %collective-permute-done.2 = bf16[192,1536]{1,0:T(8,128)(2,1)S(1)} collective-permute-done((bf16[192,1536]{1,0:T(8,128)(2,1)S(1)}, bf16[192,1536]{1,0:T(8,128)(2,1)S(1)}, u32[]{:S(2)}, u32[]{:S(2)}) %collective-permute-start.2) | collective-permute-done | bytes 589856 | tf_op jit(solution)/shard_map/ppermute | solution.py:120
  343.5 3.7 fusion.5
  347.5 2.1 collective-permute-start.3
  349.6 15.5 %collective-permute-done.3 = bf16[192,1536]{1,0:T(8,128)(2,1)S(1)} collective-permute-done((bf16[192,1536]{1,0:T(8,128)(2,1)S(1)}, bf16[192,1536]{1,0:T(8,128)(2,1)S(1)}, u32[]{:S(2)}, u32[]{:S(2)}) %collective-permute-start.3) | collective-permute-done | bytes 589856 | tf_op jit(solution)/shard_map/ppermute | solution.py:120
  365.1 3.7 fusion.6
  369.1 1.9 collective-permute-start.4
  371.1 14.8 %collective-permute-done.4 = bf16[192,1536]{1,0:T(8,128)(2,1)S(1)} collective-permute-done((bf16[192,1536]{1,0:T(8,128)(2,1)S(1)}, bf16[192,1536]{1,0:T(8,128)(2,1)S(1)}, u32[]{:S(2)}, u32[]{:S(2)}) %collective-permute-start.4) | collective-permute-done | bytes 589856 | tf_op jit(solution)/shard_map/ppermute | solution.py:120
  385.8 3.7 fusion.7
  389.8 1.9 collective-permute-start.5
  391.8 13.9 %collective-permute-done.5 = bf16[192,1536]{1,0:T(8,128)(2,1)S(1)} collective-permute-done((bf16[192,1536]{1,0:T(8,128)(2,1)S(1)}, bf16[192,1536]{1,0:T(8,128)(2,1)S(1)}, u32[]{:S(2)}, u32[]{:S(2)}) %collective-permute-start.5) | collective-permute-done | bytes 589856 | tf_op jit(solution)/shard_map/ppermute | solution.py:120
  405.7 3.7 fusion.8
  409.7 1.9 collective-permute-start.6
  411.8 13.0 %collective-permute-done.6 = bf16[192,1536]{1,0:T(8,128)(2,1)S(1)} collective-permute-done((bf16[192,1536]{1,0:T(8,128)(2,1)S(1)}, bf16[192,1536]{1,0:T(8,128)(2,1)S(1)}, u32[]{:S(2)}, u32[]{:S(2)}) %collective-permute-start.6) | collective-permute-done | bytes 589856 | tf_op jit(solution)/shard_map/ppermute | solution.py:120
  424.7 3.7 fusion.9
  428.9 3.5 collective-permute-start.13
  433.7 1.7 collective-permute-done.10
  435.4 1.6 collective-permute-done.13
  437.0 5.8 %collective-permute-done.8 = bf16[192,192]{0,1:T(8,128)(2,1)S(1)} collective-permute-done((bf16[192,192]{0,1:T(8,128)(2,1)S(1)}, bf16[192,192]{0,1:T(8,128)(2,1)S(1)}, u32[]{:S(2)}, u32[]{:S(2)}) %collective-permute-start.8) | collective-permute-done | bytes 73760 | tf_op jit(solution)/shard_map/ppermute | solution.py:138
  (36 shorter events, 10.6 us)
Async XLA Ops:
  6.5 180.4 %reduce-scatter.2.cloned.1.call-start = ((), (), s32[]{:S(2)}) async-start(), calls=%async_computation.1 | async-start | bytes 17694720 | tf_op jit(solution)/shard_map/reduce_scatter | solution.py:98
  55.5 216.1 %all-reduce.2.cloned.1.call-start = ((), (), s32[]{:S(2)}) async-start(), calls=%async_computation.2 | async-start | bytes 9437184 | tf_op jit(solution)/shard_map/psum | solution.py:105
  271.5 3.8 copy-start
  277.2 2.1 copy-start.1
  279.9 18.0 %collective-permute-start = (bf16[192,1536]{1,0:T(8,128)(2,1)S(1)}, bf16[192,1536]{1,0:T(8,128)(2,1)S(1)}, u32[]{:S(2)}, u32[]{:S(2)}) collective-permute-start(bf16[192,1536]{1,0:T(8,128)(2,1)S(1)} %copy.17), channel_id=1, source_target_pairs={{0,32},{32,64},{64,96},{96,128},{128,160},{160,192},{192,224},{1,3... | collective-permute-start | bytes 1769480 | tf_op jit(solution)/shard_map/ppermute | solution.py:120
  301.9 19.1 %collective-permute-start.1 = (bf16[192,1536]{1,0:T(8,128)(2,1)S(1)}, bf16[192,1536]{1,0:T(8,128)(2,1)S(1)}, u32[]{:S(2)}, u32[]{:S(2)}) collective-permute-start(bf16[192,1536]{1,0:T(8,128)(2,1)S(1)} %copy.19), channel_id=1, source_target_pairs={{0,32},{32,64},{64,96},{96,128},{128,160},{160,192},{192,224},{1,3... | collective-permute-start | bytes 1769480 | tf_op jit(solution)/shard_map/ppermute | solution.py:120
  325.0 18.4 %collective-permute-start.2 = (bf16[192,1536]{1,0:T(8,128)(2,1)S(1)}, bf16[192,1536]{1,0:T(8,128)(2,1)S(1)}, u32[]{:S(2)}, u32[]{:S(2)}) collective-permute-start(bf16[192,1536]{1,0:T(8,128)(2,1)S(1)} %copy.21), channel_id=1, source_target_pairs={{0,32},{32,64},{64,96},{96,128},{128,160},{160,192},{192,224},{1,3... | collective-permute-start | bytes 1769480 | tf_op jit(solution)/shard_map/ppermute | solution.py:120
  347.5 17.6 %collective-permute-start.3 = (bf16[192,1536]{1,0:T(8,128)(2,1)S(1)}, bf16[192,1536]{1,0:T(8,128)(2,1)S(1)}, u32[]{:S(2)}, u32[]{:S(2)}) collective-permute-start(bf16[192,1536]{1,0:T(8,128)(2,1)S(1)} %copy.23), channel_id=1, source_target_pairs={{0,32},{32,64},{64,96},{96,128},{128,160},{160,192},{192,224},{1,3... | collective-permute-start | bytes 1769480 | tf_op jit(solution)/shard_map/ppermute | solution.py:120
  369.1 16.7 %collective-permute-start.4 = (bf16[192,1536]{1,0:T(8,128)(2,1)S(1)}, bf16[192,1536]{1,0:T(8,128)(2,1)S(1)}, u32[]{:S(2)}, u32[]{:S(2)}) collective-permute-start(bf16[192,1536]{1,0:T(8,128)(2,1)S(1)} %copy.25), channel_id=1, source_target_pairs={{0,32},{32,64},{64,96},{96,128},{128,160},{160,192},{192,224},{1,3... | collective-permute-start | bytes 1769480 | tf_op jit(solution)/shard_map/ppermute | solution.py:120
  389.8 15.9 %collective-permute-start.5 = (bf16[192,1536]{1,0:T(8,128)(2,1)S(1)}, bf16[192,1536]{1,0:T(8,128)(2,1)S(1)}, u32[]{:S(2)}, u32[]{:S(2)}) collective-permute-start(bf16[192,1536]{1,0:T(8,128)(2,1)S(1)} %copy.27), channel_id=1, source_target_pairs={{0,32},{32,64},{64,96},{96,128},{128,160},{160,192},{192,224},{1,3... | collective-permute-start | bytes 1769480 | tf_op jit(solution)/shard_map/ppermute | solution.py:120
  409.7 15.0 %collective-permute-start.6 = (bf16[192,1536]{1,0:T(8,128)(2,1)S(1)}, bf16[192,1536]{1,0:T(8,128)(2,1)S(1)}, u32[]{:S(2)}, u32[]{:S(2)}) collective-permute-start(bf16[192,1536]{1,0:T(8,128)(2,1)S(1)} %copy.29), channel_id=1, source_target_pairs={{0,32},{32,64},{64,96},{96,128},{128,160},{160,192},{192,224},{1,3... | collective-permute-start | bytes 1769480 | tf_op jit(solution)/shard_map/ppermute | solution.py:120
  428.6 6.8 %collective-permute-start.10 = (bf16[192,192]{0,1:T(8,128)(2,1)S(1)}, bf16[192,192]{0,1:T(8,128)(2,1)S(1)}, u32[]{:S(2)}, u32[]{:S(2)}) collective-permute-start(bf16[192,192]{0,1:T(8,128)(2,1)S(1)} %get-tuple-element.10), channel_id=1, source_target_pairs={{0,4},{1,5},{2,6},{3,7},{4,0},{5,1},{6,2},{7,3},{8,12},{9,13},{10,... | collective-permute-start | bytes 221192 | tf_op jit(solution)/shard_map/ppermute | solution.py:138
  428.7 6.7 %collective-permute-start.11 = (bf16[192,192]{0,1:T(8,128)(2,1)S(1)}, bf16[192,192]{0,1:T(8,128)(2,1)S(1)}, u32[]{:S(2)}, u32[]{:S(2)}) collective-permute-start(bf16[192,192]{0,1:T(8,128)(2,1)S(1)} %get-tuple-element.9), channel_id=1, source_target_pairs={{0,3},{1,4},{2,5},{3,6},{4,7},{5,0},{6,1},{7,2},{8,11},{9,12},{10,... | collective-permute-start | bytes 221192 | tf_op jit(solution)/shard_map/ppermute | solution.py:138
  428.8 6.7 %collective-permute-start.12 = (bf16[192,192]{0,1:T(8,128)(2,1)S(1)}, bf16[192,192]{0,1:T(8,128)(2,1)S(1)}, u32[]{:S(2)}, u32[]{:S(2)}) collective-permute-start(bf16[192,192]{0,1:T(8,128)(2,1)S(1)} %get-tuple-element.8), channel_id=1, source_target_pairs={{0,2},{1,3},{2,4},{3,5},{4,6},{5,7},{6,0},{7,1},{8,10},{9,11},{10,... | collective-permute-start | bytes 221192 | tf_op jit(solution)/shard_map/ppermute | solution.py:138
  428.9 8.1 %collective-permute-start.13 = (bf16[192,192]{0,1:T(8,128)(2,1)S(1)}, bf16[192,192]{0,1:T(8,128)(2,1)S(1)}, u32[]{:S(2)}, u32[]{:S(2)}) collective-permute-start(bf16[192,192]{0,1:T(8,128)(2,1)S(1)} %get-tuple-element.7), channel_id=1, source_target_pairs={{0,1},{1,2},{2,3},{3,4},{4,5},{5,6},{6,7},{7,0},{8,9},{9,10},{10,1... | collective-permute-start | bytes 221192 | tf_op jit(solution)/shard_map/ppermute | solution.py:138
  432.3 4.7 %collective-permute-start.7 = (bf16[192,192]{0,1:T(8,128)(2,1)S(1)}, bf16[192,192]{0,1:T(8,128)(2,1)S(1)}, u32[]{:S(2)}, u32[]{:S(2)}) collective-permute-start(bf16[192,192]{0,1:T(8,128)(2,1)S(1)} %get-tuple-element.13), channel_id=1, source_target_pairs={{0,7},{1,0},{2,1},{3,2},{4,3},{5,4},{6,5},{7,6},{8,15},{9,8},{10,9... | collective-permute-start | bytes 221192 | tf_op jit(solution)/shard_map/ppermute | solution.py:138
  435.4 7.4 %collective-permute-start.8 = (bf16[192,192]{0,1:T(8,128)(2,1)S(1)}, bf16[192,192]{0,1:T(8,128)(2,1)S(1)}, u32[]{:S(2)}, u32[]{:S(2)}) collective-permute-start(bf16[192,192]{0,1:T(8,128)(2,1)S(1)} %get-tuple-element.12), channel_id=1, source_target_pairs={{0,6},{1,7},{2,0},{3,1},{4,2},{5,3},{6,4},{7,5},{8,14},{9,15},{10,... | collective-permute-start | bytes 221192 | tf_op jit(solution)/shard_map/ppermute | solution.py:138
  435.4 7.4 %collective-permute-start.9 = (bf16[192,192]{0,1:T(8,128)(2,1)S(1)}, bf16[192,192]{0,1:T(8,128)(2,1)S(1)}, u32[]{:S(2)}, u32[]{:S(2)}) collective-permute-start(bf16[192,192]{0,1:T(8,128)(2,1)S(1)} %get-tuple-element.11), channel_id=1, source_target_pairs={{0,5},{1,6},{2,7},{3,0},{4,1},{5,2},{6,3},{7,4},{8,13},{9,14},{10,... | collective-permute-start | bytes 221192 | tf_op jit(solution)/shard_map/ppermute | solution.py:138
Sparse Core Ops, SparseCore 0:
  55.6 131.2 reduce-scatter.1
  195.1 76.4 all-reduce.1

commit v4 on v2

--- a/solution.py
+++ b/solution.py
@@ -9,26 +9,44 @@
 BLK = 512
 ACTIVE_SLOTS = 3
 LAYERS = 8
-CHUNKS = 4
+CHUNKS = 1
+ROW_TILE = 64
 
 
 def select_kernel(src_loc, tgt_loc, src_live, tgt_live, dec_ref, enc_ref, act_ref, out_ref):
     prompt = pl.program_id(0)
     column = pl.program_id(1)
+    rows = dec_ref.shape[0]
+    steps = rows // ROW_TILE
 
     @pl.when(column < ACTIVE_SLOTS)
     def _():
         weights = act_ref[...].astype(jnp.float32)
         row = lax.broadcasted_iota(jnp.int32, weights.shape, 0)
         factor = jnp.sum(jnp.where(row == prompt, weights, 0.0), axis=0, keepdims=True)
-        value = dec_ref[...].astype(jnp.float32) * factor
         live = src_live[prompt, column] > 0
-        out_ref[0] = jnp.where(live, value, 0.0).astype(out_ref.dtype)
+
+        def body(index, carry):
+            lower = pl.multiple_of(index * ROW_TILE, ROW_TILE)
+            value = dec_ref[pl.ds(lower, ROW_TILE), :].astype(jnp.float32) * factor
+            out_ref[0, pl.ds(lower, ROW_TILE), :] = jnp.where(live, value, 0.0).astype(
+                out_ref.dtype
+            )
+            return carry
+
+        lax.fori_loop(0, steps, body, 0)
 
     @pl.when(column >= ACTIVE_SLOTS)
     def _():
         live = tgt_live[prompt, column - ACTIVE_SLOTS] > 0
-        out_ref[0] = jnp.where(live, enc_ref[...], jnp.zeros_like(enc_ref[...]))
+
+        def body(index, carry):
+            lower = pl.multiple_of(index * ROW_TILE, ROW_TILE)
+            value = enc_ref[pl.ds(lower, ROW_TILE), :]
+            out_ref[0, pl.ds(lower, ROW_TILE), :] = jnp.where(live, value, jnp.zeros_like(value))
+            return carry
+
+        lax.fori_loop(0, steps, body, 0)
 
 
 def select_blocks(decoder, encoder, activation, src_loc, tgt_loc, src_live, tgt_live):
@@ -105,16 +123,17 @@
         jnp.bfloat16
     )
 
-    mine = lax.dynamic_slice_in_dim(edges, fblk * share, share, 1).T
+    edges_t = edges.T
+    mine = lax.dynamic_slice_in_dim(edges_t, fblk * share, share, 0)
     width = share // CHUNKS
     forward = [(index, index + 1) for index in range(group_count - 1)]
     for step in range(1, group_count + CHUNKS - 1):
         sent = jnp.clip(step - 1 - layer_group, 0, CHUNKS - 1)
         outgoing = lax.dynamic_slice_in_dim(mine, sent * width, width, 0)
         previous = lax.ppermute(outgoing, "lg", forward)
-        product = lax.dot_general(
-            previous, edges, (((1,), (1,)), ((), ())), preferred_element_type=jnp.float32
-        ).astype(jnp.bfloat16)
+        product = jnp.dot(previous, edges_t, preferred_element_type=jnp.float32).astype(
+            jnp.bfloat16
+        )
         chunk = step - layer_group
         valid = (layer_group >= 1) & (chunk >= 0) & (chunk < CHUNKS)
         place = jnp.clip(chunk, 0, CHUNKS - 1)

time: 463 us -> 429 us (0.927)
  local copies, waits for them, and re-layouts: 30.7 us -> 8.64 us
  matrix products: 43 us -> 34.2 us
  starting transfers between devices: 27.1 us -> 19.4 us
  waiting for transfers between devices: 316 us -> 321 us
    dynamic_update_slice x10 -> x0, local copies, waits for them, and re-layouts: 24.1 us -> none  [on_device(): lax.dynamic_update_slice_in_dim(mine, jnp.where(valid, product, kept), pl...]
    dot_general x10 -> x7, matrix products: 34.9 us -> 26.2 us  [on_device(): jnp.dot(previous, edges_t, preferred_element_type=jnp.float32)]
    ppermute x10 -> x7, starting transfers between devices: 20.2 us -> 14.3 us  [on_device(): previous = lax.ppermute(outgoing, 'lg', forward)]
    ppermute x10 -> x7, waiting for transfers between devices: 103 us -> 106 us  [on_device(): previous = lax.ppermute(outgoing, 'lg', forward)]
  transfers between devices with their start and end apart: 19 -> 16, of which waited for: 14 -> 12; matrix products, arithmetic and copies ran while one was open for 0% -> 0% of each run, Pallas kernels for 0% -> 0%
where the time goes in v4:
time: 429 us; the launch traced here: 428 us
  waiting for transfers between devices  321 us (75%)
  matrix products  34.2 us (8%)
  Pallas kernels  22.2 us (5%)
  starting transfers between devices  19.4 us (5%)
  between operations  14.6 us (3%)
  local copies, waits for them, and re-layouts  8.64 us (2%)
  other arithmetic  7.76 us (2%)
    reduce_scatter x1, waiting for transfers between devices, on_device(): combined = lax.psum_scatter(combined, 'q', scatter_dimension=0, tiled=True)  131 us
    ppermute x7, waiting for transfers between devices, on_device(): previous = lax.ppermute(outgoing, 'lg', forward)  106 us
    psum x1, waiting for transfers between devices, on_device(): gram_sum = lax.psum(partial_gram, 'fblk').astype(jnp.float32)  74.6 us
    dot_general x7, matrix products, on_device(): jnp.dot(previous, edges_t, preferred_element_type=jnp.float32)  26.2 us
    pallas_call x1, Pallas kernels, select_blocks(): pl.pallas_call(select_kernel, grid_spec=grid_spec, out_shape=jax.ShapeDty...  22.2 us
    ppermute x7, starting transfers between devices, on_device(): previous = lax.ppermute(outgoing, 'lg', forward)  14.3 us
    ppermute x7, waiting for transfers between devices, on_device(): piece = lax.ppermute(piece, 'fblk', pairs)  9.08 us
  transfers between devices with their start and end apart: 16, of which 12 were waited for; matrix products, arithmetic and copies ran while one was open for 0% of the time, Pallas kernels for 0%

profile of v4, /device:TPU:134, one launch (start us, length us, event | category | flops | bytes accessed | tf_op | source)
XLA Modules:
  0.0 428.1 jit_solution(12356158382190174592)
XLA Ops:
  9.8 22.2 %shard_map.55 = bf16[4,576,3072]{2,1,0:T(8,128)(2,1)} custom-call(s32[4,3]{1,0:T(4,128)} %get-tuple-element.18.src_loc, s32[4,3]{1,0:T(4,128)} %get-tuple-element.17.tgt_loc, s32[4,3]{1,0:T(4,128)} %get-tuple-element.19.src_live, s32[4,3]{1,0:T(4,128)} %get-tuple-element.20.tgt_live, bf16[576,4096]{1,0:T(8,128)(2,1)} %dec_ref.1, bf16[576,4096]{1,0:T(8,128)(2,1)} %enc_ref.1, ...), custom_call_target="tpu_custom_call" | custom-call | flops 3538944 | bytes 28311552 | tf_op jit(solution)/shard_map/pallas_call | solution.py:77
  32.1 131.4 %reduce-scatter.2.cloned.1.call-done = bf16[1,576,3072]{2,1,0:T(8,128)(2,1)} async-done(((bf16[4,576,3072]{2,1,0:T(8,128)(2,1)}), bf16[1,576,3072]{2,1,0:T(8,128)(2,1)}) %reduce-scatter.2.cloned.1.call-update) | async-done | bytes 3538960 | tf_op jit(solution)/shard_map/reduce_scatter | solution.py:110
  163.5 8.0 %convolution_convert_fusion = bf16[1536,1536]{1,0:T(8,128)(2,1)} fusion(bf16[1,576,3072]{2,1,0:T(8,128)(2,1)} %reduce-scatter.2.cloned.1.call-done), kind=kOutput, calls=%fused_computation.5 | convolution fusion | flops 2720268288 | bytes 8257536 | tf_op jit(solution)/shard_map/dot_general | solution.py:114
  173.5 74.6 %all-reduce.2.cloned.1.call-done = bf16[1536,1536]{1,0:T(8,128)(2,1)} async-done(((bf16[1536,1536]{1,0:T(8,128)(2,1)}), bf16[1536,1536]{1,0:T(8,128)(2,1)}) %all-reduce.2.cloned.1.call-update) | async-done | bytes 4718608 | tf_op jit(solution)/shard_map/psum | solution.py:117
  248.1 3.5 fusion.2
  251.9 1.9 fusion.1
  253.8 2.1 copy-done.1
  256.5 2.6 collective-permute-start
  259.1 15.4 %collective-permute-done = bf16[192,1536]{1,0:T(8,128)(2,1)S(1)} collective-permute-done((bf16[192,1536]{1,0:T(8,128)(2,1)S(1)}, bf16[192,1536]{1,0:T(8,128)(2,1)S(1)}, u32[]{:S(2)}, u32[]{:S(2)}) %collective-permute-start) | collective-permute-done | bytes 589856 | tf_op jit(solution)/shard_map/ppermute | solution.py:133
  274.5 3.7 fusion.3
  278.5 1.9 collective-permute-start.1
  280.4 17.2 %collective-permute-done.1 = bf16[192,1536]{1,0:T(8,128)(2,1)S(1)} collective-permute-done((bf16[192,1536]{1,0:T(8,128)(2,1)S(1)}, bf16[192,1536]{1,0:T(8,128)(2,1)S(1)}, u32[]{:S(2)}, u32[]{:S(2)}) %collective-permute-start.1) | collective-permute-done | bytes 589856 | tf_op jit(solution)/shard_map/ppermute | solution.py:133
  297.6 3.7 fusion.4
  301.6 1.9 collective-permute-start.2
  303.6 16.5 %collective-permute-done.2 = bf16[192,1536]{1,0:T(8,128)(2,1)S(1)} collective-permute-done((bf16[192,1536]{1,0:T(8,128)(2,1)S(1)}, bf16[192,1536]{1,0:T(8,128)(2,1)S(1)}, u32[]{:S(2)}, u32[]{:S(2)}) %collective-permute-start.2) | collective-permute-done | bytes 589856 | tf_op jit(solution)/shard_map/ppermute | solution.py:133
  320.1 3.7 fusion.5
  324.1 2.1 collective-permute-start.3
  326.2 15.5 %collective-permute-done.3 = bf16[192,1536]{1,0:T(8,128)(2,1)S(1)} collective-permute-done((bf16[192,1536]{1,0:T(8,128)(2,1)S(1)}, bf16[192,1536]{1,0:T(8,128)(2,1)S(1)}, u32[]{:S(2)}, u32[]{:S(2)}) %collective-permute-start.3) | collective-permute-done | bytes 589856 | tf_op jit(solution)/shard_map/ppermute | solution.py:133
  341.7 3.7 fusion.6
  345.7 1.9 collective-permute-start.4
  347.6 14.8 %collective-permute-done.4 = bf16[192,1536]{1,0:T(8,128)(2,1)S(1)} collective-permute-done((bf16[192,1536]{1,0:T(8,128)(2,1)S(1)}, bf16[192,1536]{1,0:T(8,128)(2,1)S(1)}, u32[]{:S(2)}, u32[]{:S(2)}) %collective-permute-start.4) | collective-permute-done | bytes 589856 | tf_op jit(solution)/shard_map/ppermute | solution.py:133
  362.4 3.7 fusion.7
  366.5 1.9 collective-permute-start.5
  368.4 13.9 %collective-permute-done.5 = bf16[192,1536]{1,0:T(8,128)(2,1)S(1)} collective-permute-done((bf16[192,1536]{1,0:T(8,128)(2,1)S(1)}, bf16[192,1536]{1,0:T(8,128)(2,1)S(1)}, u32[]{:S(2)}, u32[]{:S(2)}) %collective-permute-start.5) | collective-permute-done | bytes 589856 | tf_op jit(solution)/shard_map/ppermute | solution.py:133
  382.3 3.7 fusion.8
  386.3 1.9 collective-permute-start.6
  388.4 13.0 %collective-permute-done.6 = bf16[192,1536]{1,0:T(8,128)(2,1)S(1)} collective-permute-done((bf16[192,1536]{1,0:T(8,128)(2,1)S(1)}, bf16[192,1536]{1,0:T(8,128)(2,1)S(1)}, u32[]{:S(2)}, u32[]{:S(2)}) %collective-permute-start.6) | collective-permute-done | bytes 589856 | tf_op jit(solution)/shard_map/ppermute | solution.py:133
  401.4 3.7 fusion.9
  405.5 3.5 collective-permute-start.13
  410.3 1.7 collective-permute-done.10
  412.0 1.6 collective-permute-done.13
  413.6 5.8 %collective-permute-done.8 = bf16[192,192]{0,1:T(8,128)(2,1)S(1)} collective-permute-done((bf16[192,192]{0,1:T(8,128)(2,1)S(1)}, bf16[192,192]{0,1:T(8,128)(2,1)S(1)}, u32[]{:S(2)}, u32[]{:S(2)}) %collective-permute-start.8) | collective-permute-done | bytes 73760 | tf_op jit(solution)/shard_map/ppermute | solution.py:151
  (36 shorter events, 10.6 us)
Async XLA Ops:
  6.5 157.0 %reduce-scatter.2.cloned.1.call-start = ((), (), s32[]{:S(2)}) async-start(), calls=%async_computation.1 | async-start | bytes 17694720 | tf_op jit(solution)/shard_map/reduce_scatter | solution.py:110
  32.1 216.0 %all-reduce.2.cloned.1.call-start = ((), (), s32[]{:S(2)}) async-start(), calls=%async_computation.2 | async-start | bytes 9437184 | tf_op jit(solution)/shard_map/psum | solution.py:117
  248.1 3.8 copy-start
  253.8 2.1 copy-start.1
  256.5 18.0 %collective-permute-start = (bf16[192,1536]{1,0:T(8,128)(2,1)S(1)}, bf16[192,1536]{1,0:T(8,128)(2,1)S(1)}, u32[]{:S(2)}, u32[]{:S(2)}) collective-permute-start(bf16[192,1536]{1,0:T(8,128)(2,1)S(1)} %copy.17), channel_id=1, source_target_pairs={{0,32},{32,64},{64,96},{96,128},{128,160},{160,192},{192,224},{1,3... | collective-permute-start | bytes 1769480 | tf_op jit(solution)/shard_map/ppermute | solution.py:133
  278.5 19.1 %collective-permute-start.1 = (bf16[192,1536]{1,0:T(8,128)(2,1)S(1)}, bf16[192,1536]{1,0:T(8,128)(2,1)S(1)}, u32[]{:S(2)}, u32[]{:S(2)}) collective-permute-start(bf16[192,1536]{1,0:T(8,128)(2,1)S(1)} %copy.19), channel_id=1, source_target_pairs={{0,32},{32,64},{64,96},{96,128},{128,160},{160,192},{192,224},{1,3... | collective-permute-start | bytes 1769480 | tf_op jit(solution)/shard_map/ppermute | solution.py:133
  301.6 18.5 %collective-permute-start.2 = (bf16[192,1536]{1,0:T(8,128)(2,1)S(1)}, bf16[192,1536]{1,0:T(8,128)(2,1)S(1)}, u32[]{:S(2)}, u32[]{:S(2)}) collective-permute-start(bf16[192,1536]{1,0:T(8,128)(2,1)S(1)} %copy.21), channel_id=1, source_target_pairs={{0,32},{32,64},{64,96},{96,128},{128,160},{160,192},{192,224},{1,3... | collective-permute-start | bytes 1769480 | tf_op jit(solution)/shard_map/ppermute | solution.py:133
  324.1 17.6 %collective-permute-start.3 = (bf16[192,1536]{1,0:T(8,128)(2,1)S(1)}, bf16[192,1536]{1,0:T(8,128)(2,1)S(1)}, u32[]{:S(2)}, u32[]{:S(2)}) collective-permute-start(bf16[192,1536]{1,0:T(8,128)(2,1)S(1)} %copy.23), channel_id=1, source_target_pairs={{0,32},{32,64},{64,96},{96,128},{128,160},{160,192},{192,224},{1,3... | collective-permute-start | bytes 1769480 | tf_op jit(solution)/shard_map/ppermute | solution.py:133
  345.7 16.7 %collective-permute-start.4 = (bf16[192,1536]{1,0:T(8,128)(2,1)S(1)}, bf16[192,1536]{1,0:T(8,128)(2,1)S(1)}, u32[]{:S(2)}, u32[]{:S(2)}) collective-permute-start(bf16[192,1536]{1,0:T(8,128)(2,1)S(1)} %copy.25), channel_id=1, source_target_pairs={{0,32},{32,64},{64,96},{96,128},{128,160},{160,192},{192,224},{1,3... | collective-permute-start | bytes 1769480 | tf_op jit(solution)/shard_map/ppermute | solution.py:133
  366.5 15.9 %collective-permute-start.5 = (bf16[192,1536]{1,0:T(8,128)(2,1)S(1)}, bf16[192,1536]{1,0:T(8,128)(2,1)S(1)}, u32[]{:S(2)}, u32[]{:S(2)}) collective-permute-start(bf16[192,1536]{1,0:T(8,128)(2,1)S(1)} %copy.27), channel_id=1, source_target_pairs={{0,32},{32,64},{64,96},{96,128},{128,160},{160,192},{192,224},{1,3... | collective-permute-start | bytes 1769480 | tf_op jit(solution)/shard_map/ppermute | solution.py:133
  386.3 15.0 %collective-permute-start.6 = (bf16[192,1536]{1,0:T(8,128)(2,1)S(1)}, bf16[192,1536]{1,0:T(8,128)(2,1)S(1)}, u32[]{:S(2)}, u32[]{:S(2)}) collective-permute-start(bf16[192,1536]{1,0:T(8,128)(2,1)S(1)} %copy.29), channel_id=1, source_target_pairs={{0,32},{32,64},{64,96},{96,128},{128,160},{160,192},{192,224},{1,3... | collective-permute-start | bytes 1769480 | tf_op jit(solution)/shard_map/ppermute | solution.py:133
  405.2 6.8 %collective-permute-start.10 = (bf16[192,192]{0,1:T(8,128)(2,1)S(1)}, bf16[192,192]{0,1:T(8,128)(2,1)S(1)}, u32[]{:S(2)}, u32[]{:S(2)}) collective-permute-start(bf16[192,192]{0,1:T(8,128)(2,1)S(1)} %get-tuple-element.10), channel_id=1, source_target_pairs={{0,4},{1,5},{2,6},{3,7},{4,0},{5,1},{6,2},{7,3},{8,12},{9,13},{10,... | collective-permute-start | bytes 221192 | tf_op jit(solution)/shard_map/ppermute | solution.py:151
  405.3 6.7 %collective-permute-start.11 = (bf16[192,192]{0,1:T(8,128)(2,1)S(1)}, bf16[192,192]{0,1:T(8,128)(2,1)S(1)}, u32[]{:S(2)}, u32[]{:S(2)}) collective-permute-start(bf16[192,192]{0,1:T(8,128)(2,1)S(1)} %get-tuple-element.9), channel_id=1, source_target_pairs={{0,3},{1,4},{2,5},{3,6},{4,7},{5,0},{6,1},{7,2},{8,11},{9,12},{10,... | collective-permute-start | bytes 221192 | tf_op jit(solution)/shard_map/ppermute | solution.py:151
  405.4 6.7 %collective-permute-start.12 = (bf16[192,192]{0,1:T(8,128)(2,1)S(1)}, bf16[192,192]{0,1:T(8,128)(2,1)S(1)}, u32[]{:S(2)}, u32[]{:S(2)}) collective-permute-start(bf16[192,192]{0,1:T(8,128)(2,1)S(1)} %get-tuple-element.8), channel_id=1, source_target_pairs={{0,2},{1,3},{2,4},{3,5},{4,6},{5,7},{6,0},{7,1},{8,10},{9,11},{10,... | collective-permute-start | bytes 221192 | tf_op jit(solution)/shard_map/ppermute | solution.py:151
  405.5 8.1 %collective-permute-start.13 = (bf16[192,192]{0,1:T(8,128)(2,1)S(1)}, bf16[192,192]{0,1:T(8,128)(2,1)S(1)}, u32[]{:S(2)}, u32[]{:S(2)}) collective-permute-start(bf16[192,192]{0,1:T(8,128)(2,1)S(1)} %get-tuple-element.7), channel_id=1, source_target_pairs={{0,1},{1,2},{2,3},{3,4},{4,5},{5,6},{6,7},{7,0},{8,9},{9,10},{10,1... | collective-permute-start | bytes 221192 | tf_op jit(solution)/shard_map/ppermute | solution.py:151
  408.9 4.7 %collective-permute-start.7 = (bf16[192,192]{0,1:T(8,128)(2,1)S(1)}, bf16[192,192]{0,1:T(8,128)(2,1)S(1)}, u32[]{:S(2)}, u32[]{:S(2)}) collective-permute-start(bf16[192,192]{0,1:T(8,128)(2,1)S(1)} %get-tuple-element.13), channel_id=1, source_target_pairs={{0,7},{1,0},{2,1},{3,2},{4,3},{5,4},{6,5},{7,6},{8,15},{9,8},{10,9... | collective-permute-start | bytes 221192 | tf_op jit(solution)/shard_map/ppermute | solution.py:151
  412.0 7.4 %collective-permute-start.8 = (bf16[192,192]{0,1:T(8,128)(2,1)S(1)}, bf16[192,192]{0,1:T(8,128)(2,1)S(1)}, u32[]{:S(2)}, u32[]{:S(2)}) collective-permute-start(bf16[192,192]{0,1:T(8,128)(2,1)S(1)} %get-tuple-element.12), channel_id=1, source_target_pairs={{0,6},{1,7},{2,0},{3,1},{4,2},{5,3},{6,4},{7,5},{8,14},{9,15},{10,... | collective-permute-start | bytes 221192 | tf_op jit(solution)/shard_map/ppermute | solution.py:151
  412.0 7.4 %collective-permute-start.9 = (bf16[192,192]{0,1:T(8,128)(2,1)S(1)}, bf16[192,192]{0,1:T(8,128)(2,1)S(1)}, u32[]{:S(2)}, u32[]{:S(2)}) collective-permute-start(bf16[192,192]{0,1:T(8,128)(2,1)S(1)} %get-tuple-element.11), channel_id=1, source_target_pairs={{0,5},{1,6},{2,7},{3,0},{4,1},{5,2},{6,3},{7,4},{8,13},{9,14},{10,... | collective-permute-start | bytes 221192 | tf_op jit(solution)/shard_map/ppermute | solution.py:151
Sparse Core Ops, SparseCore 0:
  32.2 131.2 reduce-scatter.1
  171.7 76.3 all-reduce.1

commit v5 on v4

--- a/solution.py
+++ b/solution.py
@@ -1,3 +1,5 @@
+import functools
+
 import jax
 import jax.numpy as jnp
 from jax import lax
@@ -13,77 +15,61 @@
 ROW_TILE = 64
 
 
-def select_kernel(src_loc, tgt_loc, src_live, tgt_live, dec_ref, enc_ref, act_ref, out_ref):
+def select_kernel(block_loc, block_live, matrix_ref, act_ref, out_ref, scaled):
     prompt = pl.program_id(0)
-    column = pl.program_id(1)
-    rows = dec_ref.shape[0]
+    slot = pl.program_id(1)
+    rows = matrix_ref.shape[0]
     steps = rows // ROW_TILE
-
-    @pl.when(column < ACTIVE_SLOTS)
-    def _():
+    live = block_live[prompt, slot] > 0
+    if scaled:
         weights = act_ref[...].astype(jnp.float32)
         row = lax.broadcasted_iota(jnp.int32, weights.shape, 0)
         factor = jnp.sum(jnp.where(row == prompt, weights, 0.0), axis=0, keepdims=True)
-        live = src_live[prompt, column] > 0
 
-        def body(index, carry):
-            lower = pl.multiple_of(index * ROW_TILE, ROW_TILE)
-            value = dec_ref[pl.ds(lower, ROW_TILE), :].astype(jnp.float32) * factor
-            out_ref[0, pl.ds(lower, ROW_TILE), :] = jnp.where(live, value, 0.0).astype(
-                out_ref.dtype
-            )
-            return carry
+    def body(index, carry):
+        lower = pl.multiple_of(index * ROW_TILE, ROW_TILE)
+        value = matrix_ref[pl.ds(lower, ROW_TILE), :]
+        if scaled:
+            value = jnp.where(live, value.astype(jnp.float32) * factor, 0.0)
+        else:
+            value = jnp.where(live, value, jnp.zeros_like(value))
+        out_ref[0, pl.ds(lower, ROW_TILE), :] = value.astype(out_ref.dtype)
+        return carry
 
-        lax.fori_loop(0, steps, body, 0)
-
-    @pl.when(column >= ACTIVE_SLOTS)
-    def _():
-        live = tgt_live[prompt, column - ACTIVE_SLOTS] > 0
-
-        def body(index, carry):
-            lower = pl.multiple_of(index * ROW_TILE, ROW_TILE)
-            value = enc_ref[pl.ds(lower, ROW_TILE), :]
-            out_ref[0, pl.ds(lower, ROW_TILE), :] = jnp.where(live, value, jnp.zeros_like(value))
-            return carry
-
-        lax.fori_loop(0, steps, body, 0)
+    lax.fori_loop(0, steps, body, 0)
 
 
-def select_blocks(decoder, encoder, activation, src_loc, tgt_loc, src_live, tgt_live):
-    rows, _ = decoder.shape
+def select_blocks(matrix, activation, block_loc, block_live, scaled):
+    rows, _ = matrix.shape
     prompts = activation.shape[0]
     slots = ACTIVE_SLOTS
 
-    def dec_map(p, j, sl, tl, sv, tv):
-        return (0, sl[p, jnp.minimum(j, slots - 1)])
+    def in_map(p, j, loc, live):
+        return (0, loc[p, j])
 
-    def enc_map(p, j, sl, tl, sv, tv):
-        return (0, tl[p, jnp.maximum(j - slots, 0)])
-
-    def out_map(p, j, sl, tl, sv, tv):
+    def out_map(p, j, loc, live):
         return (p, 0, j)
 
     grid_spec = pltpu.PrefetchScalarGridSpec(
-        num_scalar_prefetch=4,
-        grid=(prompts, 2 * slots),
+        num_scalar_prefetch=2,
+        grid=(prompts, slots),
         in_specs=[
-            pl.BlockSpec((rows, BLK), dec_map),
-            pl.BlockSpec((rows, BLK), enc_map),
-            pl.BlockSpec((prompts, BLK), dec_map),
+            pl.BlockSpec((rows, BLK), in_map),
+            pl.BlockSpec((prompts, BLK), in_map),
         ],
         out_specs=pl.BlockSpec((1, rows, BLK), out_map),
     )
     block_bytes = rows * BLK * 2
     return pl.pallas_call(
-        select_kernel,
+        functools.partial(select_kernel, scaled=scaled),
         grid_spec=grid_spec,
-        out_shape=jax.ShapeDtypeStruct((prompts, rows, 2 * slots * BLK), jnp.bfloat16),
+        out_shape=jax.ShapeDtypeStruct((prompts, rows, slots * BLK), jnp.bfloat16),
         cost_estimate=pl.CostEstimate(
             flops=prompts * slots * rows * BLK,
             transcendentals=0,
-            bytes_accessed=4 * prompts * slots * block_bytes,
+            bytes_accessed=2 * prompts * slots * block_bytes,
         ),
-    )(src_loc, tgt_loc, src_live, tgt_live, decoder, encoder, activation)
+    )(block_loc, block_live, matrix, activation)
 
 
 def slot_tables(blocks, counts, layer, quarter, local_blocks):
@@ -106,10 +92,10 @@
 
     src_loc, src_live = slot_tables(blocks, counts, layer_group, quarter, local_blocks)
     tgt_loc, tgt_live = slot_tables(blocks, counts, layer_group + 1, quarter, local_blocks)
-    combined = select_blocks(decoder, encoder, activation, src_loc, tgt_loc, src_live, tgt_live)
-    combined = lax.psum_scatter(combined, "q", scatter_dimension=0, tiled=True)
-    source = combined[0, :, :active_width]
-    target = combined[0, :, active_width:]
+    source = select_blocks(decoder, activation, src_loc, src_live, True)
+    source = lax.psum_scatter(source, "q", scatter_dimension=0, tiled=True)[0]
+    target = select_blocks(encoder, activation, tgt_loc, tgt_live, False)
+    target = lax.psum_scatter(target, "q", scatter_dimension=0, tiled=True)[0]
 
     partial_gram = lax.dot_general(
         target, source, (((0,), (0,)), ((), ())), preferred_element_type=jnp.float32

time: 429 us -> 436 us (1.016)
  waiting for transfers between devices: 321 us -> 328 us
    reduce_scatter x1 -> x2, waiting for transfers between devices: 131 us -> 138 us  [the longest x1 75.3 us: on_device(): source = lax.psum_scatter(source, 'q', scatter_dimension=0, tiled=True)[0]]
    pallas_call x1 -> x2, Pallas kernels: 22.2 us -> 21.9 us  [select_blocks(): pl.pallas_call(functools.partial(select_kernel, scaled=scaled), grid_spec...]
  transfers between devices with their start and end apart: 16 -> 17, of which waited for: 12 -> 13; matrix products, arithmetic and copies ran while one was open for 0% -> 0% of each run, Pallas kernels for 0% -> 3%
where the time goes in v5:
time: 436 us; the launch traced here: 435 us
  waiting for transfers between devices  328 us (75%)
  matrix products  34.2 us (8%)
  Pallas kernels  21.9 us (5%)
  starting transfers between devices  19.4 us (4%)
  between operations  14.3 us (3%)
  local copies, waits for them, and re-layouts  8.65 us (2%)
  other arithmetic  8.38 us (2%)
    ppermute x7, waiting for transfers between devices, on_device(): previous = lax.ppermute(outgoing, 'lg', forward)  106 us
    reduce_scatter x1, waiting for transfers between devices, on_device(): source = lax.psum_scatter(source, 'q', scatter_dimension=0, tiled=True)[0]  75.3 us
    psum x1, waiting for transfers between devices, on_device(): gram_sum = lax.psum(partial_gram, 'fblk').astype(jnp.float32)  74.6 us
    reduce_scatter x1, waiting for transfers between devices, on_device(): target = lax.psum_scatter(target, 'q', scatter_dimension=0, tiled=True)[0]  62.8 us
    dot_general x7, matrix products, on_device(): jnp.dot(previous, edges_t, preferred_element_type=jnp.float32)  26.2 us
    pallas_call x2, Pallas kernels, select_blocks(): pl.pallas_call(functools.partial(select_kernel, scaled=scaled), grid_spec...  21.9 us
    ppermute x7, starting transfers between devices, on_device(): previous = lax.ppermute(outgoing, 'lg', forward)  14.3 us
    ppermute x7, waiting for transfers between devices, on_device(): piece = lax.ppermute(piece, 'fblk', pairs)  9.08 us
  transfers between devices with their start and end apart: 17, of which 13 were waited for; matrix products, arithmetic and copies ran while one was open for 0% of the time, Pallas kernels for 3%

profile of v5, /device:TPU:134, one launch (start us, length us, event | category | flops | bytes accessed | tf_op | source)
XLA Modules:
  0.0 434.8 jit_solution(12315705422974085100)
XLA Ops:
  9.8 10.8 %shard_map.55 = bf16[4,576,1536]{2,1,0:T(8,128)(2,1)} custom-call(s32[4,3]{1,0:T(4,128)} %get-tuple-element.18.block_loc, s32[4,3]{1,0:T(4,128)} %fusion.20.block_live, bf16[576,4096]{1,0:T(8,128)(2,1)} %matrix_ref.2, bf16[4,4096]{1,0:T(4,128)(2,1)} %act_ref.3), custom_call_target="tpu_custom_call" | custom-call | flops 3538944 | bytes 14155776 | tf_op jit(solution)/shard_map/pallas_call | solution.py:63
  21.3 11.1 %shard_map.56 = bf16[4,576,1536]{2,1,0:T(8,128)(2,1)} custom-call(s32[4,3]{1,0:T(4,128)} %get-tuple-element.17.block_loc, s32[4,3]{1,0:T(4,128)} %fusion.22.block_live, bf16[576,4096]{1,0:T(8,128)(2,1)} %matrix_ref.3, bf16[4,4096]{1,0:T(4,128)(2,1)} %act_ref.3), custom_call_target="tpu_custom_call" | custom-call | flops 3538944 | bytes 14155776 | tf_op jit(solution)/shard_map/pallas_call | solution.py:63
  32.5 62.8 %reduce-scatter.3.cloned.1.call-done = bf16[1,576,1536]{2,1,0:T(8,128)(2,1)} async-done(((bf16[4,576,1536]{2,1,0:T(8,128)(2,1)}), bf16[1,576,1536]{2,1,0:T(8,128)(2,1)}) %reduce-scatter.3.cloned.1.call-update) | async-done | bytes 1769488 | tf_op jit(solution)/shard_map/reduce_scatter | solution.py:98
  95.3 75.3 %reduce-scatter.5.cloned.1.call-done = bf16[1,576,1536]{2,1,0:T(8,128)(2,1)} async-done(((bf16[4,576,1536]{2,1,0:T(8,128)(2,1)}), bf16[1,576,1536]{2,1,0:T(8,128)(2,1)}) %reduce-scatter.5.cloned.1.call-update) | async-done | bytes 1769488 | tf_op jit(solution)/shard_map/reduce_scatter | solution.py:96
  170.6 8.0 %convolution_convert_fusion = bf16[1536,1536]{1,0:T(8,128)(2,1)} fusion(bf16[1,576,1536]{2,1,0:T(8,128)(2,1)} %reduce-scatter.5.cloned.1.call-done, bf16[1,576,1536]{2,1,0:T(8,128)(2,1)} %reduce-scatter.3.cloned.1.call-done), kind=kOutput, calls=%fused_computation.5 | convolution fusion | flops 2720268288 | bytes 8257536 | tf_op jit(solution)/shard_map/dot_general | solution.py:100
  180.6 74.6 %all-reduce.2.cloned.1.call-done = bf16[1536,1536]{1,0:T(8,128)(2,1)} async-done(((bf16[1536,1536]{1,0:T(8,128)(2,1)}), bf16[1536,1536]{1,0:T(8,128)(2,1)}) %all-reduce.2.cloned.1.call-update) | async-done | bytes 4718608 | tf_op jit(solution)/shard_map/psum | solution.py:103
  255.2 3.5 fusion.2
  258.9 1.9 fusion.1
  260.9 2.1 copy-done.1
  263.6 2.6 collective-permute-start
  266.2 15.4 %collective-permute-done = bf16[192,1536]{1,0:T(8,128)(2,1)S(1)} collective-permute-done((bf16[192,1536]{1,0:T(8,128)(2,1)S(1)}, bf16[192,1536]{1,0:T(8,128)(2,1)S(1)}, u32[]{:S(2)}, u32[]{:S(2)}) %collective-permute-start) | collective-permute-done | bytes 589856 | tf_op jit(solution)/shard_map/ppermute | solution.py:119
  281.5 3.7 fusion.3
  285.6 1.9 collective-permute-start.1
  287.5 17.2 %collective-permute-done.1 = bf16[192,1536]{1,0:T(8,128)(2,1)S(1)} collective-permute-done((bf16[192,1536]{1,0:T(8,128)(2,1)S(1)}, bf16[192,1536]{1,0:T(8,128)(2,1)S(1)}, u32[]{:S(2)}, u32[]{:S(2)}) %collective-permute-start.1) | collective-permute-done | bytes 589856 | tf_op jit(solution)/shard_map/ppermute | solution.py:119
  304.7 3.7 fusion.4
  308.7 1.9 collective-permute-start.2
  310.6 16.5 %collective-permute-done.2 = bf16[192,1536]{1,0:T(8,128)(2,1)S(1)} collective-permute-done((bf16[192,1536]{1,0:T(8,128)(2,1)S(1)}, bf16[192,1536]{1,0:T(8,128)(2,1)S(1)}, u32[]{:S(2)}, u32[]{:S(2)}) %collective-permute-start.2) | collective-permute-done | bytes 589856 | tf_op jit(solution)/shard_map/ppermute | solution.py:119
  327.1 3.7 fusion.5
  331.1 2.1 collective-permute-start.3
  333.3 15.5 %collective-permute-done.3 = bf16[192,1536]{1,0:T(8,128)(2,1)S(1)} collective-permute-done((bf16[192,1536]{1,0:T(8,128)(2,1)S(1)}, bf16[192,1536]{1,0:T(8,128)(2,1)S(1)}, u32[]{:S(2)}, u32[]{:S(2)}) %collective-permute-start.3) | collective-permute-done | bytes 589856 | tf_op jit(solution)/shard_map/ppermute | solution.py:119
  348.7 3.7 fusion.6
  352.7 1.9 collective-permute-start.4
  354.7 14.8 %collective-permute-done.4 = bf16[192,1536]{1,0:T(8,128)(2,1)S(1)} collective-permute-done((bf16[192,1536]{1,0:T(8,128)(2,1)S(1)}, bf16[192,1536]{1,0:T(8,128)(2,1)S(1)}, u32[]{:S(2)}, u32[]{:S(2)}) %collective-permute-start.4) | collective-permute-done | bytes 589856 | tf_op jit(solution)/shard_map/ppermute | solution.py:119
  369.5 3.7 fusion.7
  373.5 1.9 collective-permute-start.5
  375.4 13.9 %collective-permute-done.5 = bf16[192,1536]{1,0:T(8,128)(2,1)S(1)} collective-permute-done((bf16[192,1536]{1,0:T(8,128)(2,1)S(1)}, bf16[192,1536]{1,0:T(8,128)(2,1)S(1)}, u32[]{:S(2)}, u32[]{:S(2)}) %collective-permute-start.5) | collective-permute-done | bytes 589856 | tf_op jit(solution)/shard_map/ppermute | solution.py:119
  389.4 3.7 fusion.8
  393.4 1.9 collective-permute-start.6
  395.4 13.0 %collective-permute-done.6 = bf16[192,1536]{1,0:T(8,128)(2,1)S(1)} collective-permute-done((bf16[192,1536]{1,0:T(8,128)(2,1)S(1)}, bf16[192,1536]{1,0:T(8,128)(2,1)S(1)}, u32[]{:S(2)}, u32[]{:S(2)}) %collective-permute-start.6) | collective-permute-done | bytes 589856 | tf_op jit(solution)/shard_map/ppermute | solution.py:119
  408.4 3.7 fusion.9
  412.5 3.5 collective-permute-start.13
  420.7 5.8 %collective-permute-done.8 = bf16[192,192]{0,1:T(8,128)(2,1)S(1)} collective-permute-done((bf16[192,192]{0,1:T(8,128)(2,1)S(1)}, bf16[192,192]{0,1:T(8,128)(2,1)S(1)}, u32[]{:S(2)}, u32[]{:S(2)}) %collective-permute-start.8) | collective-permute-done | bytes 73760 | tf_op jit(solution)/shard_map/ppermute | solution.py:137
  (41 shorter events, 14.6 us)
Async XLA Ops:
  6.5 88.7 %reduce-scatter.3.cloned.1.call-start = ((), (), s32[]{:S(2)}) async-start(), calls=%async_computation.2 | async-start | bytes 8847360 | tf_op jit(solution)/shard_map/reduce_scatter | solution.py:98
  20.7 149.9 %reduce-scatter.5.cloned.1.call-start = ((), (), s32[]{:S(2)}) async-start(), calls=%async_computation.3 | async-start | bytes 8847360 | tf_op jit(solution)/shard_map/reduce_scatter | solution.py:96
  32.4 222.7 %all-reduce.2.cloned.1.call-start = ((), (), s32[]{:S(2)}) async-start(), calls=%async_computation.4 | async-start | bytes 9437184 | tf_op jit(solution)/shard_map/psum | solution.py:103
  255.2 3.8 copy-start
  260.8 2.1 copy-start.1
  263.6 18.0 %collective-permute-start = (bf16[192,1536]{1,0:T(8,128)(2,1)S(1)}, bf16[192,1536]{1,0:T(8,128)(2,1)S(1)}, u32[]{:S(2)}, u32[]{:S(2)}) collective-permute-start(bf16[192,1536]{1,0:T(8,128)(2,1)S(1)} %copy.17), channel_id=1, source_target_pairs={{0,32},{32,64},{64,96},{96,128},{128,160},{160,192},{192,224},{1,3... | collective-permute-start | bytes 1769480 | tf_op jit(solution)/shard_map/ppermute | solution.py:119
  285.6 19.1 %collective-permute-start.1 = (bf16[192,1536]{1,0:T(8,128)(2,1)S(1)}, bf16[192,1536]{1,0:T(8,128)(2,1)S(1)}, u32[]{:S(2)}, u32[]{:S(2)}) collective-permute-start(bf16[192,1536]{1,0:T(8,128)(2,1)S(1)} %copy.19), channel_id=1, source_target_pairs={{0,32},{32,64},{64,96},{96,128},{128,160},{160,192},{192,224},{1,3... | collective-permute-start | bytes 1769480 | tf_op jit(solution)/shard_map/ppermute | solution.py:119
  308.7 18.5 %collective-permute-start.2 = (bf16[192,1536]{1,0:T(8,128)(2,1)S(1)}, bf16[192,1536]{1,0:T(8,128)(2,1)S(1)}, u32[]{:S(2)}, u32[]{:S(2)}) collective-permute-start(bf16[192,1536]{1,0:T(8,128)(2,1)S(1)} %copy.21), channel_id=1, source_target_pairs={{0,32},{32,64},{64,96},{96,128},{128,160},{160,192},{192,224},{1,3... | collective-permute-start | bytes 1769480 | tf_op jit(solution)/shard_map/ppermute | solution.py:119
  331.1 17.6 %collective-permute-start.3 = (bf16[192,1536]{1,0:T(8,128)(2,1)S(1)}, bf16[192,1536]{1,0:T(8,128)(2,1)S(1)}, u32[]{:S(2)}, u32[]{:S(2)}) collective-permute-start(bf16[192,1536]{1,0:T(8,128)(2,1)S(1)} %copy.23), channel_id=1, source_target_pairs={{0,32},{32,64},{64,96},{96,128},{128,160},{160,192},{192,224},{1,3... | collective-permute-start | bytes 1769480 | tf_op jit(solution)/shard_map/ppermute | solution.py:119
  352.7 16.7 %collective-permute-start.4 = (bf16[192,1536]{1,0:T(8,128)(2,1)S(1)}, bf16[192,1536]{1,0:T(8,128)(2,1)S(1)}, u32[]{:S(2)}, u32[]{:S(2)}) collective-permute-start(bf16[192,1536]{1,0:T(8,128)(2,1)S(1)} %copy.25), channel_id=1, source_target_pairs={{0,32},{32,64},{64,96},{96,128},{128,160},{160,192},{192,224},{1,3... | collective-permute-start | bytes 1769480 | tf_op jit(solution)/shard_map/ppermute | solution.py:119
  373.5 15.9 %collective-permute-start.5 = (bf16[192,1536]{1,0:T(8,128)(2,1)S(1)}, bf16[192,1536]{1,0:T(8,128)(2,1)S(1)}, u32[]{:S(2)}, u32[]{:S(2)}) collective-permute-start(bf16[192,1536]{1,0:T(8,128)(2,1)S(1)} %copy.27), channel_id=1, source_target_pairs={{0,32},{32,64},{64,96},{96,128},{128,160},{160,192},{192,224},{1,3... | collective-permute-start | bytes 1769480 | tf_op jit(solution)/shard_map/ppermute | solution.py:119
  393.4 15.0 %collective-permute-start.6 = (bf16[192,1536]{1,0:T(8,128)(2,1)S(1)}, bf16[192,1536]{1,0:T(8,128)(2,1)S(1)}, u32[]{:S(2)}, u32[]{:S(2)}) collective-permute-start(bf16[192,1536]{1,0:T(8,128)(2,1)S(1)} %copy.29), channel_id=1, source_target_pairs={{0,32},{32,64},{64,96},{96,128},{128,160},{160,192},{192,224},{1,3... | collective-permute-start | bytes 1769480 | tf_op jit(solution)/shard_map/ppermute | solution.py:119
  412.2 6.8 %collective-permute-start.10 = (bf16[192,192]{0,1:T(8,128)(2,1)S(1)}, bf16[192,192]{0,1:T(8,128)(2,1)S(1)}, u32[]{:S(2)}, u32[]{:S(2)}) collective-permute-start(bf16[192,192]{0,1:T(8,128)(2,1)S(1)} %get-tuple-element.10), channel_id=1, source_target_pairs={{0,4},{1,5},{2,6},{3,7},{4,0},{5,1},{6,2},{7,3},{8,12},{9,13},{10,... | collective-permute-start | bytes 221192 | tf_op jit(solution)/shard_map/ppermute | solution.py:137
  412.3 6.7 %collective-permute-start.11 = (bf16[192,192]{0,1:T(8,128)(2,1)S(1)}, bf16[192,192]{0,1:T(8,128)(2,1)S(1)}, u32[]{:S(2)}, u32[]{:S(2)}) collective-permute-start(bf16[192,192]{0,1:T(8,128)(2,1)S(1)} %get-tuple-element.9), channel_id=1, source_target_pairs={{0,3},{1,4},{2,5},{3,6},{4,7},{5,0},{6,1},{7,2},{8,11},{9,12},{10,... | collective-permute-start | bytes 221192 | tf_op jit(solution)/shard_map/ppermute | solution.py:137
  412.4 6.7 %collective-permute-start.12 = (bf16[192,192]{0,1:T(8,128)(2,1)S(1)}, bf16[192,192]{0,1:T(8,128)(2,1)S(1)}, u32[]{:S(2)}, u32[]{:S(2)}) collective-permute-start(bf16[192,192]{0,1:T(8,128)(2,1)S(1)} %get-tuple-element.8), channel_id=1, source_target_pairs={{0,2},{1,3},{2,4},{3,5},{4,6},{5,7},{6,0},{7,1},{8,10},{9,11},{10,... | collective-permute-start | bytes 221192 | tf_op jit(solution)/shard_map/ppermute | solution.py:137
  412.5 8.1 %collective-permute-start.13 = (bf16[192,192]{0,1:T(8,128)(2,1)S(1)}, bf16[192,192]{0,1:T(8,128)(2,1)S(1)}, u32[]{:S(2)}, u32[]{:S(2)}) collective-permute-start(bf16[192,192]{0,1:T(8,128)(2,1)S(1)} %get-tuple-element.7), channel_id=1, source_target_pairs={{0,1},{1,2},{2,3},{3,4},{4,5},{5,6},{6,7},{7,0},{8,9},{9,10},{10,1... | collective-permute-start | bytes 221192 | tf_op jit(solution)/shard_map/ppermute | solution.py:137
  416.0 4.7 %collective-permute-start.7 = (bf16[192,192]{0,1:T(8,128)(2,1)S(1)}, bf16[192,192]{0,1:T(8,128)(2,1)S(1)}, u32[]{:S(2)}, u32[]{:S(2)}) collective-permute-start(bf16[192,192]{0,1:T(8,128)(2,1)S(1)} %get-tuple-element.13), channel_id=1, source_target_pairs={{0,7},{1,0},{2,1},{3,2},{4,3},{5,4},{6,5},{7,6},{8,15},{9,8},{10,9... | collective-permute-start | bytes 221192 | tf_op jit(solution)/shard_map/ppermute | solution.py:137
  419.1 7.4 %collective-permute-start.8 = (bf16[192,192]{0,1:T(8,128)(2,1)S(1)}, bf16[192,192]{0,1:T(8,128)(2,1)S(1)}, u32[]{:S(2)}, u32[]{:S(2)}) collective-permute-start(bf16[192,192]{0,1:T(8,128)(2,1)S(1)} %get-tuple-element.12), channel_id=1, source_target_pairs={{0,6},{1,7},{2,0},{3,1},{4,2},{5,3},{6,4},{7,5},{8,14},{9,15},{10,... | collective-permute-start | bytes 221192 | tf_op jit(solution)/shard_map/ppermute | solution.py:137
  419.1 7.4 %collective-permute-start.9 = (bf16[192,192]{0,1:T(8,128)(2,1)S(1)}, bf16[192,192]{0,1:T(8,128)(2,1)S(1)}, u32[]{:S(2)}, u32[]{:S(2)}) collective-permute-start(bf16[192,192]{0,1:T(8,128)(2,1)S(1)} %get-tuple-element.11), channel_id=1, source_target_pairs={{0,5},{1,6},{2,7},{3,0},{4,1},{5,2},{6,3},{7,4},{8,13},{9,14},{10,... | collective-permute-start | bytes 221192 | tf_op jit(solution)/shard_map/ppermute | solution.py:137
Sparse Core Ops, SparseCore 0:
  20.8 74.4 reduce-scatter.2
  97.8 72.6 reduce-scatter.4
  178.7 76.3 all-reduce.1

commit v6 on v4

--- a/solution.py
+++ b/solution.py
@@ -55,10 +55,10 @@
     slots = ACTIVE_SLOTS
 
     def dec_map(p, j, sl, tl, sv, tv):
-        return (0, sl[p, jnp.minimum(j, slots - 1)])
+        return (0, sl[p, j])
 
     def enc_map(p, j, sl, tl, sv, tv):
-        return (0, tl[p, jnp.maximum(j - slots, 0)])
+        return (0, tl[p, j])
 
     def out_map(p, j, sl, tl, sv, tv):
         return (p, 0, j)
@@ -86,6 +86,22 @@
     )(src_loc, tgt_loc, src_live, tgt_live, decoder, encoder, activation)
 
 
+def held_blocks(block_loc, block_live, first):
+    prompts, slots = block_loc.shape
+    column = jnp.arange(2 * slots)[None, :]
+    index = jnp.clip(column - first, 0, slots - 1)
+    value = jnp.take_along_axis(block_loc, jnp.broadcast_to(index, (prompts, 2 * slots)), axis=1)
+    need = jnp.take_along_axis(block_live, jnp.broadcast_to(index, (prompts, 2 * slots)), axis=1) > 0
+    need = need & (column >= first) & (column < first + slots)
+    value = value.reshape(-1)
+    need = need.reshape(-1)
+    position = jnp.arange(value.shape[0])
+    last = lax.cummax(jnp.where(need, position, -1), axis=0)
+    earliest = jnp.argmax(need)
+    last = jnp.where(last < 0, earliest, last)
+    return jnp.take(value, last).reshape(prompts, 2 * slots).astype(jnp.int32)
+
+
 def slot_tables(blocks, counts, layer, quarter, local_blocks):
     ids = lax.dynamic_index_in_dim(blocks, layer, 1, False)
     count = lax.dynamic_index_in_dim(counts, layer, 1, False)
@@ -106,7 +122,9 @@
 
     src_loc, src_live = slot_tables(blocks, counts, layer_group, quarter, local_blocks)
     tgt_loc, tgt_live = slot_tables(blocks, counts, layer_group + 1, quarter, local_blocks)
-    combined = select_blocks(decoder, encoder, activation, src_loc, tgt_loc, src_live, tgt_live)
+    dec_held = held_blocks(src_loc, src_live, 0)
+    enc_held = held_blocks(tgt_loc, tgt_live, ACTIVE_SLOTS)
+    combined = select_blocks(decoder, encoder, activation, dec_held, enc_held, src_live, tgt_live)
     combined = lax.psum_scatter(combined, "q", scatter_dimension=0, tiled=True)
     source = combined[0, :, :active_width]
     target = combined[0, :, active_width:]

time: 429 us -> 434 us (1.012)
  local copies, waits for them, and re-layouts: 8.64 us -> 15.9 us
  Pallas kernels: 22.2 us -> 16.7 us
    pallas_call x1, Pallas kernels: 22.2 us -> 16.7 us  [select_blocks(): pl.pallas_call(select_kernel, grid_spec=grid_spec, out_shape=jax.ShapeDty...]
    gather x0 -> x12, local copies, waits for them, and re-layouts: none -> 5.28 us  [the longest x6 2.03 us: held_blocks(): jnp.take_along_axis(block_live, jnp.broadcast_to(index, (prompts, 2 * slo...]
  transfers between devices with their start and end apart: 16 -> 16, of which waited for: 12 -> 13; matrix products, arithmetic and copies ran while one was open for 0% -> 0% of each run, Pallas kernels for 0% -> 0%
where the time goes in v6:
time: 434 us; the launch traced here: 432 us
  waiting for transfers between devices  320 us (74%)
  matrix products  34.2 us (8%)
  starting transfers between devices  20.9 us (5%)
  Pallas kernels  16.7 us (4%)
  local copies, waits for them, and re-layouts  15.9 us (4%)
  between operations  14.7 us (3%)
  other arithmetic  9.75 us (2%)
    reduce_scatter x1, waiting for transfers between devices, on_device(): combined = lax.psum_scatter(combined, 'q', scatter_dimension=0, tiled=True)  130 us
    ppermute x7, waiting for transfers between devices, on_device(): previous = lax.ppermute(outgoing, 'lg', forward)  106 us
    psum x1, waiting for transfers between devices, on_device(): gram_sum = lax.psum(partial_gram, 'fblk').astype(jnp.float32)  74.6 us
    dot_general x7, matrix products, on_device(): jnp.dot(previous, edges_t, preferred_element_type=jnp.float32)  26.2 us
    pallas_call x1, Pallas kernels, select_blocks(): pl.pallas_call(select_kernel, grid_spec=grid_spec, out_shape=jax.ShapeDty...  16.7 us
    ppermute x7, starting transfers between devices, on_device(): previous = lax.ppermute(outgoing, 'lg', forward)  14.3 us
  transfers between devices with their start and end apart: 16, of which 13 were waited for; matrix products, arithmetic and copies ran while one was open for 0% of the time, Pallas kernels for 0%

profile of v6, /device:TPU:134, one launch (start us, length us, event | category | flops | bytes accessed | tf_op | source)
XLA Modules:
  0.0 432.1 jit_solution(4633417450135604391)
XLA Ops:
  19.3 16.7 %shard_map.55 = bf16[4,576,3072]{2,1,0:T(8,128)(2,1)} custom-call(s32[4,6]{1,0:T(4,128)} %reshape.144.src_loc, s32[4,6]{1,0:T(4,128)} %reshape.149.tgt_loc, s32[4,3]{1,0:T(4,128)} %copy-done.1, s32[4,3]{1,0:T(4,128)} %copy-done, bf16[576,4096]{1,0:T(8,128)(2,1)} %dec_ref.1, bf16[576,4096]{1,0:T(8,128)(2,1)} %enc_ref.1, bf16[4,4096]{1,0:T(4,128)(2,1)} %act_ref.1), custom_call_target="tpu_custom_call" | custom-call | flops 3538944 | bytes 28311552 | tf_op jit(solution)/shard_map/pallas_call | solution.py:77
  36.1 130.4 %reduce-scatter.2.cloned.1.call-done = bf16[1,576,3072]{2,1,0:T(8,128)(2,1)} async-done(((bf16[4,576,3072]{2,1,0:T(8,128)(2,1)}), bf16[1,576,3072]{2,1,0:T(8,128)(2,1)}) %reduce-scatter.2.cloned.1.call-update) | async-done | bytes 3538960 | tf_op jit(solution)/shard_map/reduce_scatter | solution.py:128
  166.5 8.0 %convolution_convert_fusion = bf16[1536,1536]{1,0:T(8,128)(2,1)} fusion(bf16[1,576,3072]{2,1,0:T(8,128)(2,1)} %reduce-scatter.2.cloned.1.call-done), kind=kOutput, calls=%fused_computation.11 | convolution fusion | flops 2720268288 | bytes 8257536 | tf_op jit(solution)/shard_map/dot_general | solution.py:132
  176.5 74.6 %all-reduce.2.cloned.1.call-done = bf16[1536,1536]{1,0:T(8,128)(2,1)} async-done(((bf16[1536,1536]{1,0:T(8,128)(2,1)}), bf16[1536,1536]{1,0:T(8,128)(2,1)}) %all-reduce.2.cloned.1.call-update) | async-done | bytes 4718608 | tf_op jit(solution)/shard_map/psum | solution.py:135
  251.1 3.5 fusion.2
  254.9 1.9 fusion.1
  256.8 2.1 copy-done.3
  259.5 2.6 collective-permute-start
  262.1 15.4 %collective-permute-done = bf16[192,1536]{1,0:T(8,128)(2,1)S(1)} collective-permute-done((bf16[192,1536]{1,0:T(8,128)(2,1)S(1)}, bf16[192,1536]{1,0:T(8,128)(2,1)S(1)}, u32[]{:S(2)}, u32[]{:S(2)}) %collective-permute-start) | collective-permute-done | bytes 589856 | tf_op jit(solution)/shard_map/ppermute | solution.py:151
  277.5 3.7 fusion.3
  281.5 2.1 collective-permute-start.1
  283.6 17.0 %collective-permute-done.1 = bf16[192,1536]{1,0:T(8,128)(2,1)S(1)} collective-permute-done((bf16[192,1536]{1,0:T(8,128)(2,1)S(1)}, bf16[192,1536]{1,0:T(8,128)(2,1)S(1)}, u32[]{:S(2)}, u32[]{:S(2)}) %collective-permute-start.1) | collective-permute-done | bytes 589856 | tf_op jit(solution)/shard_map/ppermute | solution.py:151
  300.6 3.7 fusion.4
  304.6 1.9 collective-permute-start.2
  306.5 16.5 %collective-permute-done.2 = bf16[192,1536]{1,0:T(8,128)(2,1)S(1)} collective-permute-done((bf16[192,1536]{1,0:T(8,128)(2,1)S(1)}, bf16[192,1536]{1,0:T(8,128)(2,1)S(1)}, u32[]{:S(2)}, u32[]{:S(2)}) %collective-permute-start.2) | collective-permute-done | bytes 589856 | tf_op jit(solution)/shard_map/ppermute | solution.py:151
  323.0 3.7 fusion.5
  327.0 1.9 collective-permute-start.3
  329.0 15.7 %collective-permute-done.3 = bf16[192,1536]{1,0:T(8,128)(2,1)S(1)} collective-permute-done((bf16[192,1536]{1,0:T(8,128)(2,1)S(1)}, bf16[192,1536]{1,0:T(8,128)(2,1)S(1)}, u32[]{:S(2)}, u32[]{:S(2)}) %collective-permute-start.3) | collective-permute-done | bytes 589856 | tf_op jit(solution)/shard_map/ppermute | solution.py:151
  344.6 3.7 fusion.6
  348.6 1.9 collective-permute-start.4
  350.6 14.8 %collective-permute-done.4 = bf16[192,1536]{1,0:T(8,128)(2,1)S(1)} collective-permute-done((bf16[192,1536]{1,0:T(8,128)(2,1)S(1)}, bf16[192,1536]{1,0:T(8,128)(2,1)S(1)}, u32[]{:S(2)}, u32[]{:S(2)}) %collective-permute-start.4) | collective-permute-done | bytes 589856 | tf_op jit(solution)/shard_map/ppermute | solution.py:151
  365.4 3.7 fusion.7
  369.4 1.9 collective-permute-start.5
  371.3 13.9 %collective-permute-done.5 = bf16[192,1536]{1,0:T(8,128)(2,1)S(1)} collective-permute-done((bf16[192,1536]{1,0:T(8,128)(2,1)S(1)}, bf16[192,1536]{1,0:T(8,128)(2,1)S(1)}, u32[]{:S(2)}, u32[]{:S(2)}) %collective-permute-start.5) | collective-permute-done | bytes 589856 | tf_op jit(solution)/shard_map/ppermute | solution.py:151
  385.3 3.7 fusion.8
  389.3 1.9 collective-permute-start.6
  391.3 13.0 %collective-permute-done.6 = bf16[192,1536]{1,0:T(8,128)(2,1)S(1)} collective-permute-done((bf16[192,1536]{1,0:T(8,128)(2,1)S(1)}, bf16[192,1536]{1,0:T(8,128)(2,1)S(1)}, u32[]{:S(2)}, u32[]{:S(2)}) %collective-permute-start.6) | collective-permute-done | bytes 589856 | tf_op jit(solution)/shard_map/ppermute | solution.py:151
  404.3 3.7 fusion.9
  408.3 3.5 collective-permute-start.10
  411.8 3.0 collective-permute-start.12
  414.8 4.6 %collective-permute-done.8 = bf16[192,192]{0,1:T(8,128)(2,1)S(1)} collective-permute-done((bf16[192,192]{0,1:T(8,128)(2,1)S(1)}, bf16[192,192]{0,1:T(8,128)(2,1)S(1)}, u32[]{:S(2)}, u32[]{:S(2)}) %collective-permute-start.8) | collective-permute-done | bytes 73760 | tf_op jit(solution)/shard_map/ppermute | solution.py:169
  420.3 3.1 collective-permute-done.13
  (91 shorter events, 19.4 us)
Async XLA Ops:
  6.5 160.0 %reduce-scatter.2.cloned.1.call-start = ((), (), s32[]{:S(2)}) async-start(), calls=%async_computation.1 | async-start | bytes 17694720 | tf_op jit(solution)/shard_map/reduce_scatter | solution.py:128
  8.7 9.8 %copy-start = (s32[4,3]{1,0:T(4,128)}, s32[4,3]{1,0:T(4,128)S(1)}, u32[]{:S(2)}) copy-start(s32[4,3]{1,0:T(4,128)S(1)} %fusion.28.tgt_live) | copy-start | bytes 148
  10.1 9.1 %copy-start.1 = (s32[4,3]{1,0:T(4,128)}, s32[4,3]{1,0:T(4,128)S(1)}, u32[]{:S(2)}) copy-start(s32[4,3]{1,0:T(4,128)S(1)} %fusion.26.src_live) | copy-start | bytes 148
  36.0 215.1 %all-reduce.2.cloned.1.call-start = ((), (), s32[]{:S(2)}) async-start(), calls=%async_computation.2 | async-start | bytes 9437184 | tf_op jit(solution)/shard_map/psum | solution.py:135
  251.1 3.8 copy-start.2
  256.8 2.1 copy-start.3
  259.5 18.0 %collective-permute-start = (bf16[192,1536]{1,0:T(8,128)(2,1)S(1)}, bf16[192,1536]{1,0:T(8,128)(2,1)S(1)}, u32[]{:S(2)}, u32[]{:S(2)}) collective-permute-start(bf16[192,1536]{1,0:T(8,128)(2,1)S(1)} %copy.32), channel_id=1, source_target_pairs={{0,32},{32,64},{64,96},{96,128},{128,160},{160,192},{192,224},{1,3... | collective-permute-start | bytes 1769480 | tf_op jit(solution)/shard_map/ppermute | solution.py:151
  281.5 19.1 %collective-permute-start.1 = (bf16[192,1536]{1,0:T(8,128)(2,1)S(1)}, bf16[192,1536]{1,0:T(8,128)(2,1)S(1)}, u32[]{:S(2)}, u32[]{:S(2)}) collective-permute-start(bf16[192,1536]{1,0:T(8,128)(2,1)S(1)} %copy.34), channel_id=1, source_target_pairs={{0,32},{32,64},{64,96},{96,128},{128,160},{160,192},{192,224},{1,3... | collective-permute-start | bytes 1769480 | tf_op jit(solution)/shard_map/ppermute | solution.py:151
  304.6 18.5 %collective-permute-start.2 = (bf16[192,1536]{1,0:T(8,128)(2,1)S(1)}, bf16[192,1536]{1,0:T(8,128)(2,1)S(1)}, u32[]{:S(2)}, u32[]{:S(2)}) collective-permute-start(bf16[192,1536]{1,0:T(8,128)(2,1)S(1)} %copy.36), channel_id=1, source_target_pairs={{0,32},{32,64},{64,96},{96,128},{128,160},{160,192},{192,224},{1,3... | collective-permute-start | bytes 1769480 | tf_op jit(solution)/shard_map/ppermute | solution.py:151
  327.0 17.6 %collective-permute-start.3 = (bf16[192,1536]{1,0:T(8,128)(2,1)S(1)}, bf16[192,1536]{1,0:T(8,128)(2,1)S(1)}, u32[]{:S(2)}, u32[]{:S(2)}) collective-permute-start(bf16[192,1536]{1,0:T(8,128)(2,1)S(1)} %copy.38), channel_id=1, source_target_pairs={{0,32},{32,64},{64,96},{96,128},{128,160},{160,192},{192,224},{1,3... | collective-permute-start | bytes 1769480 | tf_op jit(solution)/shard_map/ppermute | solution.py:151
  348.6 16.7 %collective-permute-start.4 = (bf16[192,1536]{1,0:T(8,128)(2,1)S(1)}, bf16[192,1536]{1,0:T(8,128)(2,1)S(1)}, u32[]{:S(2)}, u32[]{:S(2)}) collective-permute-start(bf16[192,1536]{1,0:T(8,128)(2,1)S(1)} %copy.40), channel_id=1, source_target_pairs={{0,32},{32,64},{64,96},{96,128},{128,160},{160,192},{192,224},{1,3... | collective-permute-start | bytes 1769480 | tf_op jit(solution)/shard_map/ppermute | solution.py:151
  369.4 15.9 %collective-permute-start.5 = (bf16[192,1536]{1,0:T(8,128)(2,1)S(1)}, bf16[192,1536]{1,0:T(8,128)(2,1)S(1)}, u32[]{:S(2)}, u32[]{:S(2)}) collective-permute-start(bf16[192,1536]{1,0:T(8,128)(2,1)S(1)} %copy.42), channel_id=1, source_target_pairs={{0,32},{32,64},{64,96},{96,128},{128,160},{160,192},{192,224},{1,3... | collective-permute-start | bytes 1769480 | tf_op jit(solution)/shard_map/ppermute | solution.py:151
  389.3 15.0 %collective-permute-start.6 = (bf16[192,1536]{1,0:T(8,128)(2,1)S(1)}, bf16[192,1536]{1,0:T(8,128)(2,1)S(1)}, u32[]{:S(2)}, u32[]{:S(2)}) collective-permute-start(bf16[192,1536]{1,0:T(8,128)(2,1)S(1)} %copy.44), channel_id=1, source_target_pairs={{0,32},{32,64},{64,96},{96,128},{128,160},{160,192},{192,224},{1,3... | collective-permute-start | bytes 1769480 | tf_op jit(solution)/shard_map/ppermute | solution.py:151
  408.1 3.7 collective-permute-start.7
  408.2 11.2 %collective-permute-start.8 = (bf16[192,192]{0,1:T(8,128)(2,1)S(1)}, bf16[192,192]{0,1:T(8,128)(2,1)S(1)}, u32[]{:S(2)}, u32[]{:S(2)}) collective-permute-start(bf16[192,192]{0,1:T(8,128)(2,1)S(1)} %get-tuple-element.18), channel_id=1, source_target_pairs={{0,6},{1,7},{2,0},{3,1},{4,2},{5,3},{6,4},{7,5},{8,14},{9,15},{10,... | collective-permute-start | bytes 221192 | tf_op jit(solution)/shard_map/ppermute | solution.py:169
  408.3 11.6 %collective-permute-start.9 = (bf16[192,192]{0,1:T(8,128)(2,1)S(1)}, bf16[192,192]{0,1:T(8,128)(2,1)S(1)}, u32[]{:S(2)}, u32[]{:S(2)}) collective-permute-start(bf16[192,192]{0,1:T(8,128)(2,1)S(1)} %get-tuple-element.17), channel_id=1, source_target_pairs={{0,5},{1,6},{2,7},{3,0},{4,1},{5,2},{6,3},{7,4},{8,13},{9,14},{10,... | collective-permute-start | bytes 221192 | tf_op jit(solution)/shard_map/ppermute | solution.py:169
  408.3 11.5 %collective-permute-start.10 = (bf16[192,192]{0,1:T(8,128)(2,1)S(1)}, bf16[192,192]{0,1:T(8,128)(2,1)S(1)}, u32[]{:S(2)}, u32[]{:S(2)}) collective-permute-start(bf16[192,192]{0,1:T(8,128)(2,1)S(1)} %get-tuple-element.16), channel_id=1, source_target_pairs={{0,4},{1,5},{2,6},{3,7},{4,0},{5,1},{6,2},{7,3},{8,12},{9,13},{10,... | collective-permute-start | bytes 221192 | tf_op jit(solution)/shard_map/ppermute | solution.py:169
  411.8 8.0 %collective-permute-start.11 = (bf16[192,192]{0,1:T(8,128)(2,1)S(1)}, bf16[192,192]{0,1:T(8,128)(2,1)S(1)}, u32[]{:S(2)}, u32[]{:S(2)}) collective-permute-start(bf16[192,192]{0,1:T(8,128)(2,1)S(1)} %get-tuple-element.15), channel_id=1, source_target_pairs={{0,3},{1,4},{2,5},{3,6},{4,7},{5,0},{6,1},{7,2},{8,11},{9,12},{10,... | collective-permute-start | bytes 221192 | tf_op jit(solution)/shard_map/ppermute | solution.py:169
  411.8 8.5 %collective-permute-start.12 = (bf16[192,192]{0,1:T(8,128)(2,1)S(1)}, bf16[192,192]{0,1:T(8,128)(2,1)S(1)}, u32[]{:S(2)}, u32[]{:S(2)}) collective-permute-start(bf16[192,192]{0,1:T(8,128)(2,1)S(1)} %get-tuple-element.14), channel_id=1, source_target_pairs={{0,2},{1,3},{2,4},{3,5},{4,6},{5,7},{6,0},{7,1},{8,10},{9,11},{10,... | collective-permute-start | bytes 221192 | tf_op jit(solution)/shard_map/ppermute | solution.py:169
  419.3 4.0 collective-permute-start.13
Sparse Core Ops, SparseCore 0:
  36.2 130.3 reduce-scatter.1
  174.7 76.3 all-reduce.1

commit v7 on v4

--- a/solution.py
+++ b/solution.py
@@ -13,40 +13,50 @@
 ROW_TILE = 64
 
 
-def select_kernel(src_loc, tgt_loc, src_live, tgt_live, dec_ref, enc_ref, act_ref, out_ref):
+def select_kernel(src_loc, tgt_loc, src_live, tgt_live, *refs):
+    dec_refs = refs[:ACTIVE_SLOTS]
+    enc_refs = refs[ACTIVE_SLOTS : 2 * ACTIVE_SLOTS]
+    act_refs = refs[2 * ACTIVE_SLOTS : 3 * ACTIVE_SLOTS]
+    out_ref = refs[3 * ACTIVE_SLOTS]
     prompt = pl.program_id(0)
-    column = pl.program_id(1)
-    rows = dec_ref.shape[0]
+    kind = pl.program_id(1)
+    rows = dec_refs[0].shape[0]
     steps = rows // ROW_TILE
 
-    @pl.when(column < ACTIVE_SLOTS)
+    @pl.when(kind == 0)
     def _():
-        weights = act_ref[...].astype(jnp.float32)
-        row = lax.broadcasted_iota(jnp.int32, weights.shape, 0)
-        factor = jnp.sum(jnp.where(row == prompt, weights, 0.0), axis=0, keepdims=True)
-        live = src_live[prompt, column] > 0
+        for slot in range(ACTIVE_SLOTS):
+            weights = act_refs[slot][...].astype(jnp.float32)
+            row = lax.broadcasted_iota(jnp.int32, weights.shape, 0)
+            factor = jnp.sum(jnp.where(row == prompt, weights, 0.0), axis=0, keepdims=True)
+            live = src_live[prompt, slot] > 0
+            matrix_ref = dec_refs[slot]
 
-        def body(index, carry):
-            lower = pl.multiple_of(index * ROW_TILE, ROW_TILE)
-            value = dec_ref[pl.ds(lower, ROW_TILE), :].astype(jnp.float32) * factor
-            out_ref[0, pl.ds(lower, ROW_TILE), :] = jnp.where(live, value, 0.0).astype(
-                out_ref.dtype
-            )
-            return carry
+            def body(index, carry, matrix_ref=matrix_ref, factor=factor, live=live, slot=slot):
+                lower = pl.multiple_of(index * ROW_TILE, ROW_TILE)
+                value = matrix_ref[pl.ds(lower, ROW_TILE), :].astype(jnp.float32) * factor
+                out_ref[0, pl.ds(lower, ROW_TILE), pl.ds(slot * BLK, BLK)] = jnp.where(
+                    live, value, 0.0
+                ).astype(out_ref.dtype)
+                return carry
 
-        lax.fori_loop(0, steps, body, 0)
+            lax.fori_loop(0, steps, body, 0)
 
-    @pl.when(column >= ACTIVE_SLOTS)
+    @pl.when(kind == 1)
     def _():
-        live = tgt_live[prompt, column - ACTIVE_SLOTS] > 0
+        for slot in range(ACTIVE_SLOTS):
+            live = tgt_live[prompt, slot] > 0
+            matrix_ref = enc_refs[slot]
 
-        def body(index, carry):
-            lower = pl.multiple_of(index * ROW_TILE, ROW_TILE)
-            value = enc_ref[pl.ds(lower, ROW_TILE), :]
-            out_ref[0, pl.ds(lower, ROW_TILE), :] = jnp.where(live, value, jnp.zeros_like(value))
-            return carry
+            def body(index, carry, matrix_ref=matrix_ref, live=live, slot=slot):
+                lower = pl.multiple_of(index * ROW_TILE, ROW_TILE)
+                value = matrix_ref[pl.ds(lower, ROW_TILE), :]
+                out_ref[0, pl.ds(lower, ROW_TILE), pl.ds(slot * BLK, BLK)] = jnp.where(
+                    live, value, jnp.zeros_like(value)
+                )
+                return carry
 
-        lax.fori_loop(0, steps, body, 0)
+            lax.fori_loop(0, steps, body, 0)
 
 
 def select_blocks(decoder, encoder, activation, src_loc, tgt_loc, src_live, tgt_live):
@@ -54,24 +64,22 @@
     prompts = activation.shape[0]
     slots = ACTIVE_SLOTS
 
-    def dec_map(p, j, sl, tl, sv, tv):
-        return (0, sl[p, jnp.minimum(j, slots - 1)])
+    def dec_map(slot):
+        return lambda p, k, sl, tl, sv, tv: (0, sl[p, slot])
 
-    def enc_map(p, j, sl, tl, sv, tv):
-        return (0, tl[p, jnp.maximum(j - slots, 0)])
+    def enc_map(slot):
+        return lambda p, k, sl, tl, sv, tv: (0, tl[p, slot])
 
-    def out_map(p, j, sl, tl, sv, tv):
-        return (p, 0, j)
+    def out_map(p, k, sl, tl, sv, tv):
+        return (p, 0, k)
 
     grid_spec = pltpu.PrefetchScalarGridSpec(
         num_scalar_prefetch=4,
-        grid=(prompts, 2 * slots),
-        in_specs=[
-            pl.BlockSpec((rows, BLK), dec_map),
-            pl.BlockSpec((rows, BLK), enc_map),
-            pl.BlockSpec((prompts, BLK), dec_map),
-        ],
-        out_specs=pl.BlockSpec((1, rows, BLK), out_map),
+        grid=(prompts, 2),
+        in_specs=[pl.BlockSpec((rows, BLK), dec_map(slot)) for slot in range(slots)]
+        + [pl.BlockSpec((rows, BLK), enc_map(slot)) for slot in range(slots)]
+        + [pl.BlockSpec((prompts, BLK), dec_map(slot)) for slot in range(slots)],
+        out_specs=pl.BlockSpec((1, rows, slots * BLK), out_map),
     )
     block_bytes = rows * BLK * 2
     return pl.pallas_call(
@@ -83,7 +91,15 @@
             transcendentals=0,
             bytes_accessed=4 * prompts * slots * block_bytes,
         ),
-    )(src_loc, tgt_loc, src_live, tgt_live, decoder, encoder, activation)
+    )(
+        src_loc,
+        tgt_loc,
+        src_live,
+        tgt_live,
+        *([decoder] * slots),
+        *([encoder] * slots),
+        *([activation] * slots),
+    )
 
 
 def slot_tables(blocks, counts, layer, quarter, local_blocks):

time: 429 us -> 423 us (0.986)
  Pallas kernels: 22.2 us -> 16.6 us
    pallas_call x1, Pallas kernels: 22.2 us -> 16.6 us  [select_blocks(): pl.pallas_call(select_kernel, grid_spec=grid_spec, out_shape=jax.ShapeDty...]
where the time goes in v7:
time: 423 us; the launch traced here: 422 us
  waiting for transfers between devices  321 us (76%)
  matrix products  34.2 us (8%)
  starting transfers between devices  19.4 us (5%)
  Pallas kernels  16.6 us (4%)
  between operations  14.6 us (3%)
  local copies, waits for them, and re-layouts  8.64 us (2%)
  other arithmetic  7.76 us (2%)
    reduce_scatter x1, waiting for transfers between devices, on_device(): combined = lax.psum_scatter(combined, 'q', scatter_dimension=0, tiled=True)  131 us
    ppermute x7, waiting for transfers between devices, on_device(): previous = lax.ppermute(outgoing, 'lg', forward)  106 us
    psum x1, waiting for transfers between devices, on_device(): gram_sum = lax.psum(partial_gram, 'fblk').astype(jnp.float32)  74.6 us
    dot_general x7, matrix products, on_device(): jnp.dot(previous, edges_t, preferred_element_type=jnp.float32)  26.2 us
    pallas_call x1, Pallas kernels, select_blocks(): pl.pallas_call(select_kernel, grid_spec=grid_spec, out_shape=jax.ShapeDty...  16.6 us
    ppermute x7, starting transfers between devices, on_device(): previous = lax.ppermute(outgoing, 'lg', forward)  14.3 us
    ppermute x7, waiting for transfers between devices, on_device(): piece = lax.ppermute(piece, 'fblk', pairs)  9.08 us
  transfers between devices with their start and end apart: 16, of which 12 were waited for; matrix products, arithmetic and copies ran while one was open for 0% of the time, Pallas kernels for 0%

profile of v7, /device:TPU:134, one launch (start us, length us, event | category | flops | bytes accessed | tf_op | source)
XLA Modules:
  0.0 422.4 jit_solution(17079582794782159782)
XLA Ops:
  9.8 16.6 %shard_map.55 = bf16[4,576,3072]{2,1,0:T(8,128)(2,1)} custom-call(s32[4,3]{1,0:T(4,128)} %get-tuple-element.18.src_loc, s32[4,3]{1,0:T(4,128)} %get-tuple-element.17.tgt_loc, s32[4,3]{1,0:T(4,128)} %get-tuple-element.19.src_live, s32[4,3]{1,0:T(4,128)} %get-tuple-element.20.tgt_live, bf16[576,4096]{1,0:T(8,128)(2,1)} %refs_2_.1, bf16[576,4096]{1,0:T(8,128)(2,1)} %refs_2_.1, ...), custom_call_target="tpu_custom_call" | custom-call | flops 3538944 | bytes 28311552 | tf_op jit(solution)/shard_map/pallas_call | solution.py:85
  26.5 131.4 %reduce-scatter.2.cloned.1.call-done = bf16[1,576,3072]{2,1,0:T(8,128)(2,1)} async-done(((bf16[4,576,3072]{2,1,0:T(8,128)(2,1)}), bf16[1,576,3072]{2,1,0:T(8,128)(2,1)}) %reduce-scatter.2.cloned.1.call-update) | async-done | bytes 3538960 | tf_op jit(solution)/shard_map/reduce_scatter | solution.py:126
  157.9 8.0 %convolution_convert_fusion = bf16[1536,1536]{1,0:T(8,128)(2,1)} fusion(bf16[1,576,3072]{2,1,0:T(8,128)(2,1)} %reduce-scatter.2.cloned.1.call-done), kind=kOutput, calls=%fused_computation.5 | convolution fusion | flops 2720268288 | bytes 8257536 | tf_op jit(solution)/shard_map/dot_general | solution.py:130
  167.9 74.6 %all-reduce.2.cloned.1.call-done = bf16[1536,1536]{1,0:T(8,128)(2,1)} async-done(((bf16[1536,1536]{1,0:T(8,128)(2,1)}), bf16[1536,1536]{1,0:T(8,128)(2,1)}) %all-reduce.2.cloned.1.call-update) | async-done | bytes 4718608 | tf_op jit(solution)/shard_map/psum | solution.py:133
  242.5 3.5 fusion.2
  246.2 1.9 fusion.1
  248.1 2.1 copy-done.1
  250.9 2.6 collective-permute-start
  253.4 15.4 %collective-permute-done = bf16[192,1536]{1,0:T(8,128)(2,1)S(1)} collective-permute-done((bf16[192,1536]{1,0:T(8,128)(2,1)S(1)}, bf16[192,1536]{1,0:T(8,128)(2,1)S(1)}, u32[]{:S(2)}, u32[]{:S(2)}) %collective-permute-start) | collective-permute-done | bytes 589856 | tf_op jit(solution)/shard_map/ppermute | solution.py:149
  268.8 3.7 fusion.3
  272.8 1.9 collective-permute-start.1
  274.8 17.2 %collective-permute-done.1 = bf16[192,1536]{1,0:T(8,128)(2,1)S(1)} collective-permute-done((bf16[192,1536]{1,0:T(8,128)(2,1)S(1)}, bf16[192,1536]{1,0:T(8,128)(2,1)S(1)}, u32[]{:S(2)}, u32[]{:S(2)}) %collective-permute-start.1) | collective-permute-done | bytes 589856 | tf_op jit(solution)/shard_map/ppermute | solution.py:149
  291.9 3.7 fusion.4
  296.0 2.1 collective-permute-start.2
  298.1 16.3 %collective-permute-done.2 = bf16[192,1536]{1,0:T(8,128)(2,1)S(1)} collective-permute-done((bf16[192,1536]{1,0:T(8,128)(2,1)S(1)}, bf16[192,1536]{1,0:T(8,128)(2,1)S(1)}, u32[]{:S(2)}, u32[]{:S(2)}) %collective-permute-start.2) | collective-permute-done | bytes 589856 | tf_op jit(solution)/shard_map/ppermute | solution.py:149
  314.4 3.7 fusion.5
  318.4 1.9 collective-permute-start.3
  320.4 15.6 %collective-permute-done.3 = bf16[192,1536]{1,0:T(8,128)(2,1)S(1)} collective-permute-done((bf16[192,1536]{1,0:T(8,128)(2,1)S(1)}, bf16[192,1536]{1,0:T(8,128)(2,1)S(1)}, u32[]{:S(2)}, u32[]{:S(2)}) %collective-permute-start.3) | collective-permute-done | bytes 589856 | tf_op jit(solution)/shard_map/ppermute | solution.py:149
  336.0 3.7 fusion.6
  340.0 1.9 collective-permute-start.4
  342.0 14.8 %collective-permute-done.4 = bf16[192,1536]{1,0:T(8,128)(2,1)S(1)} collective-permute-done((bf16[192,1536]{1,0:T(8,128)(2,1)S(1)}, bf16[192,1536]{1,0:T(8,128)(2,1)S(1)}, u32[]{:S(2)}, u32[]{:S(2)}) %collective-permute-start.4) | collective-permute-done | bytes 589856 | tf_op jit(solution)/shard_map/ppermute | solution.py:149
  356.7 3.7 fusion.7
  360.8 1.9 collective-permute-start.5
  362.7 13.9 %collective-permute-done.5 = bf16[192,1536]{1,0:T(8,128)(2,1)S(1)} collective-permute-done((bf16[192,1536]{1,0:T(8,128)(2,1)S(1)}, bf16[192,1536]{1,0:T(8,128)(2,1)S(1)}, u32[]{:S(2)}, u32[]{:S(2)}) %collective-permute-start.5) | collective-permute-done | bytes 589856 | tf_op jit(solution)/shard_map/ppermute | solution.py:149
  376.6 3.7 fusion.8
  380.6 1.9 collective-permute-start.6
  382.7 13.0 %collective-permute-done.6 = bf16[192,1536]{1,0:T(8,128)(2,1)S(1)} collective-permute-done((bf16[192,1536]{1,0:T(8,128)(2,1)S(1)}, bf16[192,1536]{1,0:T(8,128)(2,1)S(1)}, u32[]{:S(2)}, u32[]{:S(2)}) %collective-permute-start.6) | collective-permute-done | bytes 589856 | tf_op jit(solution)/shard_map/ppermute | solution.py:149
  395.7 3.7 fusion.9
  399.8 3.5 collective-permute-start.13
  404.6 1.7 collective-permute-done.10
  406.3 1.6 collective-permute-done.13
  407.9 5.8 %collective-permute-done.8 = bf16[192,192]{0,1:T(8,128)(2,1)S(1)} collective-permute-done((bf16[192,192]{0,1:T(8,128)(2,1)S(1)}, bf16[192,192]{0,1:T(8,128)(2,1)S(1)}, u32[]{:S(2)}, u32[]{:S(2)}) %collective-permute-start.8) | collective-permute-done | bytes 73760 | tf_op jit(solution)/shard_map/ppermute | solution.py:167
  (36 shorter events, 10.6 us)
Async XLA Ops:
  6.5 151.3 %reduce-scatter.2.cloned.1.call-start = ((), (), s32[]{:S(2)}) async-start(), calls=%async_computation.1 | async-start | bytes 17694720 | tf_op jit(solution)/shard_map/reduce_scatter | solution.py:126
  26.4 216.0 %all-reduce.2.cloned.1.call-start = ((), (), s32[]{:S(2)}) async-start(), calls=%async_computation.2 | async-start | bytes 9437184 | tf_op jit(solution)/shard_map/psum | solution.py:133
  242.5 3.8 copy-start
  248.1 2.1 copy-start.1
  250.9 18.0 %collective-permute-start = (bf16[192,1536]{1,0:T(8,128)(2,1)S(1)}, bf16[192,1536]{1,0:T(8,128)(2,1)S(1)}, u32[]{:S(2)}, u32[]{:S(2)}) collective-permute-start(bf16[192,1536]{1,0:T(8,128)(2,1)S(1)} %copy.17), channel_id=1, source_target_pairs={{0,32},{32,64},{64,96},{96,128},{128,160},{160,192},{192,224},{1,3... | collective-permute-start | bytes 1769480 | tf_op jit(solution)/shard_map/ppermute | solution.py:149
  272.8 19.1 %collective-permute-start.1 = (bf16[192,1536]{1,0:T(8,128)(2,1)S(1)}, bf16[192,1536]{1,0:T(8,128)(2,1)S(1)}, u32[]{:S(2)}, u32[]{:S(2)}) collective-permute-start(bf16[192,1536]{1,0:T(8,128)(2,1)S(1)} %copy.19), channel_id=1, source_target_pairs={{0,32},{32,64},{64,96},{96,128},{128,160},{160,192},{192,224},{1,3... | collective-permute-start | bytes 1769480 | tf_op jit(solution)/shard_map/ppermute | solution.py:149
  296.0 18.4 %collective-permute-start.2 = (bf16[192,1536]{1,0:T(8,128)(2,1)S(1)}, bf16[192,1536]{1,0:T(8,128)(2,1)S(1)}, u32[]{:S(2)}, u32[]{:S(2)}) collective-permute-start(bf16[192,1536]{1,0:T(8,128)(2,1)S(1)} %copy.21), channel_id=1, source_target_pairs={{0,32},{32,64},{64,96},{96,128},{128,160},{160,192},{192,224},{1,3... | collective-permute-start | bytes 1769480 | tf_op jit(solution)/shard_map/ppermute | solution.py:149
  318.4 17.6 %collective-permute-start.3 = (bf16[192,1536]{1,0:T(8,128)(2,1)S(1)}, bf16[192,1536]{1,0:T(8,128)(2,1)S(1)}, u32[]{:S(2)}, u32[]{:S(2)}) collective-permute-start(bf16[192,1536]{1,0:T(8,128)(2,1)S(1)} %copy.23), channel_id=1, source_target_pairs={{0,32},{32,64},{64,96},{96,128},{128,160},{160,192},{192,224},{1,3... | collective-permute-start | bytes 1769480 | tf_op jit(solution)/shard_map/ppermute | solution.py:149
  340.0 16.7 %collective-permute-start.4 = (bf16[192,1536]{1,0:T(8,128)(2,1)S(1)}, bf16[192,1536]{1,0:T(8,128)(2,1)S(1)}, u32[]{:S(2)}, u32[]{:S(2)}) collective-permute-start(bf16[192,1536]{1,0:T(8,128)(2,1)S(1)} %copy.25), channel_id=1, source_target_pairs={{0,32},{32,64},{64,96},{96,128},{128,160},{160,192},{192,224},{1,3... | collective-permute-start | bytes 1769480 | tf_op jit(solution)/shard_map/ppermute | solution.py:149
  360.8 15.9 %collective-permute-start.5 = (bf16[192,1536]{1,0:T(8,128)(2,1)S(1)}, bf16[192,1536]{1,0:T(8,128)(2,1)S(1)}, u32[]{:S(2)}, u32[]{:S(2)}) collective-permute-start(bf16[192,1536]{1,0:T(8,128)(2,1)S(1)} %copy.27), channel_id=1, source_target_pairs={{0,32},{32,64},{64,96},{96,128},{128,160},{160,192},{192,224},{1,3... | collective-permute-start | bytes 1769480 | tf_op jit(solution)/shard_map/ppermute | solution.py:149
  380.6 15.0 %collective-permute-start.6 = (bf16[192,1536]{1,0:T(8,128)(2,1)S(1)}, bf16[192,1536]{1,0:T(8,128)(2,1)S(1)}, u32[]{:S(2)}, u32[]{:S(2)}) collective-permute-start(bf16[192,1536]{1,0:T(8,128)(2,1)S(1)} %copy.29), channel_id=1, source_target_pairs={{0,32},{32,64},{64,96},{96,128},{128,160},{160,192},{192,224},{1,3... | collective-permute-start | bytes 1769480 | tf_op jit(solution)/shard_map/ppermute | solution.py:149
  399.5 6.8 %collective-permute-start.10 = (bf16[192,192]{0,1:T(8,128)(2,1)S(1)}, bf16[192,192]{0,1:T(8,128)(2,1)S(1)}, u32[]{:S(2)}, u32[]{:S(2)}) collective-permute-start(bf16[192,192]{0,1:T(8,128)(2,1)S(1)} %get-tuple-element.10), channel_id=1, source_target_pairs={{0,4},{1,5},{2,6},{3,7},{4,0},{5,1},{6,2},{7,3},{8,12},{9,13},{10,... | collective-permute-start | bytes 221192 | tf_op jit(solution)/shard_map/ppermute | solution.py:167
  399.6 6.7 %collective-permute-start.11 = (bf16[192,192]{0,1:T(8,128)(2,1)S(1)}, bf16[192,192]{0,1:T(8,128)(2,1)S(1)}, u32[]{:S(2)}, u32[]{:S(2)}) collective-permute-start(bf16[192,192]{0,1:T(8,128)(2,1)S(1)} %get-tuple-element.9), channel_id=1, source_target_pairs={{0,3},{1,4},{2,5},{3,6},{4,7},{5,0},{6,1},{7,2},{8,11},{9,12},{10,... | collective-permute-start | bytes 221192 | tf_op jit(solution)/shard_map/ppermute | solution.py:167
  399.7 6.7 %collective-permute-start.12 = (bf16[192,192]{0,1:T(8,128)(2,1)S(1)}, bf16[192,192]{0,1:T(8,128)(2,1)S(1)}, u32[]{:S(2)}, u32[]{:S(2)}) collective-permute-start(bf16[192,192]{0,1:T(8,128)(2,1)S(1)} %get-tuple-element.8), channel_id=1, source_target_pairs={{0,2},{1,3},{2,4},{3,5},{4,6},{5,7},{6,0},{7,1},{8,10},{9,11},{10,... | collective-permute-start | bytes 221192 | tf_op jit(solution)/shard_map/ppermute | solution.py:167
  399.8 8.1 %collective-permute-start.13 = (bf16[192,192]{0,1:T(8,128)(2,1)S(1)}, bf16[192,192]{0,1:T(8,128)(2,1)S(1)}, u32[]{:S(2)}, u32[]{:S(2)}) collective-permute-start(bf16[192,192]{0,1:T(8,128)(2,1)S(1)} %get-tuple-element.7), channel_id=1, source_target_pairs={{0,1},{1,2},{2,3},{3,4},{4,5},{5,6},{6,7},{7,0},{8,9},{9,10},{10,1... | collective-permute-start | bytes 221192 | tf_op jit(solution)/shard_map/ppermute | solution.py:167
  403.2 4.7 %collective-permute-start.7 = (bf16[192,192]{0,1:T(8,128)(2,1)S(1)}, bf16[192,192]{0,1:T(8,128)(2,1)S(1)}, u32[]{:S(2)}, u32[]{:S(2)}) collective-permute-start(bf16[192,192]{0,1:T(8,128)(2,1)S(1)} %get-tuple-element.13), channel_id=1, source_target_pairs={{0,7},{1,0},{2,1},{3,2},{4,3},{5,4},{6,5},{7,6},{8,15},{9,8},{10,9... | collective-permute-start | bytes 221192 | tf_op jit(solution)/shard_map/ppermute | solution.py:167
  406.3 7.4 %collective-permute-start.8 = (bf16[192,192]{0,1:T(8,128)(2,1)S(1)}, bf16[192,192]{0,1:T(8,128)(2,1)S(1)}, u32[]{:S(2)}, u32[]{:S(2)}) collective-permute-start(bf16[192,192]{0,1:T(8,128)(2,1)S(1)} %get-tuple-element.12), channel_id=1, source_target_pairs={{0,6},{1,7},{2,0},{3,1},{4,2},{5,3},{6,4},{7,5},{8,14},{9,15},{10,... | collective-permute-start | bytes 221192 | tf_op jit(solution)/shard_map/ppermute | solution.py:167
  406.3 7.4 %collective-permute-start.9 = (bf16[192,192]{0,1:T(8,128)(2,1)S(1)}, bf16[192,192]{0,1:T(8,128)(2,1)S(1)}, u32[]{:S(2)}, u32[]{:S(2)}) collective-permute-start(bf16[192,192]{0,1:T(8,128)(2,1)S(1)} %get-tuple-element.11), channel_id=1, source_target_pairs={{0,5},{1,6},{2,7},{3,0},{4,1},{5,2},{6,3},{7,4},{8,13},{9,14},{10,... | collective-permute-start | bytes 221192 | tf_op jit(solution)/shard_map/ppermute | solution.py:167
Sparse Core Ops, SparseCore 0:
  26.5 131.2 reduce-scatter.1
  166.0 76.3 all-reduce.1

commit v8 on v7

--- a/solution.py
+++ b/solution.py
@@ -64,11 +64,19 @@
     prompts = activation.shape[0]
     slots = ACTIVE_SLOTS
 
+    def held(loc, live, p, slot):
+        block = loc[0, slot]
+        for earlier in reversed(range(prompts)):
+            block = jnp.where(live[earlier, slot] > 0, loc[earlier, slot], block)
+        for earlier in range(prompts):
+            block = jnp.where((earlier <= p) & (live[earlier, slot] > 0), loc[earlier, slot], block)
+        return block
+
     def dec_map(slot):
-        return lambda p, k, sl, tl, sv, tv: (0, sl[p, slot])
+        return lambda p, k, sl, tl, sv, tv: (0, held(sl, sv, p, slot))
 
     def enc_map(slot):
-        return lambda p, k, sl, tl, sv, tv: (0, tl[p, slot])
+        return lambda p, k, sl, tl, sv, tv: (0, held(tl, tv, p, slot))
 
     def out_map(p, k, sl, tl, sv, tv):
         return (p, 0, k)

time: 423 us -> 419 us (level)
  Pallas kernels: 16.6 us -> 11.1 us
    pallas_call x1, Pallas kernels: 16.6 us -> 11.1 us  [select_blocks(): pl.pallas_call(select_kernel, grid_spec=grid_spec, out_shape=jax.ShapeDty...]
where the time goes in v8:
time: 419 us; the launch traced here: 418 us
  waiting for transfers between devices  322 us (77%)
  matrix products  34.2 us (8%)
  starting transfers between devices  19.4 us (5%)
  between operations  14.6 us (3%)
  Pallas kernels  11.1 us (3%)
  local copies, waits for them, and re-layouts  8.64 us (2%)
  other arithmetic  7.76 us (2%)
    reduce_scatter x1, waiting for transfers between devices, on_device(): combined = lax.psum_scatter(combined, 'q', scatter_dimension=0, tiled=True)  132 us
    ppermute x7, waiting for transfers between devices, on_device(): previous = lax.ppermute(outgoing, 'lg', forward)  106 us
    psum x1, waiting for transfers between devices, on_device(): gram_sum = lax.psum(partial_gram, 'fblk').astype(jnp.float32)  74.6 us
    dot_general x7, matrix products, on_device(): jnp.dot(previous, edges_t, preferred_element_type=jnp.float32)  26.2 us
    ppermute x7, starting transfers between devices, on_device(): previous = lax.ppermute(outgoing, 'lg', forward)  14.3 us
    pallas_call x1, Pallas kernels, select_blocks(): pl.pallas_call(select_kernel, grid_spec=grid_spec, out_shape=jax.ShapeDty...  11.1 us
    ppermute x7, waiting for transfers between devices, on_device(): piece = lax.ppermute(piece, 'fblk', pairs)  9.08 us
  transfers between devices with their start and end apart: 16, of which 12 were waited for; matrix products, arithmetic and copies ran while one was open for 0% of the time, Pallas kernels for 0%

profile of v8, /device:TPU:134, one launch (start us, length us, event | category | flops | bytes accessed | tf_op | source)
XLA Modules:
  0.0 417.9 jit_solution(14456575509020531946)
XLA Ops:
  9.8 11.1 %shard_map.55 = bf16[4,576,3072]{2,1,0:T(8,128)(2,1)} custom-call(s32[4,3]{1,0:T(4,128)} %get-tuple-element.18.src_loc, s32[4,3]{1,0:T(4,128)} %get-tuple-element.17.tgt_loc, s32[4,3]{1,0:T(4,128)} %get-tuple-element.19.src_live, s32[4,3]{1,0:T(4,128)} %get-tuple-element.20.tgt_live, bf16[576,4096]{1,0:T(8,128)(2,1)} %refs_2_.1, bf16[576,4096]{1,0:T(8,128)(2,1)} %refs_2_.1, ...), custom_call_target="tpu_custom_call" | custom-call | flops 3538944 | bytes 28311552 | tf_op jit(solution)/shard_map/pallas_call | solution.py:93
  21.0 132.3 %reduce-scatter.2.cloned.1.call-done = bf16[1,576,3072]{2,1,0:T(8,128)(2,1)} async-done(((bf16[4,576,3072]{2,1,0:T(8,128)(2,1)}), bf16[1,576,3072]{2,1,0:T(8,128)(2,1)}) %reduce-scatter.2.cloned.1.call-update) | async-done | bytes 3538960 | tf_op jit(solution)/shard_map/reduce_scatter | solution.py:134
  153.3 8.0 %convolution_convert_fusion = bf16[1536,1536]{1,0:T(8,128)(2,1)} fusion(bf16[1,576,3072]{2,1,0:T(8,128)(2,1)} %reduce-scatter.2.cloned.1.call-done), kind=kOutput, calls=%fused_computation.5 | convolution fusion | flops 2720268288 | bytes 8257536 | tf_op jit(solution)/shard_map/dot_general | solution.py:138
  163.3 74.6 %all-reduce.2.cloned.1.call-done = bf16[1536,1536]{1,0:T(8,128)(2,1)} async-done(((bf16[1536,1536]{1,0:T(8,128)(2,1)}), bf16[1536,1536]{1,0:T(8,128)(2,1)}) %all-reduce.2.cloned.1.call-update) | async-done | bytes 4718608 | tf_op jit(solution)/shard_map/psum | solution.py:141
  237.9 3.5 fusion.2
  241.7 1.9 fusion.1
  243.6 2.1 copy-done.1
  246.3 2.6 collective-permute-start
  248.9 15.4 %collective-permute-done = bf16[192,1536]{1,0:T(8,128)(2,1)S(1)} collective-permute-done((bf16[192,1536]{1,0:T(8,128)(2,1)S(1)}, bf16[192,1536]{1,0:T(8,128)(2,1)S(1)}, u32[]{:S(2)}, u32[]{:S(2)}) %collective-permute-start) | collective-permute-done | bytes 589856 | tf_op jit(solution)/shard_map/ppermute | solution.py:157
  264.3 3.7 fusion.3
  268.3 1.9 collective-permute-start.1
  270.2 17.2 %collective-permute-done.1 = bf16[192,1536]{1,0:T(8,128)(2,1)S(1)} collective-permute-done((bf16[192,1536]{1,0:T(8,128)(2,1)S(1)}, bf16[192,1536]{1,0:T(8,128)(2,1)S(1)}, u32[]{:S(2)}, u32[]{:S(2)}) %collective-permute-start.1) | collective-permute-done | bytes 589856 | tf_op jit(solution)/shard_map/ppermute | solution.py:157
  287.4 3.7 fusion.4
  291.4 2.1 collective-permute-start.2
  293.5 16.3 %collective-permute-done.2 = bf16[192,1536]{1,0:T(8,128)(2,1)S(1)} collective-permute-done((bf16[192,1536]{1,0:T(8,128)(2,1)S(1)}, bf16[192,1536]{1,0:T(8,128)(2,1)S(1)}, u32[]{:S(2)}, u32[]{:S(2)}) %collective-permute-start.2) | collective-permute-done | bytes 589856 | tf_op jit(solution)/shard_map/ppermute | solution.py:157
  309.9 3.7 fusion.5
  313.9 1.9 collective-permute-start.3
  315.8 15.6 %collective-permute-done.3 = bf16[192,1536]{1,0:T(8,128)(2,1)S(1)} collective-permute-done((bf16[192,1536]{1,0:T(8,128)(2,1)S(1)}, bf16[192,1536]{1,0:T(8,128)(2,1)S(1)}, u32[]{:S(2)}, u32[]{:S(2)}) %collective-permute-start.3) | collective-permute-done | bytes 589856 | tf_op jit(solution)/shard_map/ppermute | solution.py:157
  331.5 3.7 fusion.6
  335.5 1.9 collective-permute-start.4
  337.4 14.8 %collective-permute-done.4 = bf16[192,1536]{1,0:T(8,128)(2,1)S(1)} collective-permute-done((bf16[192,1536]{1,0:T(8,128)(2,1)S(1)}, bf16[192,1536]{1,0:T(8,128)(2,1)S(1)}, u32[]{:S(2)}, u32[]{:S(2)}) %collective-permute-start.4) | collective-permute-done | bytes 589856 | tf_op jit(solution)/shard_map/ppermute | solution.py:157
  352.2 3.7 fusion.7
  356.2 1.9 collective-permute-start.5
  358.2 13.9 %collective-permute-done.5 = bf16[192,1536]{1,0:T(8,128)(2,1)S(1)} collective-permute-done((bf16[192,1536]{1,0:T(8,128)(2,1)S(1)}, bf16[192,1536]{1,0:T(8,128)(2,1)S(1)}, u32[]{:S(2)}, u32[]{:S(2)}) %collective-permute-start.5) | collective-permute-done | bytes 589856 | tf_op jit(solution)/shard_map/ppermute | solution.py:157
  372.1 3.7 fusion.8
  376.1 1.9 collective-permute-start.6
  378.2 13.0 %collective-permute-done.6 = bf16[192,1536]{1,0:T(8,128)(2,1)S(1)} collective-permute-done((bf16[192,1536]{1,0:T(8,128)(2,1)S(1)}, bf16[192,1536]{1,0:T(8,128)(2,1)S(1)}, u32[]{:S(2)}, u32[]{:S(2)}) %collective-permute-start.6) | collective-permute-done | bytes 589856 | tf_op jit(solution)/shard_map/ppermute | solution.py:157
  391.1 3.7 fusion.9
  395.3 3.5 collective-permute-start.13
  400.1 1.7 collective-permute-done.10
  401.8 1.6 collective-permute-done.13
  403.4 5.8 %collective-permute-done.8 = bf16[192,192]{0,1:T(8,128)(2,1)S(1)} collective-permute-done((bf16[192,192]{0,1:T(8,128)(2,1)S(1)}, bf16[192,192]{0,1:T(8,128)(2,1)S(1)}, u32[]{:S(2)}, u32[]{:S(2)}) %collective-permute-start.8) | collective-permute-done | bytes 73760 | tf_op jit(solution)/shard_map/ppermute | solution.py:175
  (36 shorter events, 10.6 us)
Async XLA Ops:
  6.5 146.8 %reduce-scatter.2.cloned.1.call-start = ((), (), s32[]{:S(2)}) async-start(), calls=%async_computation.1 | async-start | bytes 17694720 | tf_op jit(solution)/shard_map/reduce_scatter | solution.py:134
  21.0 216.9 %all-reduce.2.cloned.1.call-start = ((), (), s32[]{:S(2)}) async-start(), calls=%async_computation.2 | async-start | bytes 9437184 | tf_op jit(solution)/shard_map/psum | solution.py:141
  237.9 3.8 copy-start
  243.6 2.1 copy-start.1
  246.3 18.0 %collective-permute-start = (bf16[192,1536]{1,0:T(8,128)(2,1)S(1)}, bf16[192,1536]{1,0:T(8,128)(2,1)S(1)}, u32[]{:S(2)}, u32[]{:S(2)}) collective-permute-start(bf16[192,1536]{1,0:T(8,128)(2,1)S(1)} %copy.17), channel_id=1, source_target_pairs={{0,32},{32,64},{64,96},{96,128},{128,160},{160,192},{192,224},{1,3... | collective-permute-start | bytes 1769480 | tf_op jit(solution)/shard_map/ppermute | solution.py:157
  268.3 19.1 %collective-permute-start.1 = (bf16[192,1536]{1,0:T(8,128)(2,1)S(1)}, bf16[192,1536]{1,0:T(8,128)(2,1)S(1)}, u32[]{:S(2)}, u32[]{:S(2)}) collective-permute-start(bf16[192,1536]{1,0:T(8,128)(2,1)S(1)} %copy.19), channel_id=1, source_target_pairs={{0,32},{32,64},{64,96},{96,128},{128,160},{160,192},{192,224},{1,3... | collective-permute-start | bytes 1769480 | tf_op jit(solution)/shard_map/ppermute | solution.py:157
  291.4 18.5 %collective-permute-start.2 = (bf16[192,1536]{1,0:T(8,128)(2,1)S(1)}, bf16[192,1536]{1,0:T(8,128)(2,1)S(1)}, u32[]{:S(2)}, u32[]{:S(2)}) collective-permute-start(bf16[192,1536]{1,0:T(8,128)(2,1)S(1)} %copy.21), channel_id=1, source_target_pairs={{0,32},{32,64},{64,96},{96,128},{128,160},{160,192},{192,224},{1,3... | collective-permute-start | bytes 1769480 | tf_op jit(solution)/shard_map/ppermute | solution.py:157
  313.9 17.6 %collective-permute-start.3 = (bf16[192,1536]{1,0:T(8,128)(2,1)S(1)}, bf16[192,1536]{1,0:T(8,128)(2,1)S(1)}, u32[]{:S(2)}, u32[]{:S(2)}) collective-permute-start(bf16[192,1536]{1,0:T(8,128)(2,1)S(1)} %copy.23), channel_id=1, source_target_pairs={{0,32},{32,64},{64,96},{96,128},{128,160},{160,192},{192,224},{1,3... | collective-permute-start | bytes 1769480 | tf_op jit(solution)/shard_map/ppermute | solution.py:157
  335.5 16.7 %collective-permute-start.4 = (bf16[192,1536]{1,0:T(8,128)(2,1)S(1)}, bf16[192,1536]{1,0:T(8,128)(2,1)S(1)}, u32[]{:S(2)}, u32[]{:S(2)}) collective-permute-start(bf16[192,1536]{1,0:T(8,128)(2,1)S(1)} %copy.25), channel_id=1, source_target_pairs={{0,32},{32,64},{64,96},{96,128},{128,160},{160,192},{192,224},{1,3... | collective-permute-start | bytes 1769480 | tf_op jit(solution)/shard_map/ppermute | solution.py:157
  356.2 15.9 %collective-permute-start.5 = (bf16[192,1536]{1,0:T(8,128)(2,1)S(1)}, bf16[192,1536]{1,0:T(8,128)(2,1)S(1)}, u32[]{:S(2)}, u32[]{:S(2)}) collective-permute-start(bf16[192,1536]{1,0:T(8,128)(2,1)S(1)} %copy.27), channel_id=1, source_target_pairs={{0,32},{32,64},{64,96},{96,128},{128,160},{160,192},{192,224},{1,3... | collective-permute-start | bytes 1769480 | tf_op jit(solution)/shard_map/ppermute | solution.py:157
  376.1 15.0 %collective-permute-start.6 = (bf16[192,1536]{1,0:T(8,128)(2,1)S(1)}, bf16[192,1536]{1,0:T(8,128)(2,1)S(1)}, u32[]{:S(2)}, u32[]{:S(2)}) collective-permute-start(bf16[192,1536]{1,0:T(8,128)(2,1)S(1)} %copy.29), channel_id=1, source_target_pairs={{0,32},{32,64},{64,96},{96,128},{128,160},{160,192},{192,224},{1,3... | collective-permute-start | bytes 1769480 | tf_op jit(solution)/shard_map/ppermute | solution.py:157
  395.0 6.8 %collective-permute-start.10 = (bf16[192,192]{0,1:T(8,128)(2,1)S(1)}, bf16[192,192]{0,1:T(8,128)(2,1)S(1)}, u32[]{:S(2)}, u32[]{:S(2)}) collective-permute-start(bf16[192,192]{0,1:T(8,128)(2,1)S(1)} %get-tuple-element.10), channel_id=1, source_target_pairs={{0,4},{1,5},{2,6},{3,7},{4,0},{5,1},{6,2},{7,3},{8,12},{9,13},{10,... | collective-permute-start | bytes 221192 | tf_op jit(solution)/shard_map/ppermute | solution.py:175
  395.1 6.7 %collective-permute-start.11 = (bf16[192,192]{0,1:T(8,128)(2,1)S(1)}, bf16[192,192]{0,1:T(8,128)(2,1)S(1)}, u32[]{:S(2)}, u32[]{:S(2)}) collective-permute-start(bf16[192,192]{0,1:T(8,128)(2,1)S(1)} %get-tuple-element.9), channel_id=1, source_target_pairs={{0,3},{1,4},{2,5},{3,6},{4,7},{5,0},{6,1},{7,2},{8,11},{9,12},{10,... | collective-permute-start | bytes 221192 | tf_op jit(solution)/shard_map/ppermute | solution.py:175
  395.2 6.7 %collective-permute-start.12 = (bf16[192,192]{0,1:T(8,128)(2,1)S(1)}, bf16[192,192]{0,1:T(8,128)(2,1)S(1)}, u32[]{:S(2)}, u32[]{:S(2)}) collective-permute-start(bf16[192,192]{0,1:T(8,128)(2,1)S(1)} %get-tuple-element.8), channel_id=1, source_target_pairs={{0,2},{1,3},{2,4},{3,5},{4,6},{5,7},{6,0},{7,1},{8,10},{9,11},{10,... | collective-permute-start | bytes 221192 | tf_op jit(solution)/shard_map/ppermute | solution.py:175
  395.3 8.1 %collective-permute-start.13 = (bf16[192,192]{0,1:T(8,128)(2,1)S(1)}, bf16[192,192]{0,1:T(8,128)(2,1)S(1)}, u32[]{:S(2)}, u32[]{:S(2)}) collective-permute-start(bf16[192,192]{0,1:T(8,128)(2,1)S(1)} %get-tuple-element.7), channel_id=1, source_target_pairs={{0,1},{1,2},{2,3},{3,4},{4,5},{5,6},{6,7},{7,0},{8,9},{9,10},{10,1... | collective-permute-start | bytes 221192 | tf_op jit(solution)/shard_map/ppermute | solution.py:175
  398.7 4.7 %collective-permute-start.7 = (bf16[192,192]{0,1:T(8,128)(2,1)S(1)}, bf16[192,192]{0,1:T(8,128)(2,1)S(1)}, u32[]{:S(2)}, u32[]{:S(2)}) collective-permute-start(bf16[192,192]{0,1:T(8,128)(2,1)S(1)} %get-tuple-element.13), channel_id=1, source_target_pairs={{0,7},{1,0},{2,1},{3,2},{4,3},{5,4},{6,5},{7,6},{8,15},{9,8},{10,9... | collective-permute-start | bytes 221192 | tf_op jit(solution)/shard_map/ppermute | solution.py:175
  401.8 7.4 %collective-permute-start.8 = (bf16[192,192]{0,1:T(8,128)(2,1)S(1)}, bf16[192,192]{0,1:T(8,128)(2,1)S(1)}, u32[]{:S(2)}, u32[]{:S(2)}) collective-permute-start(bf16[192,192]{0,1:T(8,128)(2,1)S(1)} %get-tuple-element.12), channel_id=1, source_target_pairs={{0,6},{1,7},{2,0},{3,1},{4,2},{5,3},{6,4},{7,5},{8,14},{9,15},{10,... | collective-permute-start | bytes 221192 | tf_op jit(solution)/shard_map/ppermute | solution.py:175
  401.8 7.4 %collective-permute-start.9 = (bf16[192,192]{0,1:T(8,128)(2,1)S(1)}, bf16[192,192]{0,1:T(8,128)(2,1)S(1)}, u32[]{:S(2)}, u32[]{:S(2)}) collective-permute-start(bf16[192,192]{0,1:T(8,128)(2,1)S(1)} %get-tuple-element.11), channel_id=1, source_target_pairs={{0,5},{1,6},{2,7},{3,0},{4,1},{5,2},{6,3},{7,4},{8,13},{9,14},{10,... | collective-permute-start | bytes 221192 | tf_op jit(solution)/shard_map/ppermute | solution.py:175
Sparse Core Ops, SparseCore 0:
  21.1 132.1 reduce-scatter.1
  161.5 76.3 all-reduce.1

commit v9 on v8

--- a/solution.py
+++ b/solution.py
@@ -9,7 +9,6 @@
 BLK = 512
 ACTIVE_SLOTS = 3
 LAYERS = 8
-CHUNKS = 1
 ROW_TILE = 64
 
 
@@ -147,33 +146,23 @@
         jnp.bfloat16
     )
 
-    edges_t = edges.T
-    mine = lax.dynamic_slice_in_dim(edges_t, fblk * share, share, 0)
-    width = share // CHUNKS
+    mine = lax.dynamic_slice_in_dim(edges, fblk * share, share, 1)
     forward = [(index, index + 1) for index in range(group_count - 1)]
-    for step in range(1, group_count + CHUNKS - 1):
-        sent = jnp.clip(step - 1 - layer_group, 0, CHUNKS - 1)
-        outgoing = lax.dynamic_slice_in_dim(mine, sent * width, width, 0)
-        previous = lax.ppermute(outgoing, "lg", forward)
-        product = jnp.dot(previous, edges_t, preferred_element_type=jnp.float32).astype(
+    for step in range(1, group_count):
+        previous = lax.ppermute(mine, "lg", forward)
+        product = jnp.dot(edges, previous, preferred_element_type=jnp.float32).astype(
             jnp.bfloat16
         )
-        chunk = step - layer_group
-        valid = (layer_group >= 1) & (chunk >= 0) & (chunk < CHUNKS)
-        place = jnp.clip(chunk, 0, CHUNKS - 1)
-        kept = lax.dynamic_slice_in_dim(mine, place * width, width, 0)
-        mine = lax.dynamic_update_slice_in_dim(
-            mine, jnp.where(valid, product, kept), place * width, 0
-        )
+        mine = jnp.where(layer_group == step, product, mine)
 
     parts = []
     for shift in range(fblk_count):
         wanted = (fblk + shift) % fblk_count
-        piece = lax.dynamic_slice_in_dim(mine, wanted * share, share, 1)
+        piece = lax.dynamic_slice_in_dim(mine, wanted * share, share, 0)
         if shift:
             pairs = [(index, (index + shift) % fblk_count) for index in range(fblk_count)]
             piece = lax.ppermute(piece, "fblk", pairs)
-        parts.append(piece.T)
+        parts.append(piece)
     ordered = [parts[(fblk_count - m) % fblk_count] for m in range(fblk_count)]
     doubled = jnp.concatenate(ordered + ordered, axis=1)
     rows = lax.dynamic_slice_in_dim(doubled, (fblk_count - fblk) * share, active_width, 1)

time: 419 us -> 419 us (level)
  no operation moved by 1% of the time
where the time goes in v9:
time: 419 us
  waiting for transfers between devices  323 us (77%)
  matrix products  34.2 us (8%)
  starting transfers between devices  19.4 us (5%)
  between operations  14.5 us (3%)
  Pallas kernels  11.1 us (3%)
  local copies, waits for them, and re-layouts  8.64 us (2%)
  other arithmetic  7.76 us (2%)
    reduce_scatter x1, waiting for transfers between devices, on_device(): combined = lax.psum_scatter(combined, 'q', scatter_dimension=0, tiled=True)  133 us
    ppermute x7, waiting for transfers between devices, on_device(): previous = lax.ppermute(mine, 'lg', forward)  106 us
    psum x1, waiting for transfers between devices, on_device(): gram_sum = lax.psum(partial_gram, 'fblk').astype(jnp.float32)  74.6 us
    dot_general x7, matrix products, on_device(): jnp.dot(edges, previous, preferred_element_type=jnp.float32)  26.2 us
    ppermute x7, starting transfers between devices, on_device(): previous = lax.ppermute(mine, 'lg', forward)  14.3 us
    pallas_call x1, Pallas kernels, select_blocks(): pl.pallas_call(select_kernel, grid_spec=grid_spec, out_shape=jax.ShapeDty...  11.1 us
    ppermute x7, waiting for transfers between devices, on_device(): piece = lax.ppermute(piece, 'fblk', pairs)  9.08 us
  transfers between devices with their start and end apart: 16, of which 12 were waited for; matrix products, arithmetic and copies ran while one was open for 0% of the time, Pallas kernels for 0%

profile of v9, /device:TPU:134, one launch (start us, length us, event | category | flops | bytes accessed | tf_op | source)
XLA Modules:
  0.0 418.6 jit_solution(18053144048602442559)
XLA Ops:
  9.8 11.1 %shard_map.55 = bf16[4,576,3072]{2,1,0:T(8,128)(2,1)} custom-call(s32[4,3]{1,0:T(4,128)} %get-tuple-element.18.src_loc, s32[4,3]{1,0:T(4,128)} %get-tuple-element.17.tgt_loc, s32[4,3]{1,0:T(4,128)} %get-tuple-element.19.src_live, s32[4,3]{1,0:T(4,128)} %get-tuple-element.20.tgt_live, bf16[576,4096]{1,0:T(8,128)(2,1)} %refs_2_.1, bf16[576,4096]{1,0:T(8,128)(2,1)} %refs_2_.1, ...), custom_call_target="tpu_custom_call" | custom-call | flops 3538944 | bytes 28311552 | tf_op jit(solution)/shard_map/pallas_call | solution.py:92
  21.0 133.0 %reduce-scatter.2.cloned.1.call-done = bf16[1,576,3072]{2,1,0:T(8,128)(2,1)} async-done(((bf16[4,576,3072]{2,1,0:T(8,128)(2,1)}), bf16[1,576,3072]{2,1,0:T(8,128)(2,1)}) %reduce-scatter.2.cloned.1.call-update) | async-done | bytes 3538960 | tf_op jit(solution)/shard_map/reduce_scatter | solution.py:133
  154.0 8.0 %convolution_convert_fusion = bf16[1536,1536]{1,0:T(8,128)(2,1)} fusion(bf16[1,576,3072]{2,1,0:T(8,128)(2,1)} %reduce-scatter.2.cloned.1.call-done), kind=kOutput, calls=%fused_computation.5 | convolution fusion | flops 2720268288 | bytes 8257536 | tf_op jit(solution)/shard_map/dot_general | solution.py:137
  164.0 74.6 %all-reduce.2.cloned.1.call-done = bf16[1536,1536]{1,0:T(8,128)(2,1)} async-done(((bf16[1536,1536]{1,0:T(8,128)(2,1)}), bf16[1536,1536]{1,0:T(8,128)(2,1)}) %all-reduce.2.cloned.1.call-update) | async-done | bytes 4718608 | tf_op jit(solution)/shard_map/psum | solution.py:140
  238.7 3.5 fusion.2
  242.4 1.9 fusion.1
  244.4 2.1 copy-done.1
  247.1 2.6 collective-permute-start
  249.6 15.4 %collective-permute-done = bf16[1536,192]{0,1:T(8,128)(2,1)S(1)} collective-permute-done((bf16[1536,192]{0,1:T(8,128)(2,1)S(1)}, bf16[1536,192]{0,1:T(8,128)(2,1)S(1)}, u32[]{:S(2)}, u32[]{:S(2)}) %collective-permute-start) | collective-permute-done | bytes 589856 | tf_op jit(solution)/shard_map/ppermute | solution.py:152
  265.0 3.7 fusion.3
  269.0 1.9 collective-permute-start.1
  271.0 17.2 %collective-permute-done.1 = bf16[1536,192]{0,1:T(8,128)(2,1)S(1)} collective-permute-done((bf16[1536,192]{0,1:T(8,128)(2,1)S(1)}, bf16[1536,192]{0,1:T(8,128)(2,1)S(1)}, u32[]{:S(2)}, u32[]{:S(2)}) %collective-permute-start.1) | collective-permute-done | bytes 589856 | tf_op jit(solution)/shard_map/ppermute | solution.py:152
  288.1 3.7 fusion.4
  292.2 2.1 collective-permute-start.2
  294.3 16.3 %collective-permute-done.2 = bf16[1536,192]{0,1:T(8,128)(2,1)S(1)} collective-permute-done((bf16[1536,192]{0,1:T(8,128)(2,1)S(1)}, bf16[1536,192]{0,1:T(8,128)(2,1)S(1)}, u32[]{:S(2)}, u32[]{:S(2)}) %collective-permute-start.2) | collective-permute-done | bytes 589856 | tf_op jit(solution)/shard_map/ppermute | solution.py:152
  310.6 3.7 fusion.5
  314.6 1.9 collective-permute-start.3
  316.6 15.7 %collective-permute-done.3 = bf16[1536,192]{0,1:T(8,128)(2,1)S(1)} collective-permute-done((bf16[1536,192]{0,1:T(8,128)(2,1)S(1)}, bf16[1536,192]{0,1:T(8,128)(2,1)S(1)}, u32[]{:S(2)}, u32[]{:S(2)}) %collective-permute-start.3) | collective-permute-done | bytes 589856 | tf_op jit(solution)/shard_map/ppermute | solution.py:152
  332.2 3.7 fusion.6
  336.2 1.9 collective-permute-start.4
  338.2 14.8 %collective-permute-done.4 = bf16[1536,192]{0,1:T(8,128)(2,1)S(1)} collective-permute-done((bf16[1536,192]{0,1:T(8,128)(2,1)S(1)}, bf16[1536,192]{0,1:T(8,128)(2,1)S(1)}, u32[]{:S(2)}, u32[]{:S(2)}) %collective-permute-start.4) | collective-permute-done | bytes 589856 | tf_op jit(solution)/shard_map/ppermute | solution.py:152
  352.9 3.7 fusion.7
  357.0 1.9 collective-permute-start.5
  358.9 13.9 %collective-permute-done.5 = bf16[1536,192]{0,1:T(8,128)(2,1)S(1)} collective-permute-done((bf16[1536,192]{0,1:T(8,128)(2,1)S(1)}, bf16[1536,192]{0,1:T(8,128)(2,1)S(1)}, u32[]{:S(2)}, u32[]{:S(2)}) %collective-permute-start.5) | collective-permute-done | bytes 589856 | tf_op jit(solution)/shard_map/ppermute | solution.py:152
  372.8 3.7 fusion.8
  376.8 1.9 collective-permute-start.6
  378.9 13.0 %collective-permute-done.6 = bf16[1536,192]{0,1:T(8,128)(2,1)S(1)} collective-permute-done((bf16[1536,192]{0,1:T(8,128)(2,1)S(1)}, bf16[1536,192]{0,1:T(8,128)(2,1)S(1)}, u32[]{:S(2)}, u32[]{:S(2)}) %collective-permute-start.6) | collective-permute-done | bytes 589856 | tf_op jit(solution)/shard_map/ppermute | solution.py:152
  391.9 3.7 fusion.9
  396.0 3.5 collective-permute-start.13
  400.8 1.7 collective-permute-done.10
  402.5 1.6 collective-permute-done.13
  404.1 5.8 %collective-permute-done.8 = bf16[192,192]{1,0:T(8,128)(2,1)S(1)} collective-permute-done((bf16[192,192]{1,0:T(8,128)(2,1)S(1)}, bf16[192,192]{1,0:T(8,128)(2,1)S(1)}, u32[]{:S(2)}, u32[]{:S(2)}) %collective-permute-start.8) | collective-permute-done | bytes 73760 | tf_op jit(solution)/shard_map/ppermute | solution.py:164
  (36 shorter events, 10.6 us)
Async XLA Ops:
  6.5 147.5 %reduce-scatter.2.cloned.1.call-start = ((), (), s32[]{:S(2)}) async-start(), calls=%async_computation.1 | async-start | bytes 17694720 | tf_op jit(solution)/shard_map/reduce_scatter | solution.py:133
  20.9 217.7 %all-reduce.2.cloned.1.call-start = ((), (), s32[]{:S(2)}) async-start(), calls=%async_computation.2 | async-start | bytes 9437184 | tf_op jit(solution)/shard_map/psum | solution.py:140
  238.7 3.8 copy-start
  244.3 2.1 copy-start.1
  247.1 18.0 %collective-permute-start = (bf16[1536,192]{0,1:T(8,128)(2,1)S(1)}, bf16[1536,192]{0,1:T(8,128)(2,1)S(1)}, u32[]{:S(2)}, u32[]{:S(2)}) collective-permute-start(bf16[1536,192]{0,1:T(8,128)(2,1)S(1)} %copy.17), channel_id=1, source_target_pairs={{0,32},{32,64},{64,96},{96,128},{128,160},{160,192},{192,224},{1,3... | collective-permute-start | bytes 1769480 | tf_op jit(solution)/shard_map/ppermute | solution.py:152
  269.0 19.1 %collective-permute-start.1 = (bf16[1536,192]{0,1:T(8,128)(2,1)S(1)}, bf16[1536,192]{0,1:T(8,128)(2,1)S(1)}, u32[]{:S(2)}, u32[]{:S(2)}) collective-permute-start(bf16[1536,192]{0,1:T(8,128)(2,1)S(1)} %copy.19), channel_id=1, source_target_pairs={{0,32},{32,64},{64,96},{96,128},{128,160},{160,192},{192,224},{1,3... | collective-permute-start | bytes 1769480 | tf_op jit(solution)/shard_map/ppermute | solution.py:152
  292.2 18.4 %collective-permute-start.2 = (bf16[1536,192]{0,1:T(8,128)(2,1)S(1)}, bf16[1536,192]{0,1:T(8,128)(2,1)S(1)}, u32[]{:S(2)}, u32[]{:S(2)}) collective-permute-start(bf16[1536,192]{0,1:T(8,128)(2,1)S(1)} %copy.21), channel_id=1, source_target_pairs={{0,32},{32,64},{64,96},{96,128},{128,160},{160,192},{192,224},{1,3... | collective-permute-start | bytes 1769480 | tf_op jit(solution)/shard_map/ppermute | solution.py:152
  314.6 17.6 %collective-permute-start.3 = (bf16[1536,192]{0,1:T(8,128)(2,1)S(1)}, bf16[1536,192]{0,1:T(8,128)(2,1)S(1)}, u32[]{:S(2)}, u32[]{:S(2)}) collective-permute-start(bf16[1536,192]{0,1:T(8,128)(2,1)S(1)} %copy.23), channel_id=1, source_target_pairs={{0,32},{32,64},{64,96},{96,128},{128,160},{160,192},{192,224},{1,3... | collective-permute-start | bytes 1769480 | tf_op jit(solution)/shard_map/ppermute | solution.py:152
  336.2 16.7 %collective-permute-start.4 = (bf16[1536,192]{0,1:T(8,128)(2,1)S(1)}, bf16[1536,192]{0,1:T(8,128)(2,1)S(1)}, u32[]{:S(2)}, u32[]{:S(2)}) collective-permute-start(bf16[1536,192]{0,1:T(8,128)(2,1)S(1)} %copy.25), channel_id=1, source_target_pairs={{0,32},{32,64},{64,96},{96,128},{128,160},{160,192},{192,224},{1,3... | collective-permute-start | bytes 1769480 | tf_op jit(solution)/shard_map/ppermute | solution.py:152
  357.0 15.9 %collective-permute-start.5 = (bf16[1536,192]{0,1:T(8,128)(2,1)S(1)}, bf16[1536,192]{0,1:T(8,128)(2,1)S(1)}, u32[]{:S(2)}, u32[]{:S(2)}) collective-permute-start(bf16[1536,192]{0,1:T(8,128)(2,1)S(1)} %copy.27), channel_id=1, source_target_pairs={{0,32},{32,64},{64,96},{96,128},{128,160},{160,192},{192,224},{1,3... | collective-permute-start | bytes 1769480 | tf_op jit(solution)/shard_map/ppermute | solution.py:152
  376.8 15.0 %collective-permute-start.6 = (bf16[1536,192]{0,1:T(8,128)(2,1)S(1)}, bf16[1536,192]{0,1:T(8,128)(2,1)S(1)}, u32[]{:S(2)}, u32[]{:S(2)}) collective-permute-start(bf16[1536,192]{0,1:T(8,128)(2,1)S(1)} %copy.29), channel_id=1, source_target_pairs={{0,32},{32,64},{64,96},{96,128},{128,160},{160,192},{192,224},{1,3... | collective-permute-start | bytes 1769480 | tf_op jit(solution)/shard_map/ppermute | solution.py:152
  395.7 6.8 %collective-permute-start.10 = (bf16[192,192]{1,0:T(8,128)(2,1)S(1)}, bf16[192,192]{1,0:T(8,128)(2,1)S(1)}, u32[]{:S(2)}, u32[]{:S(2)}) collective-permute-start(bf16[192,192]{1,0:T(8,128)(2,1)S(1)} %get-tuple-element.10), channel_id=1, source_target_pairs={{0,4},{1,5},{2,6},{3,7},{4,0},{5,1},{6,2},{7,3},{8,12},{9,13},{10,... | collective-permute-start | bytes 221192 | tf_op jit(solution)/shard_map/ppermute | solution.py:164
  395.8 6.7 %collective-permute-start.11 = (bf16[192,192]{1,0:T(8,128)(2,1)S(1)}, bf16[192,192]{1,0:T(8,128)(2,1)S(1)}, u32[]{:S(2)}, u32[]{:S(2)}) collective-permute-start(bf16[192,192]{1,0:T(8,128)(2,1)S(1)} %get-tuple-element.9), channel_id=1, source_target_pairs={{0,3},{1,4},{2,5},{3,6},{4,7},{5,0},{6,1},{7,2},{8,11},{9,12},{10,... | collective-permute-start | bytes 221192 | tf_op jit(solution)/shard_map/ppermute | solution.py:164
  395.9 6.7 %collective-permute-start.12 = (bf16[192,192]{1,0:T(8,128)(2,1)S(1)}, bf16[192,192]{1,0:T(8,128)(2,1)S(1)}, u32[]{:S(2)}, u32[]{:S(2)}) collective-permute-start(bf16[192,192]{1,0:T(8,128)(2,1)S(1)} %get-tuple-element.8), channel_id=1, source_target_pairs={{0,2},{1,3},{2,4},{3,5},{4,6},{5,7},{6,0},{7,1},{8,10},{9,11},{10,... | collective-permute-start | bytes 221192 | tf_op jit(solution)/shard_map/ppermute | solution.py:164
  396.0 8.1 %collective-permute-start.13 = (bf16[192,192]{1,0:T(8,128)(2,1)S(1)}, bf16[192,192]{1,0:T(8,128)(2,1)S(1)}, u32[]{:S(2)}, u32[]{:S(2)}) collective-permute-start(bf16[192,192]{1,0:T(8,128)(2,1)S(1)} %get-tuple-element.7), channel_id=1, source_target_pairs={{0,1},{1,2},{2,3},{3,4},{4,5},{5,6},{6,7},{7,0},{8,9},{9,10},{10,1... | collective-permute-start | bytes 221192 | tf_op jit(solution)/shard_map/ppermute | solution.py:164
  399.4 4.7 %collective-permute-start.7 = (bf16[192,192]{1,0:T(8,128)(2,1)S(1)}, bf16[192,192]{1,0:T(8,128)(2,1)S(1)}, u32[]{:S(2)}, u32[]{:S(2)}) collective-permute-start(bf16[192,192]{1,0:T(8,128)(2,1)S(1)} %get-tuple-element.13), channel_id=1, source_target_pairs={{0,7},{1,0},{2,1},{3,2},{4,3},{5,4},{6,5},{7,6},{8,15},{9,8},{10,9... | collective-permute-start | bytes 221192 | tf_op jit(solution)/shard_map/ppermute | solution.py:164
  402.5 7.4 %collective-permute-start.8 = (bf16[192,192]{1,0:T(8,128)(2,1)S(1)}, bf16[192,192]{1,0:T(8,128)(2,1)S(1)}, u32[]{:S(2)}, u32[]{:S(2)}) collective-permute-start(bf16[192,192]{1,0:T(8,128)(2,1)S(1)} %get-tuple-element.12), channel_id=1, source_target_pairs={{0,6},{1,7},{2,0},{3,1},{4,2},{5,3},{6,4},{7,5},{8,14},{9,15},{10,... | collective-permute-start | bytes 221192 | tf_op jit(solution)/shard_map/ppermute | solution.py:164
  402.5 7.4 %collective-permute-start.9 = (bf16[192,192]{1,0:T(8,128)(2,1)S(1)}, bf16[192,192]{1,0:T(8,128)(2,1)S(1)}, u32[]{:S(2)}, u32[]{:S(2)}) collective-permute-start(bf16[192,192]{1,0:T(8,128)(2,1)S(1)} %get-tuple-element.11), channel_id=1, source_target_pairs={{0,5},{1,6},{2,7},{3,0},{4,1},{5,2},{6,3},{7,4},{8,13},{9,14},{10,... | collective-permute-start | bytes 221192 | tf_op jit(solution)/shard_map/ppermute | solution.py:164
Sparse Core Ops, SparseCore 0:
  21.1 132.9 reduce-scatter.1
  162.2 76.4 all-reduce.1

commit v10 on v9

--- a/solution.py
+++ b/solution.py
@@ -9,7 +9,7 @@
 BLK = 512
 ACTIVE_SLOTS = 3
 LAYERS = 8
-ROW_TILE = 64
+ROW_TILE = 192
 
 
 def select_kernel(src_loc, tgt_loc, src_live, tgt_live, *refs):

time: 419 us -> 418 us (level)
  no operation moved by 1% of the time
where the time goes in v10:
time: 418 us; the launch traced here: 417 us
  waiting for transfers between devices  322 us (77%)
  matrix products  34.2 us (8%)
  starting transfers between devices  19.4 us (5%)
  between operations  14.5 us (3%)
  Pallas kernels  10.7 us (3%)
  local copies, waits for them, and re-layouts  8.64 us (2%)
  other arithmetic  7.76 us (2%)
    reduce_scatter x1, waiting for transfers between devices, on_device(): combined = lax.psum_scatter(combined, 'q', scatter_dimension=0, tiled=True)  132 us
    ppermute x7, waiting for transfers between devices, on_device(): previous = lax.ppermute(mine, 'lg', forward)  106 us
    psum x1, waiting for transfers between devices, on_device(): gram_sum = lax.psum(partial_gram, 'fblk').astype(jnp.float32)  74.6 us
    dot_general x7, matrix products, on_device(): jnp.dot(edges, previous, preferred_element_type=jnp.float32)  26.2 us
    ppermute x7, starting transfers between devices, on_device(): previous = lax.ppermute(mine, 'lg', forward)  14.3 us
    pallas_call x1, Pallas kernels, select_blocks(): pl.pallas_call(select_kernel, grid_spec=grid_spec, out_shape=jax.ShapeDty...  10.7 us
    ppermute x7, waiting for transfers between devices, on_device(): piece = lax.ppermute(piece, 'fblk', pairs)  9.08 us
  transfers between devices with their start and end apart: 16, of which 12 were waited for; matrix products, arithmetic and copies ran while one was open for 0% of the time, Pallas kernels for 0%

profile of v10, /device:TPU:134, one launch (start us, length us, event | category | flops | bytes accessed | tf_op | source)
XLA Modules:
  0.0 417.0 jit_solution(12901700750659379332)
XLA Ops:
  9.8 10.7 %shard_map.55 = bf16[4,576,3072]{2,1,0:T(8,128)(2,1)} custom-call(s32[4,3]{1,0:T(4,128)} %get-tuple-element.18.src_loc, s32[4,3]{1,0:T(4,128)} %get-tuple-element.17.tgt_loc, s32[4,3]{1,0:T(4,128)} %get-tuple-element.19.src_live, s32[4,3]{1,0:T(4,128)} %get-tuple-element.20.tgt_live, bf16[576,4096]{1,0:T(8,128)(2,1)} %refs_2_.1, bf16[576,4096]{1,0:T(8,128)(2,1)} %refs_2_.1, ...), custom_call_target="tpu_custom_call" | custom-call | flops 3538944 | bytes 28311552 | tf_op jit(solution)/shard_map/pallas_call | solution.py:92
  20.6 131.8 %reduce-scatter.2.cloned.1.call-done = bf16[1,576,3072]{2,1,0:T(8,128)(2,1)} async-done(((bf16[4,576,3072]{2,1,0:T(8,128)(2,1)}), bf16[1,576,3072]{2,1,0:T(8,128)(2,1)}) %reduce-scatter.2.cloned.1.call-update) | async-done | bytes 3538960 | tf_op jit(solution)/shard_map/reduce_scatter | solution.py:133
  152.4 8.0 %convolution_convert_fusion = bf16[1536,1536]{1,0:T(8,128)(2,1)} fusion(bf16[1,576,3072]{2,1,0:T(8,128)(2,1)} %reduce-scatter.2.cloned.1.call-done), kind=kOutput, calls=%fused_computation.5 | convolution fusion | flops 2720268288 | bytes 8257536 | tf_op jit(solution)/shard_map/dot_general | solution.py:137
  162.4 74.6 %all-reduce.2.cloned.1.call-done = bf16[1536,1536]{1,0:T(8,128)(2,1)} async-done(((bf16[1536,1536]{1,0:T(8,128)(2,1)}), bf16[1536,1536]{1,0:T(8,128)(2,1)}) %all-reduce.2.cloned.1.call-update) | async-done | bytes 4718608 | tf_op jit(solution)/shard_map/psum | solution.py:140
  237.0 3.5 fusion.2
  240.8 1.9 fusion.1
  242.7 2.1 copy-done.1
  245.4 2.6 collective-permute-start
  248.0 15.4 %collective-permute-done = bf16[1536,192]{0,1:T(8,128)(2,1)S(1)} collective-permute-done((bf16[1536,192]{0,1:T(8,128)(2,1)S(1)}, bf16[1536,192]{0,1:T(8,128)(2,1)S(1)}, u32[]{:S(2)}, u32[]{:S(2)}) %collective-permute-start) | collective-permute-done | bytes 589856 | tf_op jit(solution)/shard_map/ppermute | solution.py:152
  263.4 3.7 fusion.3
  267.4 1.9 collective-permute-start.1
  269.3 17.2 %collective-permute-done.1 = bf16[1536,192]{0,1:T(8,128)(2,1)S(1)} collective-permute-done((bf16[1536,192]{0,1:T(8,128)(2,1)S(1)}, bf16[1536,192]{0,1:T(8,128)(2,1)S(1)}, u32[]{:S(2)}, u32[]{:S(2)}) %collective-permute-start.1) | collective-permute-done | bytes 589856 | tf_op jit(solution)/shard_map/ppermute | solution.py:152
  286.5 3.7 fusion.4
  290.5 2.1 collective-permute-start.2
  292.7 16.3 %collective-permute-done.2 = bf16[1536,192]{0,1:T(8,128)(2,1)S(1)} collective-permute-done((bf16[1536,192]{0,1:T(8,128)(2,1)S(1)}, bf16[1536,192]{0,1:T(8,128)(2,1)S(1)}, u32[]{:S(2)}, u32[]{:S(2)}) %collective-permute-start.2) | collective-permute-done | bytes 589856 | tf_op jit(solution)/shard_map/ppermute | solution.py:152
  309.0 3.7 fusion.5
  313.0 1.9 collective-permute-start.3
  314.9 15.7 %collective-permute-done.3 = bf16[1536,192]{0,1:T(8,128)(2,1)S(1)} collective-permute-done((bf16[1536,192]{0,1:T(8,128)(2,1)S(1)}, bf16[1536,192]{0,1:T(8,128)(2,1)S(1)}, u32[]{:S(2)}, u32[]{:S(2)}) %collective-permute-start.3) | collective-permute-done | bytes 589856 | tf_op jit(solution)/shard_map/ppermute | solution.py:152
  330.6 3.7 fusion.6
  334.6 1.9 collective-permute-start.4
  336.5 14.8 %collective-permute-done.4 = bf16[1536,192]{0,1:T(8,128)(2,1)S(1)} collective-permute-done((bf16[1536,192]{0,1:T(8,128)(2,1)S(1)}, bf16[1536,192]{0,1:T(8,128)(2,1)S(1)}, u32[]{:S(2)}, u32[]{:S(2)}) %collective-permute-start.4) | collective-permute-done | bytes 589856 | tf_op jit(solution)/shard_map/ppermute | solution.py:152
  351.3 3.7 fusion.7
  355.4 1.9 collective-permute-start.5
  357.3 13.9 %collective-permute-done.5 = bf16[1536,192]{0,1:T(8,128)(2,1)S(1)} collective-permute-done((bf16[1536,192]{0,1:T(8,128)(2,1)S(1)}, bf16[1536,192]{0,1:T(8,128)(2,1)S(1)}, u32[]{:S(2)}, u32[]{:S(2)}) %collective-permute-start.5) | collective-permute-done | bytes 589856 | tf_op jit(solution)/shard_map/ppermute | solution.py:152
  371.2 3.7 fusion.8
  375.3 1.9 collective-permute-start.6
  377.3 13.0 %collective-permute-done.6 = bf16[1536,192]{0,1:T(8,128)(2,1)S(1)} collective-permute-done((bf16[1536,192]{0,1:T(8,128)(2,1)S(1)}, bf16[1536,192]{0,1:T(8,128)(2,1)S(1)}, u32[]{:S(2)}, u32[]{:S(2)}) %collective-permute-start.6) | collective-permute-done | bytes 589856 | tf_op jit(solution)/shard_map/ppermute | solution.py:152
  390.3 3.7 fusion.9
  394.4 3.5 collective-permute-start.13
  399.2 1.7 collective-permute-done.10
  401.0 1.6 collective-permute-done.13
  402.6 5.8 %collective-permute-done.8 = bf16[192,192]{1,0:T(8,128)(2,1)S(1)} collective-permute-done((bf16[192,192]{1,0:T(8,128)(2,1)S(1)}, bf16[192,192]{1,0:T(8,128)(2,1)S(1)}, u32[]{:S(2)}, u32[]{:S(2)}) %collective-permute-start.8) | collective-permute-done | bytes 73760 | tf_op jit(solution)/shard_map/ppermute | solution.py:164
  (36 shorter events, 10.6 us)
Async XLA Ops:
  6.5 145.9 %reduce-scatter.2.cloned.1.call-start = ((), (), s32[]{:S(2)}) async-start(), calls=%async_computation.1 | async-start | bytes 17694720 | tf_op jit(solution)/shard_map/reduce_scatter | solution.py:133
  20.5 216.5 %all-reduce.2.cloned.1.call-start = ((), (), s32[]{:S(2)}) async-start(), calls=%async_computation.2 | async-start | bytes 9437184 | tf_op jit(solution)/shard_map/psum | solution.py:140
  237.0 3.8 copy-start
  242.7 2.1 copy-start.1
  245.4 18.0 %collective-permute-start = (bf16[1536,192]{0,1:T(8,128)(2,1)S(1)}, bf16[1536,192]{0,1:T(8,128)(2,1)S(1)}, u32[]{:S(2)}, u32[]{:S(2)}) collective-permute-start(bf16[1536,192]{0,1:T(8,128)(2,1)S(1)} %copy.17), channel_id=1, source_target_pairs={{0,32},{32,64},{64,96},{96,128},{128,160},{160,192},{192,224},{1,3... | collective-permute-start | bytes 1769480 | tf_op jit(solution)/shard_map/ppermute | solution.py:152
  267.4 19.1 %collective-permute-start.1 = (bf16[1536,192]{0,1:T(8,128)(2,1)S(1)}, bf16[1536,192]{0,1:T(8,128)(2,1)S(1)}, u32[]{:S(2)}, u32[]{:S(2)}) collective-permute-start(bf16[1536,192]{0,1:T(8,128)(2,1)S(1)} %copy.19), channel_id=1, source_target_pairs={{0,32},{32,64},{64,96},{96,128},{128,160},{160,192},{192,224},{1,3... | collective-permute-start | bytes 1769480 | tf_op jit(solution)/shard_map/ppermute | solution.py:152
  290.5 18.5 %collective-permute-start.2 = (bf16[1536,192]{0,1:T(8,128)(2,1)S(1)}, bf16[1536,192]{0,1:T(8,128)(2,1)S(1)}, u32[]{:S(2)}, u32[]{:S(2)}) collective-permute-start(bf16[1536,192]{0,1:T(8,128)(2,1)S(1)} %copy.21), channel_id=1, source_target_pairs={{0,32},{32,64},{64,96},{96,128},{128,160},{160,192},{192,224},{1,3... | collective-permute-start | bytes 1769480 | tf_op jit(solution)/shard_map/ppermute | solution.py:152
  313.0 17.6 %collective-permute-start.3 = (bf16[1536,192]{0,1:T(8,128)(2,1)S(1)}, bf16[1536,192]{0,1:T(8,128)(2,1)S(1)}, u32[]{:S(2)}, u32[]{:S(2)}) collective-permute-start(bf16[1536,192]{0,1:T(8,128)(2,1)S(1)} %copy.23), channel_id=1, source_target_pairs={{0,32},{32,64},{64,96},{96,128},{128,160},{160,192},{192,224},{1,3... | collective-permute-start | bytes 1769480 | tf_op jit(solution)/shard_map/ppermute | solution.py:152
  334.6 16.7 %collective-permute-start.4 = (bf16[1536,192]{0,1:T(8,128)(2,1)S(1)}, bf16[1536,192]{0,1:T(8,128)(2,1)S(1)}, u32[]{:S(2)}, u32[]{:S(2)}) collective-permute-start(bf16[1536,192]{0,1:T(8,128)(2,1)S(1)} %copy.25), channel_id=1, source_target_pairs={{0,32},{32,64},{64,96},{96,128},{128,160},{160,192},{192,224},{1,3... | collective-permute-start | bytes 1769480 | tf_op jit(solution)/shard_map/ppermute | solution.py:152
  355.4 15.9 %collective-permute-start.5 = (bf16[1536,192]{0,1:T(8,128)(2,1)S(1)}, bf16[1536,192]{0,1:T(8,128)(2,1)S(1)}, u32[]{:S(2)}, u32[]{:S(2)}) collective-permute-start(bf16[1536,192]{0,1:T(8,128)(2,1)S(1)} %copy.27), channel_id=1, source_target_pairs={{0,32},{32,64},{64,96},{96,128},{128,160},{160,192},{192,224},{1,3... | collective-permute-start | bytes 1769480 | tf_op jit(solution)/shard_map/ppermute | solution.py:152
  375.3 15.0 %collective-permute-start.6 = (bf16[1536,192]{0,1:T(8,128)(2,1)S(1)}, bf16[1536,192]{0,1:T(8,128)(2,1)S(1)}, u32[]{:S(2)}, u32[]{:S(2)}) collective-permute-start(bf16[1536,192]{0,1:T(8,128)(2,1)S(1)} %copy.29), channel_id=1, source_target_pairs={{0,32},{32,64},{64,96},{96,128},{128,160},{160,192},{192,224},{1,3... | collective-permute-start | bytes 1769480 | tf_op jit(solution)/shard_map/ppermute | solution.py:152
  394.1 6.8 %collective-permute-start.10 = (bf16[192,192]{1,0:T(8,128)(2,1)S(1)}, bf16[192,192]{1,0:T(8,128)(2,1)S(1)}, u32[]{:S(2)}, u32[]{:S(2)}) collective-permute-start(bf16[192,192]{1,0:T(8,128)(2,1)S(1)} %get-tuple-element.10), channel_id=1, source_target_pairs={{0,4},{1,5},{2,6},{3,7},{4,0},{5,1},{6,2},{7,3},{8,12},{9,13},{10,... | collective-permute-start | bytes 221192 | tf_op jit(solution)/shard_map/ppermute | solution.py:164
  394.2 6.7 %collective-permute-start.11 = (bf16[192,192]{1,0:T(8,128)(2,1)S(1)}, bf16[192,192]{1,0:T(8,128)(2,1)S(1)}, u32[]{:S(2)}, u32[]{:S(2)}) collective-permute-start(bf16[192,192]{1,0:T(8,128)(2,1)S(1)} %get-tuple-element.9), channel_id=1, source_target_pairs={{0,3},{1,4},{2,5},{3,6},{4,7},{5,0},{6,1},{7,2},{8,11},{9,12},{10,... | collective-permute-start | bytes 221192 | tf_op jit(solution)/shard_map/ppermute | solution.py:164
  394.3 6.7 %collective-permute-start.12 = (bf16[192,192]{1,0:T(8,128)(2,1)S(1)}, bf16[192,192]{1,0:T(8,128)(2,1)S(1)}, u32[]{:S(2)}, u32[]{:S(2)}) collective-permute-start(bf16[192,192]{1,0:T(8,128)(2,1)S(1)} %get-tuple-element.8), channel_id=1, source_target_pairs={{0,2},{1,3},{2,4},{3,5},{4,6},{5,7},{6,0},{7,1},{8,10},{9,11},{10,... | collective-permute-start | bytes 221192 | tf_op jit(solution)/shard_map/ppermute | solution.py:164
  394.4 8.1 %collective-permute-start.13 = (bf16[192,192]{1,0:T(8,128)(2,1)S(1)}, bf16[192,192]{1,0:T(8,128)(2,1)S(1)}, u32[]{:S(2)}, u32[]{:S(2)}) collective-permute-start(bf16[192,192]{1,0:T(8,128)(2,1)S(1)} %get-tuple-element.7), channel_id=1, source_target_pairs={{0,1},{1,2},{2,3},{3,4},{4,5},{5,6},{6,7},{7,0},{8,9},{9,10},{10,1... | collective-permute-start | bytes 221192 | tf_op jit(solution)/shard_map/ppermute | solution.py:164
  397.9 4.7 %collective-permute-start.7 = (bf16[192,192]{1,0:T(8,128)(2,1)S(1)}, bf16[192,192]{1,0:T(8,128)(2,1)S(1)}, u32[]{:S(2)}, u32[]{:S(2)}) collective-permute-start(bf16[192,192]{1,0:T(8,128)(2,1)S(1)} %get-tuple-element.13), channel_id=1, source_target_pairs={{0,7},{1,0},{2,1},{3,2},{4,3},{5,4},{6,5},{7,6},{8,15},{9,8},{10,9... | collective-permute-start | bytes 221192 | tf_op jit(solution)/shard_map/ppermute | solution.py:164
  400.9 7.4 %collective-permute-start.8 = (bf16[192,192]{1,0:T(8,128)(2,1)S(1)}, bf16[192,192]{1,0:T(8,128)(2,1)S(1)}, u32[]{:S(2)}, u32[]{:S(2)}) collective-permute-start(bf16[192,192]{1,0:T(8,128)(2,1)S(1)} %get-tuple-element.12), channel_id=1, source_target_pairs={{0,6},{1,7},{2,0},{3,1},{4,2},{5,3},{6,4},{7,5},{8,14},{9,15},{10,... | collective-permute-start | bytes 221192 | tf_op jit(solution)/shard_map/ppermute | solution.py:164
  400.9 7.4 %collective-permute-start.9 = (bf16[192,192]{1,0:T(8,128)(2,1)S(1)}, bf16[192,192]{1,0:T(8,128)(2,1)S(1)}, u32[]{:S(2)}, u32[]{:S(2)}) collective-permute-start(bf16[192,192]{1,0:T(8,128)(2,1)S(1)} %get-tuple-element.11), channel_id=1, source_target_pairs={{0,5},{1,6},{2,7},{3,0},{4,1},{5,2},{6,3},{7,4},{8,13},{9,14},{10,... | collective-permute-start | bytes 221192 | tf_op jit(solution)/shard_map/ppermute | solution.py:164
Sparse Core Ops, SparseCore 0:
  20.6 131.7 reduce-scatter.1
  160.6 76.3 all-reduce.1

commit v11 on v9

--- a/solution.py
+++ b/solution.py
@@ -155,17 +155,7 @@
         )
         mine = jnp.where(layer_group == step, product, mine)
 
-    parts = []
-    for shift in range(fblk_count):
-        wanted = (fblk + shift) % fblk_count
-        piece = lax.dynamic_slice_in_dim(mine, wanted * share, share, 0)
-        if shift:
-            pairs = [(index, (index + shift) % fblk_count) for index in range(fblk_count)]
-            piece = lax.ppermute(piece, "fblk", pairs)
-        parts.append(piece)
-    ordered = [parts[(fblk_count - m) % fblk_count] for m in range(fblk_count)]
-    doubled = jnp.concatenate(ordered + ordered, axis=1)
-    rows = lax.dynamic_slice_in_dim(doubled, (fblk_count - fblk) * share, active_width, 1)
+    rows = lax.all_to_all(mine, "fblk", 0, 1, tiled=True)
     influence = (jnp.sqrt(jnp.float32(active_width)) * rows.astype(jnp.float32)).astype(
         jnp.bfloat16
     )

time: 419 us -> 421 us (level)
  blocking collectives: 0 us -> 15.4 us
  waiting for transfers between devices: 323 us -> 314 us
  starting transfers between devices: 19.4 us -> 14.3 us
    all_to_all x0 -> x1, blocking collectives: none -> 15.4 us  [on_device(): rows = lax.all_to_all(mine, 'fblk', 0, 1, tiled=True)]
    ppermute x7 -> x0, waiting for transfers between devices: 9.08 us -> none  [on_device(): piece = lax.ppermute(piece, 'fblk', pairs)]
    ppermute x7 -> x0, starting transfers between devices: 5.07 us -> none  [on_device(): piece = lax.ppermute(piece, 'fblk', pairs)]
  transfers between devices with their start and end apart: 16 -> 9, of which waited for: 12 -> 9; matrix products, arithmetic and copies ran while one was open for 0% -> 0% of each run, Pallas kernels for 0% -> 0%
where the time goes in v11:
time: 421 us; the launch traced here: 420 us
  waiting for transfers between devices  314 us (75%)
  matrix products  34.2 us (8%)
  blocking collectives  15.4 us (4%)
  starting transfers between devices  14.3 us (3%)
  between operations  14.3 us (3%)
  Pallas kernels  10.9 us (3%)
  local copies, waits for them, and re-layouts  9.73 us (2%)
  other arithmetic  6.81 us (2%)
    reduce_scatter x1, waiting for transfers between devices, on_device(): combined = lax.psum_scatter(combined, 'q', scatter_dimension=0, tiled=True)  133 us
    ppermute x7, waiting for transfers between devices, on_device(): previous = lax.ppermute(mine, 'lg', forward)  106 us
    psum x1, waiting for transfers between devices, on_device(): gram_sum = lax.psum(partial_gram, 'fblk').astype(jnp.float32)  74.6 us
    dot_general x7, matrix products, on_device(): jnp.dot(edges, previous, preferred_element_type=jnp.float32)  26.2 us
    all_to_all x1, blocking collectives, on_device(): rows = lax.all_to_all(mine, 'fblk', 0, 1, tiled=True)  15.4 us
    ppermute x7, starting transfers between devices, on_device(): previous = lax.ppermute(mine, 'lg', forward)  14.3 us
    pallas_call x1, Pallas kernels, select_blocks(): pl.pallas_call(select_kernel, grid_spec=grid_spec, out_shape=jax.ShapeDty...  10.9 us
  transfers between devices with their start and end apart: 9, of which 9 were waited for; matrix products, arithmetic and copies ran while one was open for 0% of the time, Pallas kernels for 0%

profile of v11, /device:TPU:134, one launch (start us, length us, event | category | flops | bytes accessed | tf_op | source)
XLA Modules:
  0.0 420.0 jit_solution(17336542946681795972)
XLA Ops:
  7.6 1.0 dynamic-slice_reduce_fusion
  9.8 10.9 %shard_map.55 = bf16[4,576,3072]{2,1,0:T(8,128)(2,1)} custom-call(s32[4,3]{1,0:T(4,128)} %get-tuple-element.10.src_loc, s32[4,3]{1,0:T(4,128)} %get-tuple-element.9.tgt_loc, s32[4,3]{1,0:T(4,128)} %get-tuple-element.11.src_live, s32[4,3]{1,0:T(4,128)} %get-tuple-element.12.tgt_live, bf16[576,4096]{1,0:T(8,128)(2,1)} %refs_2_.1, bf16[576,4096]{1,0:T(8,128)(2,1)} %refs_2_.1, ...), custom_call_target="tpu_custom_call" | custom-call | flops 3538944 | bytes 28311552 | tf_op jit(solution)/shard_map/pallas_call | solution.py:92
  20.9 133.2 %reduce-scatter.2.cloned.1.call-done = bf16[1,576,3072]{2,1,0:T(8,128)(2,1)} async-done(((bf16[4,576,3072]{2,1,0:T(8,128)(2,1)}), bf16[1,576,3072]{2,1,0:T(8,128)(2,1)}) %reduce-scatter.2.cloned.1.call-update) | async-done | bytes 3538960 | tf_op jit(solution)/shard_map/reduce_scatter | solution.py:133
  154.1 8.0 %convolution_convert_fusion = bf16[1536,1536]{1,0:T(8,128)(2,1)} fusion(bf16[1,576,3072]{2,1,0:T(8,128)(2,1)} %reduce-scatter.2.cloned.1.call-done), kind=kOutput, calls=%fused_computation.5 | convolution fusion | flops 2720268288 | bytes 8257536 | tf_op jit(solution)/shard_map/dot_general | solution.py:137
  162.1 1.3 dynamic_slice.24
  164.1 74.6 %all-reduce.2.cloned.1.call-done = bf16[1536,1536]{1,0:T(8,128)(2,1)} async-done(((bf16[1536,1536]{1,0:T(8,128)(2,1)}), bf16[1536,1536]{1,0:T(8,128)(2,1)}) %all-reduce.2.cloned.1.call-update) | async-done | bytes 4718608 | tf_op jit(solution)/shard_map/psum | solution.py:140
  238.7 3.5 fusion.2
  242.4 1.9 fusion.1
  244.4 2.1 copy-done.1
  247.1 2.6 collective-permute-start
  249.6 15.4 %collective-permute-done = bf16[1536,192]{0,1:T(8,128)(2,1)S(1)} collective-permute-done((bf16[1536,192]{0,1:T(8,128)(2,1)S(1)}, bf16[1536,192]{0,1:T(8,128)(2,1)S(1)}, u32[]{:S(2)}, u32[]{:S(2)}) %collective-permute-start) | collective-permute-done | bytes 589856 | tf_op jit(solution)/shard_map/ppermute | solution.py:152
  265.0 3.7 fusion.3
  269.0 1.9 collective-permute-start.1
  271.0 17.2 %collective-permute-done.1 = bf16[1536,192]{0,1:T(8,128)(2,1)S(1)} collective-permute-done((bf16[1536,192]{0,1:T(8,128)(2,1)S(1)}, bf16[1536,192]{0,1:T(8,128)(2,1)S(1)}, u32[]{:S(2)}, u32[]{:S(2)}) %collective-permute-start.1) | collective-permute-done | bytes 589856 | tf_op jit(solution)/shard_map/ppermute | solution.py:152
  288.1 3.7 fusion.4
  292.2 2.1 collective-permute-start.2
  294.3 16.3 %collective-permute-done.2 = bf16[1536,192]{0,1:T(8,128)(2,1)S(1)} collective-permute-done((bf16[1536,192]{0,1:T(8,128)(2,1)S(1)}, bf16[1536,192]{0,1:T(8,128)(2,1)S(1)}, u32[]{:S(2)}, u32[]{:S(2)}) %collective-permute-start.2) | collective-permute-done | bytes 589856 | tf_op jit(solution)/shard_map/ppermute | solution.py:152
  310.6 3.7 fusion.5
  314.6 1.9 collective-permute-start.3
  316.6 15.7 %collective-permute-done.3 = bf16[1536,192]{0,1:T(8,128)(2,1)S(1)} collective-permute-done((bf16[1536,192]{0,1:T(8,128)(2,1)S(1)}, bf16[1536,192]{0,1:T(8,128)(2,1)S(1)}, u32[]{:S(2)}, u32[]{:S(2)}) %collective-permute-start.3) | collective-permute-done | bytes 589856 | tf_op jit(solution)/shard_map/ppermute | solution.py:152
  332.2 3.7 fusion.6
  336.2 1.9 collective-permute-start.4
  338.2 14.8 %collective-permute-done.4 = bf16[1536,192]{0,1:T(8,128)(2,1)S(1)} collective-permute-done((bf16[1536,192]{0,1:T(8,128)(2,1)S(1)}, bf16[1536,192]{0,1:T(8,128)(2,1)S(1)}, u32[]{:S(2)}, u32[]{:S(2)}) %collective-permute-start.4) | collective-permute-done | bytes 589856 | tf_op jit(solution)/shard_map/ppermute | solution.py:152
  352.9 3.7 fusion.7
  357.0 1.9 collective-permute-start.5
  358.9 13.9 %collective-permute-done.5 = bf16[1536,192]{0,1:T(8,128)(2,1)S(1)} collective-permute-done((bf16[1536,192]{0,1:T(8,128)(2,1)S(1)}, bf16[1536,192]{0,1:T(8,128)(2,1)S(1)}, u32[]{:S(2)}, u32[]{:S(2)}) %collective-permute-start.5) | collective-permute-done | bytes 589856 | tf_op jit(solution)/shard_map/ppermute | solution.py:152
  372.8 3.7 fusion.8
  376.8 1.9 collective-permute-start.6
  378.8 13.1 %collective-permute-done.6 = bf16[1536,192]{0,1:T(8,128)(2,1)S(1)} collective-permute-done((bf16[1536,192]{0,1:T(8,128)(2,1)S(1)}, bf16[1536,192]{0,1:T(8,128)(2,1)S(1)}, u32[]{:S(2)}, u32[]{:S(2)}) %collective-permute-start.6) | collective-permute-done | bytes 589856 | tf_op jit(solution)/shard_map/ppermute | solution.py:152
  391.9 3.7 fusion.9
  395.6 15.4 %all_to_all.13 = bf16[8,192,192]{2,1,0:T(8,128)(2,1)S(1)} all-to-all(bf16[8,192,192]{2,1,0:T(8,128)(2,1)S(1)} %bitcast.72), channel_id=1, replica_groups=mesh['lg'=8,'q'=4,'fblk'=8] {'fblk'}, dimensions={0} | all-to-all | bytes 1179648 | tf_op jit(solution)/shard_map/all_to_all | solution.py:158
  411.6 1.5 convert_element_type.87
  (23 shorter events, 5.4 us)
Async XLA Ops:
  6.5 147.5 %reduce-scatter.2.cloned.1.call-start = ((), (), s32[]{:S(2)}) async-start(), calls=%async_computation.2 | async-start | bytes 17694720 | tf_op jit(solution)/shard_map/reduce_scatter | solution.py:133
  20.8 217.9 %all-reduce.2.cloned.1.call-start = ((), (), s32[]{:S(2)}) async-start(), calls=%async_computation.3 | async-start | bytes 9437184 | tf_op jit(solution)/shard_map/psum | solution.py:140
  238.7 3.8 copy-start
  244.4 2.1 copy-start.1
  247.1 18.0 %collective-permute-start = (bf16[1536,192]{0,1:T(8,128)(2,1)S(1)}, bf16[1536,192]{0,1:T(8,128)(2,1)S(1)}, u32[]{:S(2)}, u32[]{:S(2)}) collective-permute-start(bf16[1536,192]{0,1:T(8,128)(2,1)S(1)} %copy.18), channel_id=1, source_target_pairs={{0,32},{32,64},{64,96},{96,128},{128,160},{160,192},{192,224},{1,3... | collective-permute-start | bytes 1769480 | tf_op jit(solution)/shard_map/ppermute | solution.py:152
  269.0 19.1 %collective-permute-start.1 = (bf16[1536,192]{0,1:T(8,128)(2,1)S(1)}, bf16[1536,192]{0,1:T(8,128)(2,1)S(1)}, u32[]{:S(2)}, u32[]{:S(2)}) collective-permute-start(bf16[1536,192]{0,1:T(8,128)(2,1)S(1)} %copy.20), channel_id=1, source_target_pairs={{0,32},{32,64},{64,96},{96,128},{128,160},{160,192},{192,224},{1,3... | collective-permute-start | bytes 1769480 | tf_op jit(solution)/shard_map/ppermute | solution.py:152
  292.2 18.4 %collective-permute-start.2 = (bf16[1536,192]{0,1:T(8,128)(2,1)S(1)}, bf16[1536,192]{0,1:T(8,128)(2,1)S(1)}, u32[]{:S(2)}, u32[]{:S(2)}) collective-permute-start(bf16[1536,192]{0,1:T(8,128)(2,1)S(1)} %copy.22), channel_id=1, source_target_pairs={{0,32},{32,64},{64,96},{96,128},{128,160},{160,192},{192,224},{1,3... | collective-permute-start | bytes 1769480 | tf_op jit(solution)/shard_map/ppermute | solution.py:152
  314.6 17.6 %collective-permute-start.3 = (bf16[1536,192]{0,1:T(8,128)(2,1)S(1)}, bf16[1536,192]{0,1:T(8,128)(2,1)S(1)}, u32[]{:S(2)}, u32[]{:S(2)}) collective-permute-start(bf16[1536,192]{0,1:T(8,128)(2,1)S(1)} %copy.24), channel_id=1, source_target_pairs={{0,32},{32,64},{64,96},{96,128},{128,160},{160,192},{192,224},{1,3... | collective-permute-start | bytes 1769480 | tf_op jit(solution)/shard_map/ppermute | solution.py:152
  336.2 16.7 %collective-permute-start.4 = (bf16[1536,192]{0,1:T(8,128)(2,1)S(1)}, bf16[1536,192]{0,1:T(8,128)(2,1)S(1)}, u32[]{:S(2)}, u32[]{:S(2)}) collective-permute-start(bf16[1536,192]{0,1:T(8,128)(2,1)S(1)} %copy.26), channel_id=1, source_target_pairs={{0,32},{32,64},{64,96},{96,128},{128,160},{160,192},{192,224},{1,3... | collective-permute-start | bytes 1769480 | tf_op jit(solution)/shard_map/ppermute | solution.py:152
  357.0 15.9 %collective-permute-start.5 = (bf16[1536,192]{0,1:T(8,128)(2,1)S(1)}, bf16[1536,192]{0,1:T(8,128)(2,1)S(1)}, u32[]{:S(2)}, u32[]{:S(2)}) collective-permute-start(bf16[1536,192]{0,1:T(8,128)(2,1)S(1)} %copy.28), channel_id=1, source_target_pairs={{0,32},{32,64},{64,96},{96,128},{128,160},{160,192},{192,224},{1,3... | collective-permute-start | bytes 1769480 | tf_op jit(solution)/shard_map/ppermute | solution.py:152
  376.8 15.0 %collective-permute-start.6 = (bf16[1536,192]{0,1:T(8,128)(2,1)S(1)}, bf16[1536,192]{0,1:T(8,128)(2,1)S(1)}, u32[]{:S(2)}, u32[]{:S(2)}) collective-permute-start(bf16[1536,192]{0,1:T(8,128)(2,1)S(1)} %copy.30), channel_id=1, source_target_pairs={{0,32},{32,64},{64,96},{96,128},{128,160},{160,192},{192,224},{1,3... | collective-permute-start | bytes 1769480 | tf_op jit(solution)/shard_map/ppermute | solution.py:152
Sparse Core Ops, SparseCore 0:
  20.9 133.0 reduce-scatter.1
  162.2 76.4 all-reduce.1
